TPU v7x, 32 devices: a whole 2x2x4 slice. The times are simulated.
32 devices in a mesh: basin: 2 (over y), tx: 8 (over z, x), ty: 2 (over core).
Axes of the slice: x: 2, y: 2, z: 4, core: 2. Of those that a mesh axis runs over, the one named last changes fastest.
Arguments:
- jac_blocks: bfloat16 [896, 128, 128], P(('basin', 'tx', 'ty')), parts along dimension 0, may hold values from -0.1875 to 0.1875
- jac_rows: int32 [896], P(('basin', 'tx', 'ty')), parts along dimension 0, may hold values from 0 to 11, as said below
- jac_cols: int32 [896], P(('basin', 'tx', 'ty')), parts along dimension 0, may hold values from 0 to 3
- landing: int32 [256], P(('basin', 'tx', 'ty')), parts along dimension 0, may hold values from 0 to 3
- covariance_root: bfloat16 [16384, 512], P(('basin', 'tx', 'ty')), parts along dimension 0
Outputs:
- rescaled_orthogonal_root: bfloat16 [16384, 512], P(('basin', 'tx', 'ty')), parts along dimension 0
- r_factor: float32 [1024, 512], P('basin'), parts along dimension 0
There are 2 independent parts, one for each index of `basin`. A program takes and returns all parts, laid end to end along the dimension named above; each array names one. Nothing has to cross between parts.
Inputs may be any that keep to these rules, and one draw needn't show every extreme that they name: `jac_rows`: in each device's list of 28 blocks every row slot from 0 to 11 appears at least once.
All inputs are finite; a program needn't handle non-finite values.
Results may differ from a plain program's by a relative error of at most 0.001.
Values sent between devices are 32-bit elements; how exact they have to be, the bound alone decides.
No kernel may reach another device: no remote copies, remote signals or barrier semaphores. Data moves between devices by JAX's collectives and lax.ppermute only.
A program may use at most 64 MiB of HBM per device.

v0:
```python
import jax
import jax.numpy as jnp
from jax import lax
from jax.experimental import pallas as pl
from jax.experimental.pallas import tpu as pltpu
from jax.sharding import PartitionSpec as P

HI = lax.Precision.HIGHEST


def factor_kernel(g_ref, f_ref, x_ref, u_ref, w_ref, inv_ref, xs_ref):
    n = g_ref.shape[0]
    b = inv_ref.shape[1]
    nb = n // b
    w_ref[...] = g_ref[...]
    u_ref[...] = jnp.zeros(u_ref.shape, jnp.float32)
    lane = lax.broadcasted_iota(jnp.int32, (1, b), 1)
    rows = lax.broadcasted_iota(jnp.int32, (b, 1), 0)
    eye = jnp.where(lax.broadcasted_iota(jnp.int32, (b, b), 0) == lax.broadcasted_iota(jnp.int32, (b, b), 1), 1.0, 0.0)
    for k in range(nb):
        o = k * b
        inv_ref[k] = eye
        for j in range(b):
            r = w_ref[o + j:o + j + 1, o:o + b]
            rs = lax.rsqrt(r[:, j:j + 1])
            u = jnp.where(lane >= j, r, 0.0) * rs
            u_ref[o + j:o + j + 1, o:o + b] = u
            brow = inv_ref[k, j:j + 1, :] * rs
            inv_ref[k, j:j + 1, :] = brow
            if j == b - 1:
                break
            s = (j + 1) // 8 * 8
            v = w_ref[o + s:o + b, o + j:o + j + 1] * rs
            v = jnp.where(rows[s:] > j, v, 0.0)
            w_ref[o + s:o + b, o:o + b] = w_ref[o + s:o + b, o:o + b] - v * u
            inv_ref[k, s:, :] = inv_ref[k, s:, :] - v * brow
        if k < nb - 1:
            e = o + b
            panel = jnp.dot(inv_ref[k], w_ref[o:e, e:], precision=HI, preferred_element_type=jnp.float32)
            u_ref[o:e, e:] = panel
            w_ref[e:, e:] = w_ref[e:, e:] - lax.dot_general(
                panel, panel, (((0,), (0,)), ((), ())), precision=HI, preferred_element_type=jnp.float32)
    for k in range(nb):
        o = k * b
        y = f_ref[:, o:o + b]
        if k > 0:
            y = y - jnp.dot(xs_ref[:, :o], u_ref[:o, o:o + b], precision=HI, preferred_element_type=jnp.float32)
        xs_ref[:, o:o + b] = lax.dot_general(
            y, inv_ref[k], (((1,), (1,)), ((), ())), precision=HI, preferred_element_type=jnp.float32)
    x_ref[...] = xs_ref[...].astype(x_ref.dtype)


def factor_solve(gram, forecast, block=128):
    n = gram.shape[0]
    m = forecast.shape[0]
    vmem = pl.BlockSpec(memory_space=pltpu.VMEM)
    return pl.pallas_call(
        factor_kernel,
        out_shape=(jax.ShapeDtypeStruct((m, n), jnp.bfloat16), jax.ShapeDtypeStruct((n, n), jnp.float32)),
        in_specs=[vmem, vmem],
        out_specs=(vmem, vmem),
        scratch_shapes=[
            pltpu.VMEM((n, n), jnp.float32),
            pltpu.VMEM((n // block, block, block), jnp.float32),
            pltpu.VMEM((m, n), jnp.float32),
        ],
    )(gram, forecast)


def shifted(block, axis, distance):
    devices = range(lax.axis_size(axis))
    route = [(i - distance, i) for i in devices if i - distance in devices]
    return lax.ppermute(block, axis, route)


def doubling_sum(block, axis):
    size = lax.axis_size(axis)
    distance = 1
    while distance < size:
        route = [(i, i ^ distance) for i in range(size)]
        block = block + lax.ppermute(block, axis, route)
        distance *= 2
    return block


def reduce_tiles(tiles):
    count = tiles.shape[0]
    if lax.axis_size("ty") != 2 or count % 2:
        return doubling_sum(doubling_sum(tiles, "tx"), "ty")
    half = count // 2
    side = lax.axis_index("ty")
    swap = [(0, 1), (1, 0)]
    sent = lax.dynamic_slice_in_dim(tiles, (1 - side) * half, half, axis=0)
    kept = lax.dynamic_slice_in_dim(tiles, side * half, half, axis=0)
    kept = kept + lax.ppermute(sent, "ty", swap)
    kept = doubling_sum(kept, "tx")
    other = lax.ppermute(kept, "ty", swap)
    return jnp.where(side == 0, jnp.concatenate([kept, other]), jnp.concatenate([other, kept]))


def apply_kernel(rows_ref, cols_ref, jac_ref, root_ref, base_ref, out_ref, acc_ref):
    nblk = root_ref.shape[0]
    acc_ref[...] = jnp.zeros(acc_ref.shape, jnp.float32)

    def step(n, carry):
        slot = rows_ref[n]
        acc_ref[slot] = acc_ref[slot] + jnp.dot(
            jac_ref[n], root_ref[cols_ref[n]], preferred_element_type=jnp.float32)
        return carry

    lax.fori_loop(0, jac_ref.shape[0], step, 0)
    base_ref[...] = root_ref[...].astype(jnp.float32) + acc_ref[:nblk]
    out_ref[...] = acc_ref[nblk:]


def apply_blocks(jac_rows, jac_cols, jac_blocks, root_blocks, slot_count):
    nblk, block, width = root_blocks.shape
    smem = pl.BlockSpec(memory_space=pltpu.SMEM)
    vmem = pl.BlockSpec(memory_space=pltpu.VMEM)
    return pl.pallas_call(
        apply_kernel,
        out_shape=(
            jax.ShapeDtypeStruct((nblk, block, width), jnp.float32),
            jax.ShapeDtypeStruct((slot_count - nblk, block, width), jnp.float32),
        ),
        in_specs=[smem, smem, vmem, vmem],
        out_specs=(vmem, vmem),
        scratch_shapes=[pltpu.VMEM((slot_count, block, width), jnp.float32)],
    )(jac_rows, jac_cols, jac_blocks, root_blocks)


def land_kernel(landing_ref, base_ref, *refs):
    pieces = refs[:4]
    forecast_ref, tiles_ref, acc_ref = refs[4:]
    nblk, block, width = base_ref.shape
    rim = pieces[0].shape[0]
    acc_ref[...] = base_ref[...]
    for k in range(4):
        for h in range(rim):
            target = landing_ref[k * rim + h]
            acc_ref[target] = acc_ref[target] + pieces[k][h]
    for i in range(nblk):
        forecast_ref[i * block:(i + 1) * block, :] = acc_ref[i]
    whole = forecast_ref[...]
    gram = lax.dot_general(whole, whole, (((0,), (0,)), ((), ())), precision=HI,
                           preferred_element_type=jnp.float32)
    tiles = width // block
    t = 0
    for a in range(tiles):
        for b in range(a, tiles):
            tiles_ref[t] = gram[a * block:(a + 1) * block, b * block:(b + 1) * block]
            t += 1


def land_and_gram(landing, base, pieces):
    nblk, block, width = base.shape
    tiles = width // block
    count = tiles * (tiles + 1) // 2
    smem = pl.BlockSpec(memory_space=pltpu.SMEM)
    vmem = pl.BlockSpec(memory_space=pltpu.VMEM)
    return pl.pallas_call(
        land_kernel,
        out_shape=(
            jax.ShapeDtypeStruct((nblk * block, width), jnp.float32),
            jax.ShapeDtypeStruct((count, block, block), jnp.float32),
        ),
        in_specs=[smem, vmem] + [vmem] * len(pieces),
        out_specs=(vmem, vmem),
        scratch_shapes=[pltpu.VMEM((nblk, block, width), jnp.float32)],
    )(landing, base, *pieces)

def per_device(jac_blocks, jac_rows, jac_cols, landing, covariance_root):
    nnz, block, _ = jac_blocks.shape
    state_rows, mode_columns = covariance_root.shape
    nblk = state_rows // block
    rim = landing.shape[0] // 4
    slot_count = nblk + 4 * rim
    blocks = covariance_root.reshape(nblk, block, mode_columns)
    base, outgoing = apply_blocks(jac_rows, jac_cols, jac_blocks, blocks, slot_count)
    from_next_x = shifted(outgoing[0:rim], "tx", -1)
    from_prev_x = shifted(outgoing[rim:2 * rim], "tx", 1)
    from_next_y = shifted(outgoing[2 * rim:3 * rim], "ty", -1)
    from_prev_y = shifted(outgoing[3 * rim:], "ty", 1)
    predicted_root, local_tiles = land_and_gram(
        landing, base, [from_next_x, from_prev_x, from_next_y, from_prev_y])
    total_rows = state_rows * lax.axis_size("tx") * lax.axis_size("ty")
    tiles = mode_columns // block
    upper_sum = reduce_tiles(local_tiles)
    position = {}
    counter = 0
    for first in range(tiles):
        for second in range(first, tiles):
            position[first, second] = counter
            counter = counter + 1
    band_rows = []
    for first in range(tiles):
        pieces = []
        for second in range(tiles):
            if first <= second:
                pieces.append(upper_sum[position[first, second]])
            else:
                pieces.append(upper_sum[position[second, first]].T)
        band_rows.append(jnp.concatenate(pieces, axis=1))
    summed = jnp.concatenate(band_rows, axis=0)
    inner_products_table = summed / total_rows
    rescaled_orthogonal_root, r_factor = factor_solve(inner_products_table, predicted_root, block)
    return (rescaled_orthogonal_root, r_factor)


def solution(mesh):
    placed = (
        P(("basin", "tx", "ty"), None, None),
        P(("basin", "tx", "ty")),
        P(("basin", "tx", "ty")),
        P(("basin", "tx", "ty")),
        P(("basin", "tx", "ty"), None),
    )
    return jax.shard_map(
        per_device,
        mesh=mesh,
        in_specs=placed,
        out_specs=(P(("basin", "tx", "ty"), None), P("basin", None)),
        check_vma=False,
    )
```

profile of v0, /device:TPU:0, one launch (start us, length us, event | category | flops | bytes accessed | tf_op | source)
XLA Modules:
  0.0 137.7 jit_solution(1907968790022426099)
XLA Ops:
  0.6 8.2 %shard_map.68 = (f32[4,128,512]{2,1,0:T(8,128)}, f32[8,128,512]{2,1,0:T(8,128)}) custom-call(s32[28]{0:T(128)} %rows_ref.1, s32[28]{0:T(128)} %cols_ref.1, bf16[28,128,128]{2,1,0:T(8,128)(2,1)} %jac_ref.1, bf16[4,128,512]{2,1,0:T(8,128)(2,1)} %bitcast.38), custom_call_target="tpu_custom_call" | custom-call | tf_op jit(solution)/shard_map/pallas_call | solution.py:120
  8.9 2.8 %fusion = (f32[2,128,512]{2,1,0:T(8,128)S(1)}, f32[2,128,512]{2,1,0:T(8,128)S(1)}, f32[2,128,512]{2,1,0:T(8,128)}, f32[2,128,512]{2,1,0:T(8,128)}) fusion(f32[8,128,512]{2,1,0:T(8,128)} %get-tuple-element.7), kind=kLoop, calls=%fused_computation.16 | loop fusion | bytes 4194304 | tf_op jit(solution)/shard_map/slice | solution.py:183
  11.6 1.3 collective-permute-start
  12.9 5.5 %collective-permute-start.1 = (f32[2,128,512]{2,1,0:T(8,128)}, f32[2,128,512]{2,1,0:T(8,128)S(1)}, u32[]{:S(2)}, u32[]{:S(2)}) collective-permute-start(f32[2,128,512]{2,1,0:T(8,128)} %get-tuple-element.12), channel_id=1, source_target_pairs={{0,2},{2,4},{4,6},{6,8},{8,10},{10,12},{12,14},{1,3},{3,5},{5,7},{... | collective-permute-start | bytes 1572872 | tf_op jit(solution)/shard_map/ppermute | solution.py:73
  18.4 1.3 collective-permute-start.2
  19.7 3.1 %collective-permute-start.3 = (f32[2,128,512]{2,1,0:T(8,128)S(1)}, f32[2,128,512]{2,1,0:T(8,128)S(1)}, u32[]{:S(2)}, u32[]{:S(2)}) collective-permute-start(f32[2,128,512]{2,1,0:T(8,128)S(1)} %get-tuple-element.10), channel_id=1, source_target_pairs={{0,1},{2,3},{4,5},{6,7},{8,9},{10,11},{12,13},{14,15},{16,17},{18,... | collective-permute-start | bytes 1572872 | tf_op jit(solution)/shard_map/ppermute | solution.py:73
  22.8 5.8 %collective-permute-done.refs_0_ = f32[2,128,512]{2,1,0:T(8,128)S(1)} collective-permute-done((f32[2,128,512]{2,1,0:T(8,128)}, f32[2,128,512]{2,1,0:T(8,128)S(1)}, u32[]{:S(2)}, u32[]{:S(2)}) %collective-permute-start) | collective-permute-done | bytes 524320 | tf_op jit(solution)/shard_map/ppermute | solution.py:73
  28.6 0.0 copy-start
  28.6 11.5 %collective-permute-done.1.refs_1_ = f32[2,128,512]{2,1,0:T(8,128)S(1)} collective-permute-done((f32[2,128,512]{2,1,0:T(8,128)}, f32[2,128,512]{2,1,0:T(8,128)S(1)}, u32[]{:S(2)}, u32[]{:S(2)}) %collective-permute-start.1) | collective-permute-done | bytes 524320 | tf_op jit(solution)/shard_map/ppermute | solution.py:73
  40.1 0.0 copy-start.1
  40.1 0.0 collective-permute-done.2.refs_2_
  40.1 0.0 copy-start.2
  40.1 0.0 collective-permute-done.3.refs_3_
  40.1 0.0 copy-start.3
  40.1 0.0 copy-done
  40.1 0.8 copy-done.1
  40.9 0.2 copy-done.2
  41.1 0.2 copy-done.3
  41.2 4.9 %shard_map.69 = (f32[512,512]{1,0:T(8,128)}, f32[10,128,128]{2,1,0:T(8,128)}) custom-call(s32[8]{0:T(128)} %landing_ref.1, f32[4,128,512]{2,1,0:T(8,128)} %get-tuple-element.6.base_ref, f32[2,128,512]{2,1,0:T(8,128)} %copy-done, f32[2,128,512]{2,1,0:T(8,128)} %copy-done.1, f32[2,128,512]{2,1,0:T(8,128)} %copy-done.2, f32[2,128,512]{2,1,0:T(8,128)} %copy-done.3), custom_call_target="tpu_custom_call" | custom-call | tf_op jit(solution)/shard_map/pallas_call | solution.py:161
  46.1 1.0 constant_dynamic-slice_fusion
  47.1 0.1 collective-permute-start.4
  47.2 1.6 %collective-permute-done.4 = f32[5,128,128]{2,1,0:T(8,128)S(1)} collective-permute-done((f32[5,128,128]{2,1,0:T(8,128)S(1)}, f32[5,128,128]{2,1,0:T(8,128)S(1)}, u32[]{:S(2)}, u32[]{:S(2)}) %collective-permute-start.4) | collective-permute-done | bytes 327712 | tf_op jit(solution)/shard_map/ppermute | solution.py:95
  48.8 1.0 dynamic-slice_add_fusion
  49.8 2.4 %collective-permute-start.5 = (f32[5,128,128]{2,1,0:T(8,128)S(1)}, f32[5,128,128]{2,1,0:T(8,128)S(1)}, u32[]{:S(2)}, u32[]{:S(2)}) collective-permute-start(f32[5,128,128]{2,1,0:T(8,128)S(1)} %dynamic-slice_add_fusion), channel_id=1, source_target_pairs={{0,2},{2,0},{4,6},{6,4},{8,10},{10,8},{12,14},{14,12},{1,3},{3,1},... | collective-permute-start | bytes 983048 | tf_op jit(solution)/shard_map/ppermute | solution.py:81
  52.3 8.0 %collective-permute-done.5 = f32[5,128,128]{2,1,0:T(8,128)S(1)} collective-permute-done((f32[5,128,128]{2,1,0:T(8,128)S(1)}, f32[5,128,128]{2,1,0:T(8,128)S(1)}, u32[]{:S(2)}, u32[]{:S(2)}) %collective-permute-start.5) | collective-permute-done | bytes 327712 | tf_op jit(solution)/shard_map/ppermute | solution.py:81
  60.3 1.6 %collective-permute-start.6 = (f32[5,128,128]{2,1,0:T(8,128)S(1)}, f32[5,128,128]{2,1,0:T(8,128)S(1)}, u32[]{:S(2)}, u32[]{:S(2)}) collective-permute-start(f32[5,128,128]{2,1,0:T(8,128)S(1)} %add.21), channel_id=1, source_target_pairs={{0,4},{2,6},{4,0},{6,2},{8,12},{10,14},{12,8},{14,10},{1,5},{3,7},... | collective-permute-start | bytes 983048 | tf_op jit(solution)/shard_map/ppermute | solution.py:81
  62.0 7.7 %collective-permute-done.6 = f32[5,128,128]{2,1,0:T(8,128)S(1)} collective-permute-done((f32[5,128,128]{2,1,0:T(8,128)S(1)}, f32[5,128,128]{2,1,0:T(8,128)S(1)}, u32[]{:S(2)}, u32[]{:S(2)}) %collective-permute-start.6) | collective-permute-done | bytes 327712 | tf_op jit(solution)/shard_map/ppermute | solution.py:81
  69.7 2.7 %collective-permute-start.7 = (f32[5,128,128]{2,1,0:T(8,128)S(1)}, f32[5,128,128]{2,1,0:T(8,128)S(1)}, u32[]{:S(2)}, u32[]{:S(2)}) collective-permute-start(f32[5,128,128]{2,1,0:T(8,128)S(1)} %add.22), channel_id=1, source_target_pairs={{0,8},{2,10},{4,12},{6,14},{8,0},{10,2},{12,4},{14,6},{1,9},{3,11}... | collective-permute-start | bytes 983048 | tf_op jit(solution)/shard_map/ppermute | solution.py:81
  72.3 13.7 %collective-permute-done.7 = f32[5,128,128]{2,1,0:T(8,128)S(1)} collective-permute-done((f32[5,128,128]{2,1,0:T(8,128)S(1)}, f32[5,128,128]{2,1,0:T(8,128)S(1)}, u32[]{:S(2)}, u32[]{:S(2)}) %collective-permute-start.7) | collective-permute-done | bytes 327712 | tf_op jit(solution)/shard_map/ppermute | solution.py:81
  86.0 0.1 collective-permute-start.8
  86.1 1.6 %collective-permute-done.8 = f32[5,128,128]{2,1,0:T(8,128)S(1)} collective-permute-done((f32[5,128,128]{2,1,0:T(8,128)S(1)}, f32[5,128,128]{2,1,0:T(8,128)S(1)}, u32[]{:S(2)}, u32[]{:S(2)}) %collective-permute-start.8) | collective-permute-done | bytes 327712 | tf_op jit(solution)/shard_map/ppermute | solution.py:97
  87.8 0.1 slice_bitcast_fusion.2
  87.9 0.1 copy.12
  88.0 0.1 copy.16
  88.1 0.1 copy.11
  88.2 0.1 copy.15
  88.3 0.1 copy.10
  88.4 0.1 copy.14
  88.5 0.1 copy.13
  88.6 1.1 maximum_multiply_fusion.g_ref
  89.7 48.0 %shard_map.70 = (bf16[512,512]{1,0:T(8,128)(2,1)}, f32[512,512]{1,0:T(8,128)}) custom-call(f32[512,512]{1,0:T(8,128)} %maximum_multiply_fusion.g_ref, f32[512,512]{1,0:T(8,128)} %get-tuple-element.9.f_ref), custom_call_target="tpu_custom_call" | custom-call | tf_op jit(solution)/shard_map/pallas_call | solution.py:57
  (5 shorter events, 0.2 us)
Async XLA Ops:
  11.6 17.0 %collective-permute-start = (f32[2,128,512]{2,1,0:T(8,128)}, f32[2,128,512]{2,1,0:T(8,128)S(1)}, u32[]{:S(2)}, u32[]{:S(2)}) collective-permute-start(f32[2,128,512]{2,1,0:T(8,128)} %get-tuple-element.13), channel_id=1, source_target_pairs={{2,0},{4,2},{6,4},{8,6},{10,8},{12,10},{14,12},{3,1},{5,3},{7,5},{... | collective-permute-start | bytes 1572872 | tf_op jit(solution)/shard_map/ppermute | solution.py:73
  12.9 27.2 %collective-permute-start.1 = (f32[2,128,512]{2,1,0:T(8,128)}, f32[2,128,512]{2,1,0:T(8,128)S(1)}, u32[]{:S(2)}, u32[]{:S(2)}) collective-permute-start(f32[2,128,512]{2,1,0:T(8,128)} %get-tuple-element.12), channel_id=1, source_target_pairs={{0,2},{2,4},{4,6},{6,8},{8,10},{10,12},{12,14},{1,3},{3,5},{5,7},{... | collective-permute-start | bytes 1572872 | tf_op jit(solution)/shard_map/ppermute | solution.py:73
  18.4 21.7 %collective-permute-start.2 = (f32[2,128,512]{2,1,0:T(8,128)S(1)}, f32[2,128,512]{2,1,0:T(8,128)S(1)}, u32[]{:S(2)}, u32[]{:S(2)}) collective-permute-start(f32[2,128,512]{2,1,0:T(8,128)S(1)} %get-tuple-element.11), channel_id=1, source_target_pairs={{1,0},{3,2},{5,4},{7,6},{9,8},{11,10},{13,12},{15,14},{17,16},{19,... | collective-permute-start | bytes 1572872 | tf_op jit(solution)/shard_map/ppermute | solution.py:73
  19.7 20.4 %collective-permute-start.3 = (f32[2,128,512]{2,1,0:T(8,128)S(1)}, f32[2,128,512]{2,1,0:T(8,128)S(1)}, u32[]{:S(2)}, u32[]{:S(2)}) collective-permute-start(f32[2,128,512]{2,1,0:T(8,128)S(1)} %get-tuple-element.10), channel_id=1, source_target_pairs={{0,1},{2,3},{4,5},{6,7},{8,9},{10,11},{12,13},{14,15},{16,17},{18,... | collective-permute-start | bytes 1572872 | tf_op jit(solution)/shard_map/ppermute | solution.py:73
  28.6 11.5 %copy-start = (f32[2,128,512]{2,1,0:T(8,128)}, f32[2,128,512]{2,1,0:T(8,128)S(1)}, u32[]{:S(2)}) copy-start(f32[2,128,512]{2,1,0:T(8,128)S(1)} %collective-permute-done.refs_0_) | copy-start | bytes 1572868
  40.1 0.8 copy-start.1
  40.1 1.0 copy-start.2
  40.1 1.1 copy-start.3
  47.1 1.7 %collective-permute-start.4 = (f32[5,128,128]{2,1,0:T(8,128)S(1)}, f32[5,128,128]{2,1,0:T(8,128)S(1)}, u32[]{:S(2)}, u32[]{:S(2)}) collective-permute-start(f32[5,128,128]{2,1,0:T(8,128)S(1)} %constant_dynamic-slice_fusion), channel_id=1, source_target_pairs={{0,1},{1,0},{2,3},{3,2},{4,5},{5,4},{6,7},{7,6},{8,9},{9,8},{10,11... | collective-permute-start | bytes 983048 | tf_op jit(solution)/shard_map/ppermute | solution.py:95
  49.8 10.5 %collective-permute-start.5 = (f32[5,128,128]{2,1,0:T(8,128)S(1)}, f32[5,128,128]{2,1,0:T(8,128)S(1)}, u32[]{:S(2)}, u32[]{:S(2)}) collective-permute-start(f32[5,128,128]{2,1,0:T(8,128)S(1)} %dynamic-slice_add_fusion), channel_id=1, source_target_pairs={{0,2},{2,0},{4,6},{6,4},{8,10},{10,8},{12,14},{14,12},{1,3},{3,1},... | collective-permute-start | bytes 983048 | tf_op jit(solution)/shard_map/ppermute | solution.py:81
  60.3 9.3 %collective-permute-start.6 = (f32[5,128,128]{2,1,0:T(8,128)S(1)}, f32[5,128,128]{2,1,0:T(8,128)S(1)}, u32[]{:S(2)}, u32[]{:S(2)}) collective-permute-start(f32[5,128,128]{2,1,0:T(8,128)S(1)} %add.21), channel_id=1, source_target_pairs={{0,4},{2,6},{4,0},{6,2},{8,12},{10,14},{12,8},{14,10},{1,5},{3,7},... | collective-permute-start | bytes 983048 | tf_op jit(solution)/shard_map/ppermute | solution.py:81
  69.7 16.3 %collective-permute-start.7 = (f32[5,128,128]{2,1,0:T(8,128)S(1)}, f32[5,128,128]{2,1,0:T(8,128)S(1)}, u32[]{:S(2)}, u32[]{:S(2)}) collective-permute-start(f32[5,128,128]{2,1,0:T(8,128)S(1)} %add.22), channel_id=1, source_target_pairs={{0,8},{2,10},{4,12},{6,14},{8,0},{10,2},{12,4},{14,6},{1,9},{3,11}... | collective-permute-start | bytes 983048 | tf_op jit(solution)/shard_map/ppermute | solution.py:81
  86.0 1.7 %collective-permute-start.8 = (f32[5,128,128]{2,1,0:T(8,128)S(1)}, f32[5,128,128]{2,1,0:T(8,128)S(1)}, u32[]{:S(2)}, u32[]{:S(2)}) collective-permute-start(f32[5,128,128]{2,1,0:T(8,128)S(1)} %add.23), channel_id=1, source_target_pairs={{0,1},{1,0},{2,3},{3,2},{4,5},{5,4},{6,7},{7,6},{8,9},{9,8},{10,11... | collective-permute-start | bytes 983048 | tf_op jit(solution)/shard_map/ppermute | solution.py:97
where the time goes:
time: 138 us
  Pallas kernels  61.1 us (44%)
  waiting for transfers between devices  49.8 us (36%)
  starting transfers between devices  18.1 us (13%)
  local copies, waits for them, and re-layouts  5.63 us (4%)
  other arithmetic  2.25 us (2%)
    pallas_call x1, Pallas kernels, factor_solve(): pl.pallas_call(factor_kernel, out_shape=(jax.ShapeDtypeStruct((m, n), jnp...  48 us
    ppermute x3, waiting for transfers between devices, doubling_sum(): block = block + lax.ppermute(block, axis, route)  29.4 us
    ppermute x4, waiting for transfers between devices, shifted(): return lax.ppermute(block, axis, route)  17.2 us
    ppermute x4, starting transfers between devices, shifted(): return lax.ppermute(block, axis, route)  11.2 us
    pallas_call x1, Pallas kernels, apply_blocks(): pl.pallas_call(apply_kernel, out_shape=(jax.ShapeDtypeStruct((nblk, block...  8.25 us
    ppermute x3, starting transfers between devices, doubling_sum(): block = block + lax.ppermute(block, axis, route)  6.74 us
    pallas_call x1, Pallas kernels, land_and_gram(): pl.pallas_call(land_kernel, out_shape=(jax.ShapeDtypeStruct((nblk * block...  4.89 us
  transfers between devices with their start and end apart: 9, of which 7 were waited for; matrix products, arithmetic and copies ran while one was open for 0% of the time, Pallas kernels for 0%

commit v1 on v0

--- a/solution.py
+++ b/solution.py
@@ -98,8 +98,39 @@
     return jnp.where(side == 0, jnp.concatenate([kept, other]), jnp.concatenate([other, kept]))
 
 
-def apply_kernel(rows_ref, cols_ref, jac_ref, root_ref, base_ref, out_ref, acc_ref):
+def halving_sum(flat):
+    levels = []
+    for axis in ("ty", "tx"):
+        size = lax.axis_size(axis)
+        distance = 1
+        while distance < size:
+            levels.append((axis, size, distance))
+            distance *= 2
+    pieces = 2 ** len(levels)
+    regular = all(size & (size - 1) == 0 for _, size, _ in levels)
+    if not regular or flat.shape[0] % pieces:
+        return doubling_sum(doubling_sum(flat, "tx"), "ty")
+    bits = []
+    for axis, size, distance in levels:
+        bit = lax.axis_index(axis) // distance % 2
+        route = [(i, i ^ distance) for i in range(size)]
+        half = flat.shape[0] // 2
+        sent = lax.dynamic_slice_in_dim(flat, (1 - bit) * half, half)
+        kept = lax.dynamic_slice_in_dim(flat, bit * half, half)
+        flat = kept + lax.ppermute(sent, axis, route)
+        bits.append(bit)
+    for (axis, size, distance), bit in reversed(list(zip(levels, bits))):
+        route = [(i, i ^ distance) for i in range(size)]
+        other = lax.ppermute(flat, axis, route)
+        flat = jnp.where(bit == 0, jnp.concatenate([flat, other]), jnp.concatenate([other, flat]))
+    return flat
+
+
+def apply_kernel(rows_ref, cols_ref, jac_ref, root_ref, base_ref, *refs):
+    out_refs = refs[:-1]
+    acc_ref = refs[-1]
     nblk = root_ref.shape[0]
+    rim = out_refs[0].shape[0]
     acc_ref[...] = jnp.zeros(acc_ref.shape, jnp.float32)
 
     def step(n, carry):
@@ -110,21 +141,21 @@
 
     lax.fori_loop(0, jac_ref.shape[0], step, 0)
     base_ref[...] = root_ref[...].astype(jnp.float32) + acc_ref[:nblk]
-    out_ref[...] = acc_ref[nblk:]
+    for k, out_ref in enumerate(out_refs):
+        out_ref[...] = acc_ref[nblk + k * rim:nblk + (k + 1) * rim]
 
 
 def apply_blocks(jac_rows, jac_cols, jac_blocks, root_blocks, slot_count):
     nblk, block, width = root_blocks.shape
+    rim = (slot_count - nblk) // 4
     smem = pl.BlockSpec(memory_space=pltpu.SMEM)
     vmem = pl.BlockSpec(memory_space=pltpu.VMEM)
     return pl.pallas_call(
         apply_kernel,
-        out_shape=(
-            jax.ShapeDtypeStruct((nblk, block, width), jnp.float32),
-            jax.ShapeDtypeStruct((slot_count - nblk, block, width), jnp.float32),
-        ),
+        out_shape=(jax.ShapeDtypeStruct((nblk, block, width), jnp.float32),)
+        + tuple(jax.ShapeDtypeStruct((rim, block, width), jnp.float32) for _ in range(4)),
         in_specs=[smem, smem, vmem, vmem],
-        out_specs=(vmem, vmem),
+        out_specs=(vmem,) * 5,
         scratch_shapes=[pltpu.VMEM((slot_count, block, width), jnp.float32)],
     )(jac_rows, jac_cols, jac_blocks, root_blocks)
 
@@ -176,16 +207,17 @@
     rim = landing.shape[0] // 4
     slot_count = nblk + 4 * rim
     blocks = covariance_root.reshape(nblk, block, mode_columns)
-    base, outgoing = apply_blocks(jac_rows, jac_cols, jac_blocks, blocks, slot_count)
-    from_next_x = shifted(outgoing[0:rim], "tx", -1)
-    from_prev_x = shifted(outgoing[rim:2 * rim], "tx", 1)
-    from_next_y = shifted(outgoing[2 * rim:3 * rim], "ty", -1)
-    from_prev_y = shifted(outgoing[3 * rim:], "ty", 1)
+    base, to_prev_x, to_next_x, to_prev_y, to_next_y = apply_blocks(
+        jac_rows, jac_cols, jac_blocks, blocks, slot_count)
+    from_next_x = shifted(to_prev_x, "tx", -1)
+    from_prev_x = shifted(to_next_x, "tx", 1)
+    from_next_y = shifted(to_prev_y, "ty", -1)
+    from_prev_y = shifted(to_next_y, "ty", 1)
     predicted_root, local_tiles = land_and_gram(
         landing, base, [from_next_x, from_prev_x, from_next_y, from_prev_y])
     total_rows = state_rows * lax.axis_size("tx") * lax.axis_size("ty")
     tiles = mode_columns // block
-    upper_sum = reduce_tiles(local_tiles)
+    upper_sum = halving_sum(local_tiles.reshape(-1)).reshape(local_tiles.shape)
     position = {}
     counter = 0
     for first in range(tiles):

time: 138 us -> 130 us (0.942)
  waiting for transfers between devices: 49.8 us -> 38.8 us
  starting transfers between devices: 18.1 us -> 24.3 us
  local copies, waits for them, and re-layouts: 5.63 us -> 3.01 us
    ppermute x5 -> x8, waiting for transfers between devices: 32.6 us -> 21.6 us  [the longest x4 11.3 us: halving_sum(): flat = kept + lax.ppermute(sent, axis, route)]
    ppermute x5 -> x8, starting transfers between devices: 6.89 us -> 13.1 us  [the longest x4 6.82 us: halving_sum(): flat = kept + lax.ppermute(sent, axis, route)]
    slice x1, local copies, waits for them, and re-layouts: 2.75 us -> 0.08 us  [per_device(): pieces.append(upper_sum[position[first, second]])]
  transfers between devices with their start and end apart: 9 -> 12, of which waited for: 7 -> 10; matrix products, arithmetic and copies ran while one was open for 0% -> 0% of each run, Pallas kernels for 0% -> 0%
where the time goes in v1:
time: 130 us; the launch traced here: 129 us
  Pallas kernels  61 us (47%)
  waiting for transfers between devices  38.8 us (30%)
  starting transfers between devices  24.3 us (19%)
  local copies, waits for them, and re-layouts  3.01 us (2%)
  other arithmetic  1.31 us (1%)
    pallas_call x1, Pallas kernels, factor_solve(): pl.pallas_call(factor_kernel, out_shape=(jax.ShapeDtypeStruct((m, n), jnp...  48 us
    ppermute x4, waiting for transfers between devices, shifted(): return lax.ppermute(block, axis, route)  17.2 us
    ppermute x4, waiting for transfers between devices, halving_sum(): flat = kept + lax.ppermute(sent, axis, route)  11.3 us
    ppermute x4, starting transfers between devices, shifted(): return lax.ppermute(block, axis, route)  11.2 us
    ppermute x4, waiting for transfers between devices, halving_sum(): other = lax.ppermute(flat, axis, route)  10.3 us
    pallas_call x1, Pallas kernels, apply_blocks(): pl.pallas_call(apply_kernel, out_shape=(jax.ShapeDtypeStruct((nblk, block...  8.18 us
    ppermute x4, starting transfers between devices, halving_sum(): flat = kept + lax.ppermute(sent, axis, route)  6.82 us
    ppermute x4, starting transfers between devices, halving_sum(): other = lax.ppermute(flat, axis, route)  6.27 us
  transfers between devices with their start and end apart: 12, of which 10 were waited for; matrix products, arithmetic and copies ran while one was open for 0% of the time, Pallas kernels for 0%

profile of v1, /device:TPU:0, one launch (start us, length us, event | category | flops | bytes accessed | tf_op | source)
XLA Modules:
  0.0 129.3 jit_solution(7000083412580553451)
XLA Ops:
  0.6 8.2 %shard_map.68 = (f32[4,128,512]{2,1,0:T(8,128)}, f32[2,128,512]{2,1,0:T(8,128)}, f32[2,128,512]{2,1,0:T(8,128)}, f32[2,128,512]{2,1,0:T(8,128)}, f32[2,128,512]{2,1,0:T(8,128)}) custom-call(s32[28]{0:T(128)} %rows_ref.1, s32[28]{0:T(128)} %cols_ref.1, bf16[28,128,128]{2,1,0:T(8,128)(2,1)} %jac_ref.1, bf16[4,128,512]{2,1,0:T(8,128)(2,1)} %bitcast.22), custom_call_target="tpu_custom_call" | custom-call | tf_op jit(solution)/shard_map/pallas_call | solution.py:153
  8.8 1.3 collective-permute-start
  10.1 5.5 %collective-permute-start.1 = (f32[2,128,512]{2,1,0:T(8,128)}, f32[2,128,512]{2,1,0:T(8,128)S(1)}, u32[]{:S(2)}, u32[]{:S(2)}) collective-permute-start(f32[2,128,512]{2,1,0:T(8,128)} %get-tuple-element.11), channel_id=1, source_target_pairs={{0,2},{2,4},{4,6},{6,8},{8,10},{10,12},{12,14},{1,3},{3,5},{5,7},{... | collective-permute-start | bytes 1572872 | tf_op jit(solution)/shard_map/ppermute | solution.py:73
  15.6 1.3 collective-permute-start.2
  16.9 3.1 %collective-permute-start.3 = (f32[2,128,512]{2,1,0:T(8,128)}, f32[2,128,512]{2,1,0:T(8,128)S(1)}, u32[]{:S(2)}, u32[]{:S(2)}) collective-permute-start(f32[2,128,512]{2,1,0:T(8,128)} %get-tuple-element.13), channel_id=1, source_target_pairs={{0,1},{2,3},{4,5},{6,7},{8,9},{10,11},{12,13},{14,15},{16,17},{18,... | collective-permute-start | bytes 1572872 | tf_op jit(solution)/shard_map/ppermute | solution.py:73
  20.0 5.7 %collective-permute-done.refs_0_ = f32[2,128,512]{2,1,0:T(8,128)S(1)} collective-permute-done((f32[2,128,512]{2,1,0:T(8,128)}, f32[2,128,512]{2,1,0:T(8,128)S(1)}, u32[]{:S(2)}, u32[]{:S(2)}) %collective-permute-start) | collective-permute-done | bytes 524320 | tf_op jit(solution)/shard_map/ppermute | solution.py:73
  25.8 0.0 copy-start.1
  25.8 11.5 %collective-permute-done.1.refs_1_ = f32[2,128,512]{2,1,0:T(8,128)S(1)} collective-permute-done((f32[2,128,512]{2,1,0:T(8,128)}, f32[2,128,512]{2,1,0:T(8,128)S(1)}, u32[]{:S(2)}, u32[]{:S(2)}) %collective-permute-start.1) | collective-permute-done | bytes 524320 | tf_op jit(solution)/shard_map/ppermute | solution.py:73
  37.3 0.0 copy-start.2
  37.3 0.0 collective-permute-done.2.refs_2_
  37.3 0.0 copy-start.3
  37.3 0.0 collective-permute-done.3.refs_3_
  37.3 0.0 copy-start.4
  37.3 0.0 copy-done.1
  37.3 0.8 copy-done.2
  38.1 0.2 copy-done.3
  38.3 0.2 copy-done.4
  38.4 4.9 %shard_map.69 = (f32[512,512]{1,0:T(8,128)}, f32[10,128,128]{2,1,0:T(8,128)}) custom-call(s32[8]{0:T(128)} %landing_ref.1, f32[4,128,512]{2,1,0:T(8,128)} %get-tuple-element.9.base_ref, f32[2,128,512]{2,1,0:T(8,128)} %copy-done.1, f32[2,128,512]{2,1,0:T(8,128)} %copy-done.2, f32[2,128,512]{2,1,0:T(8,128)} %copy-done.3, f32[2,128,512]{2,1,0:T(8,128)} %copy-done.4), custom_call_target="tpu_custom_call" | custom-call | tf_op jit(solution)/shard_map/pallas_call | solution.py:192
  43.3 0.0 copy-start
  43.3 1.1 dynamic_slice.25
  44.4 0.1 collective-permute-start.4
  44.5 1.6 %collective-permute-done.4 = f32[81920]{0:T(1024)S(1)} collective-permute-done((f32[81920]{0:T(1024)S(1)}, f32[81920]{0:T(1024)S(1)}, u32[]{:S(2)}, u32[]{:S(2)}) %collective-permute-start.4) | collective-permute-done | bytes 327712 | tf_op jit(solution)/shard_map/ppermute | solution.py:120
  46.1 0.0 copy-done
  46.2 2.4 %collective-permute-start.5 = (f32[40960]{0:T(1024)S(1)}, f32[40960]{0:T(1024)S(1)}, u32[]{:S(2)}, u32[]{:S(2)}) collective-permute-start(f32[40960]{0:T(1024)S(1)} %dynamic_slice.27), channel_id=1, source_target_pairs={{0,2},{2,0},{4,6},{6,4},{8,10},{10,8},{12,14},{14,12},{1,3},{3,1},... | collective-permute-start | bytes 491528 | tf_op jit(solution)/shard_map/ppermute | solution.py:120
  48.6 4.5 %collective-permute-done.5 = f32[40960]{0:T(1024)S(1)} collective-permute-done((f32[40960]{0:T(1024)S(1)}, f32[40960]{0:T(1024)S(1)}, u32[]{:S(2)}, u32[]{:S(2)}) %collective-permute-start.5) | collective-permute-done | bytes 163872 | tf_op jit(solution)/shard_map/ppermute | solution.py:120
  53.2 1.6 %collective-permute-start.6 = (f32[20480]{0:T(1024)S(1)}, f32[20480]{0:T(1024)S(1)}, u32[]{:S(2)}, u32[]{:S(2)}) collective-permute-start(f32[20480]{0:T(1024)S(1)} %dynamic_slice.29), channel_id=1, source_target_pairs={{0,4},{2,6},{4,0},{6,2},{8,12},{10,14},{12,8},{14,10},{1,5},{3,7},... | collective-permute-start | bytes 245768 | tf_op jit(solution)/shard_map/ppermute | solution.py:120
  54.8 2.9 %collective-permute-done.6 = f32[20480]{0:T(1024)S(1)} collective-permute-done((f32[20480]{0:T(1024)S(1)}, f32[20480]{0:T(1024)S(1)}, u32[]{:S(2)}, u32[]{:S(2)}) %collective-permute-start.6) | collective-permute-done | bytes 81952 | tf_op jit(solution)/shard_map/ppermute | solution.py:120
  57.7 2.7 %collective-permute-start.7 = (f32[10240]{0:T(1024)S(1)}, f32[10240]{0:T(1024)S(1)}, u32[]{:S(2)}, u32[]{:S(2)}) collective-permute-start(f32[10240]{0:T(1024)S(1)} %dynamic_slice.31), channel_id=1, source_target_pairs={{0,8},{2,10},{4,12},{6,14},{8,0},{10,2},{12,4},{14,6},{1,9},{3,11}... | collective-permute-start | bytes 122888 | tf_op jit(solution)/shard_map/ppermute | solution.py:120
  60.3 2.3 %collective-permute-done.7 = f32[10240]{0:T(1024)S(1)} collective-permute-done((f32[10240]{0:T(1024)S(1)}, f32[10240]{0:T(1024)S(1)}, u32[]{:S(2)}, u32[]{:S(2)}) %collective-permute-start.7) | collective-permute-done | bytes 40992 | tf_op jit(solution)/shard_map/ppermute | solution.py:120
  62.7 2.7 %collective-permute-start.8 = (f32[10240]{0:T(1024)S(1)}, f32[10240]{0:T(1024)S(1)}, u32[]{:S(2)}, u32[]{:S(2)}) collective-permute-start(f32[10240]{0:T(1024)S(1)} %dynamic-slice_add_fusion.3), channel_id=1, source_target_pairs={{0,8},{2,10},{4,12},{6,14},{8,0},{10,2},{12,4},{14,6},{1,9},{3,11}... | collective-permute-start | bytes 122888 | tf_op jit(solution)/shard_map/ppermute | solution.py:124
  65.4 2.4 %collective-permute-done.8 = f32[10240]{0:T(1024)S(1)} collective-permute-done((f32[10240]{0:T(1024)S(1)}, f32[10240]{0:T(1024)S(1)}, u32[]{:S(2)}, u32[]{:S(2)}) %collective-permute-start.8) | collective-permute-done | bytes 40992 | tf_op jit(solution)/shard_map/ppermute | solution.py:124
  67.8 1.7 %collective-permute-start.9 = (f32[20480]{0:T(1024)S(1)}, f32[20480]{0:T(1024)S(1)}, u32[]{:S(2)}, u32[]{:S(2)}) collective-permute-start(f32[20480]{0:T(1024)S(1)} %maximum_select_fusion.6), channel_id=1, source_target_pairs={{0,4},{2,6},{4,0},{6,2},{8,12},{10,14},{12,8},{14,10},{1,5},{3,7},... | collective-permute-start | bytes 245768 | tf_op jit(solution)/shard_map/ppermute | solution.py:124
  69.4 2.8 %collective-permute-done.9 = f32[20480]{0:T(1024)S(1)} collective-permute-done((f32[20480]{0:T(1024)S(1)}, f32[20480]{0:T(1024)S(1)}, u32[]{:S(2)}, u32[]{:S(2)}) %collective-permute-start.9) | collective-permute-done | bytes 81952 | tf_op jit(solution)/shard_map/ppermute | solution.py:124
  72.3 1.8 %collective-permute-start.10 = (f32[40960]{0:T(1024)S(1)}, f32[40960]{0:T(1024)S(1)}, u32[]{:S(2)}, u32[]{:S(2)}) collective-permute-start(f32[40960]{0:T(1024)S(1)} %maximum_select_fusion.4), channel_id=1, source_target_pairs={{0,2},{2,0},{4,6},{6,4},{8,10},{10,8},{12,14},{14,12},{1,3},{3,1},... | collective-permute-start | bytes 491528 | tf_op jit(solution)/shard_map/ppermute | solution.py:124
  74.1 3.6 %collective-permute-done.10 = f32[40960]{0:T(1024)S(1)} collective-permute-done((f32[40960]{0:T(1024)S(1)}, f32[40960]{0:T(1024)S(1)}, u32[]{:S(2)}, u32[]{:S(2)}) %collective-permute-start.10) | collective-permute-done | bytes 163872 | tf_op jit(solution)/shard_map/ppermute | solution.py:124
  77.7 0.1 collective-permute-start.11
  77.8 1.5 %collective-permute-done.11 = f32[81920]{0:T(1024)S(1)} collective-permute-done((f32[81920]{0:T(1024)S(1)}, f32[81920]{0:T(1024)S(1)}, u32[]{:S(2)}, u32[]{:S(2)}) %collective-permute-start.11) | collective-permute-done | bytes 327712 | tf_op jit(solution)/shard_map/ppermute | solution.py:124
  79.4 0.1 fusion
  79.5 0.1 copy.12
  79.6 0.1 copy.16
  79.7 0.1 copy.11
  79.8 0.1 copy.15
  79.9 0.1 copy.10
  80.0 0.1 copy.14
  80.2 0.1 copy.13
  80.3 1.1 maximum_multiply_fusion.g_ref
  81.4 48.0 %shard_map.70 = (bf16[512,512]{1,0:T(8,128)(2,1)}, f32[512,512]{1,0:T(8,128)}) custom-call(f32[512,512]{1,0:T(8,128)} %maximum_multiply_fusion.g_ref, f32[512,512]{1,0:T(8,128)} %get-tuple-element.15.f_ref), custom_call_target="tpu_custom_call" | custom-call | tf_op jit(solution)/shard_map/pallas_call | solution.py:57
  (15 shorter events, 0.3 us)
Async XLA Ops:
  8.8 17.0 %collective-permute-start = (f32[2,128,512]{2,1,0:T(8,128)}, f32[2,128,512]{2,1,0:T(8,128)S(1)}, u32[]{:S(2)}, u32[]{:S(2)}) collective-permute-start(f32[2,128,512]{2,1,0:T(8,128)} %get-tuple-element.10), channel_id=1, source_target_pairs={{2,0},{4,2},{6,4},{8,6},{10,8},{12,10},{14,12},{3,1},{5,3},{7,5},{... | collective-permute-start | bytes 1572872 | tf_op jit(solution)/shard_map/ppermute | solution.py:73
  10.1 27.2 %collective-permute-start.1 = (f32[2,128,512]{2,1,0:T(8,128)}, f32[2,128,512]{2,1,0:T(8,128)S(1)}, u32[]{:S(2)}, u32[]{:S(2)}) collective-permute-start(f32[2,128,512]{2,1,0:T(8,128)} %get-tuple-element.11), channel_id=1, source_target_pairs={{0,2},{2,4},{4,6},{6,8},{8,10},{10,12},{12,14},{1,3},{3,5},{5,7},{... | collective-permute-start | bytes 1572872 | tf_op jit(solution)/shard_map/ppermute | solution.py:73
  15.6 21.7 %collective-permute-start.2 = (f32[2,128,512]{2,1,0:T(8,128)}, f32[2,128,512]{2,1,0:T(8,128)S(1)}, u32[]{:S(2)}, u32[]{:S(2)}) collective-permute-start(f32[2,128,512]{2,1,0:T(8,128)} %get-tuple-element.12), channel_id=1, source_target_pairs={{1,0},{3,2},{5,4},{7,6},{9,8},{11,10},{13,12},{15,14},{17,16},{19,... | collective-permute-start | bytes 1572872 | tf_op jit(solution)/shard_map/ppermute | solution.py:73
  16.9 20.4 %collective-permute-start.3 = (f32[2,128,512]{2,1,0:T(8,128)}, f32[2,128,512]{2,1,0:T(8,128)S(1)}, u32[]{:S(2)}, u32[]{:S(2)}) collective-permute-start(f32[2,128,512]{2,1,0:T(8,128)} %get-tuple-element.13), channel_id=1, source_target_pairs={{0,1},{2,3},{4,5},{6,7},{8,9},{10,11},{12,13},{14,15},{16,17},{18,... | collective-permute-start | bytes 1572872 | tf_op jit(solution)/shard_map/ppermute | solution.py:73
  25.8 11.5 %copy-start.1 = (f32[2,128,512]{2,1,0:T(8,128)}, f32[2,128,512]{2,1,0:T(8,128)S(1)}, u32[]{:S(2)}) copy-start(f32[2,128,512]{2,1,0:T(8,128)S(1)} %collective-permute-done.refs_0_) | copy-start | bytes 1572868
  37.3 0.8 copy-start.2
  37.3 1.0 copy-start.3
  37.3 1.1 copy-start.4
  43.3 2.8 %copy-start = (f32[10,128,128]{2,1,0:T(8,128)S(1)}, f32[10,128,128]{2,1,0:T(8,128)}, u32[]{:S(2)}) copy-start(f32[10,128,128]{2,1,0:T(8,128)} %get-tuple-element.14) | copy-start | bytes 1966084
  44.4 1.7 %collective-permute-start.4 = (f32[81920]{0:T(1024)S(1)}, f32[81920]{0:T(1024)S(1)}, u32[]{:S(2)}, u32[]{:S(2)}) collective-permute-start(f32[81920]{0:T(1024)S(1)} %dynamic_slice.25), channel_id=1, source_target_pairs={{0,1},{1,0},{2,3},{3,2},{4,5},{5,4},{6,7},{7,6},{8,9},{9,8},{10,11... | collective-permute-start | bytes 983048 | tf_op jit(solution)/shard_map/ppermute | solution.py:120
  46.2 6.9 %collective-permute-start.5 = (f32[40960]{0:T(1024)S(1)}, f32[40960]{0:T(1024)S(1)}, u32[]{:S(2)}, u32[]{:S(2)}) collective-permute-start(f32[40960]{0:T(1024)S(1)} %dynamic_slice.27), channel_id=1, source_target_pairs={{0,2},{2,0},{4,6},{6,4},{8,10},{10,8},{12,14},{14,12},{1,3},{3,1},... | collective-permute-start | bytes 491528 | tf_op jit(solution)/shard_map/ppermute | solution.py:120
  53.2 4.5 %collective-permute-start.6 = (f32[20480]{0:T(1024)S(1)}, f32[20480]{0:T(1024)S(1)}, u32[]{:S(2)}, u32[]{:S(2)}) collective-permute-start(f32[20480]{0:T(1024)S(1)} %dynamic_slice.29), channel_id=1, source_target_pairs={{0,4},{2,6},{4,0},{6,2},{8,12},{10,14},{12,8},{14,10},{1,5},{3,7},... | collective-permute-start | bytes 245768 | tf_op jit(solution)/shard_map/ppermute | solution.py:120
  57.7 5.0 %collective-permute-start.7 = (f32[10240]{0:T(1024)S(1)}, f32[10240]{0:T(1024)S(1)}, u32[]{:S(2)}, u32[]{:S(2)}) collective-permute-start(f32[10240]{0:T(1024)S(1)} %dynamic_slice.31), channel_id=1, source_target_pairs={{0,8},{2,10},{4,12},{6,14},{8,0},{10,2},{12,4},{14,6},{1,9},{3,11}... | collective-permute-start | bytes 122888 | tf_op jit(solution)/shard_map/ppermute | solution.py:120
  62.7 5.1 %collective-permute-start.8 = (f32[10240]{0:T(1024)S(1)}, f32[10240]{0:T(1024)S(1)}, u32[]{:S(2)}, u32[]{:S(2)}) collective-permute-start(f32[10240]{0:T(1024)S(1)} %dynamic-slice_add_fusion.3), channel_id=1, source_target_pairs={{0,8},{2,10},{4,12},{6,14},{8,0},{10,2},{12,4},{14,6},{1,9},{3,11}... | collective-permute-start | bytes 122888 | tf_op jit(solution)/shard_map/ppermute | solution.py:124
  67.8 4.5 %collective-permute-start.9 = (f32[20480]{0:T(1024)S(1)}, f32[20480]{0:T(1024)S(1)}, u32[]{:S(2)}, u32[]{:S(2)}) collective-permute-start(f32[20480]{0:T(1024)S(1)} %maximum_select_fusion.6), channel_id=1, source_target_pairs={{0,4},{2,6},{4,0},{6,2},{8,12},{10,14},{12,8},{14,10},{1,5},{3,7},... | collective-permute-start | bytes 245768 | tf_op jit(solution)/shard_map/ppermute | solution.py:124
  72.3 5.4 %collective-permute-start.10 = (f32[40960]{0:T(1024)S(1)}, f32[40960]{0:T(1024)S(1)}, u32[]{:S(2)}, u32[]{:S(2)}) collective-permute-start(f32[40960]{0:T(1024)S(1)} %maximum_select_fusion.4), channel_id=1, source_target_pairs={{0,2},{2,0},{4,6},{6,4},{8,10},{10,8},{12,14},{14,12},{1,3},{3,1},... | collective-permute-start | bytes 491528 | tf_op jit(solution)/shard_map/ppermute | solution.py:124
  77.7 1.7 %collective-permute-start.11 = (f32[81920]{0:T(1024)S(1)}, f32[81920]{0:T(1024)S(1)}, u32[]{:S(2)}, u32[]{:S(2)}) collective-permute-start(f32[81920]{0:T(1024)S(1)} %maximum_select_fusion.2), channel_id=1, source_target_pairs={{0,1},{1,0},{2,3},{3,2},{4,5},{5,4},{6,7},{7,6},{8,9},{9,8},{10,11... | collective-permute-start | bytes 983048 | tf_op jit(solution)/shard_map/ppermute | solution.py:124

commit v2 on v1

--- a/solution.py
+++ b/solution.py
@@ -98,31 +98,52 @@
     return jnp.where(side == 0, jnp.concatenate([kept, other]), jnp.concatenate([other, kept]))
 
 
-def halving_sum(flat):
+def group_levels():
     levels = []
-    for axis in ("ty", "tx"):
+    for axis, width in (("ty", 1), ("tx", 2)):
         size = lax.axis_size(axis)
-        distance = 1
-        while distance < size:
-            levels.append((axis, size, distance))
-            distance *= 2
-    pieces = 2 ** len(levels)
-    regular = all(size & (size - 1) == 0 for _, size, _ in levels)
-    if not regular or flat.shape[0] % pieces:
+        if size & (size - 1):
+            return None
+        stride = 1
+        while stride < size:
+            bits = min(width, (size // stride).bit_length() - 1)
+            levels.append((axis, size, stride, 2 ** bits))
+            stride *= 2 ** bits
+    return levels
+
+
+def grouped_sum(flat):
+    levels = group_levels()
+    if levels is None:
         return doubling_sum(doubling_sum(flat, "tx"), "ty")
-    bits = []
-    for axis, size, distance in levels:
-        bit = lax.axis_index(axis) // distance % 2
-        route = [(i, i ^ distance) for i in range(size)]
-        half = flat.shape[0] // 2
-        sent = lax.dynamic_slice_in_dim(flat, (1 - bit) * half, half)
-        kept = lax.dynamic_slice_in_dim(flat, bit * half, half)
-        flat = kept + lax.ppermute(sent, axis, route)
-        bits.append(bit)
-    for (axis, size, distance), bit in reversed(list(zip(levels, bits))):
-        route = [(i, i ^ distance) for i in range(size)]
-        other = lax.ppermute(flat, axis, route)
-        flat = jnp.where(bit == 0, jnp.concatenate([flat, other]), jnp.concatenate([other, flat]))
+    pieces = 1
+    for level in levels:
+        pieces *= level[3]
+    if flat.shape[0] % pieces:
+        return doubling_sum(doubling_sum(flat, "tx"), "ty")
+    digits = []
+    for axis, size, stride, group in levels:
+        digit = lax.axis_index(axis) // stride % group
+        chunk = flat.shape[0] // group
+        kept = lax.dynamic_slice_in_dim(flat, digit * chunk, chunk)
+        for offset in range(1, group):
+            route = [(i, i ^ (offset * stride)) for i in range(size)]
+            sent = lax.dynamic_slice_in_dim(flat, (digit ^ offset) * chunk, chunk)
+            kept = kept + lax.ppermute(sent, axis, route)
+        flat = kept
+        digits.append(digit)
+    for (axis, size, stride, group), digit in reversed(list(zip(levels, digits))):
+        got = [flat]
+        for offset in range(1, group):
+            route = [(i, i ^ (offset * stride)) for i in range(size)]
+            got.append(lax.ppermute(flat, axis, route))
+        placed = []
+        for position in range(group):
+            pick = got[0]
+            for offset in range(1, group):
+                pick = jnp.where((digit ^ offset) == position, got[offset], pick)
+            placed.append(pick)
+        flat = jnp.concatenate(placed)
     return flat
 
 
@@ -139,7 +160,7 @@
             jac_ref[n], root_ref[cols_ref[n]], preferred_element_type=jnp.float32)
         return carry
 
-    lax.fori_loop(0, jac_ref.shape[0], step, 0)
+    lax.fori_loop(0, jac_ref.shape[0], step, 0, unroll=True)
     base_ref[...] = root_ref[...].astype(jnp.float32) + acc_ref[:nblk]
     for k, out_ref in enumerate(out_refs):
         out_ref[...] = acc_ref[nblk + k * rim:nblk + (k + 1) * rim]
@@ -217,7 +238,7 @@
         landing, base, [from_next_x, from_prev_x, from_next_y, from_prev_y])
     total_rows = state_rows * lax.axis_size("tx") * lax.axis_size("ty")
     tiles = mode_columns // block
-    upper_sum = halving_sum(local_tiles.reshape(-1)).reshape(local_tiles.shape)
+    upper_sum = grouped_sum(local_tiles.reshape(-1)).reshape(local_tiles.shape)
     position = {}
     counter = 0
     for first in range(tiles):

time: 130 us -> 120 us (0.923)
  waiting for transfers between devices: 38.8 us -> 33.4 us
  Pallas kernels: 61 us -> 57.1 us
    ppermute x8 -> x10, waiting for transfers between devices: 21.6 us -> 16.1 us  [the longest x5 8.14 us: grouped_sum(): kept = kept + lax.ppermute(sent, axis, route)]
    pallas_call x1, Pallas kernels: 8.18 us -> 4.3 us  [apply_blocks(): pl.pallas_call(apply_kernel, out_shape=(jax.ShapeDtypeStruct((nblk, block...]
    ppermute x8 -> x10, starting transfers between devices: 13.1 us -> 13.1 us  [the longest x5 6.82 us: grouped_sum(): kept = kept + lax.ppermute(sent, axis, route)]
  transfers between devices with their start and end apart: 12 -> 14, of which waited for: 10 -> 12; matrix products, arithmetic and copies ran while one was open for 0% -> 0% of each run, Pallas kernels for 0% -> 0%
where the time goes in v2:
time: 120 us
  Pallas kernels  57.1 us (48%)
  waiting for transfers between devices  33.4 us (28%)
  starting transfers between devices  24.2 us (20%)
  local copies, waits for them, and re-layouts  2.83 us (2%)
  other arithmetic  1.25 us (1%)
    pallas_call x1, Pallas kernels, factor_solve(): pl.pallas_call(factor_kernel, out_shape=(jax.ShapeDtypeStruct((m, n), jnp...  47.9 us
    ppermute x4, waiting for transfers between devices, shifted(): return lax.ppermute(block, axis, route)  17.2 us
    ppermute x4, starting transfers between devices, shifted(): return lax.ppermute(block, axis, route)  11.2 us
    ppermute x5, waiting for transfers between devices, grouped_sum(): kept = kept + lax.ppermute(sent, axis, route)  8.14 us
    ppermute x5, waiting for transfers between devices, grouped_sum(): got.append(lax.ppermute(flat, axis, route))  7.98 us
    ppermute x5, starting transfers between devices, grouped_sum(): kept = kept + lax.ppermute(sent, axis, route)  6.82 us
    ppermute x5, starting transfers between devices, grouped_sum(): got.append(lax.ppermute(flat, axis, route))  6.26 us
    pallas_call x1, Pallas kernels, land_and_gram(): pl.pallas_call(land_kernel, out_shape=(jax.ShapeDtypeStruct((nblk * block...  4.89 us
  transfers between devices with their start and end apart: 14, of which 12 were waited for; matrix products, arithmetic and copies ran while one was open for 0% of the time, Pallas kernels for 0%

profile of v2, /device:TPU:0, one launch (start us, length us, event | category | flops | bytes accessed | tf_op | source)
XLA Modules:
  0.0 119.7 jit_solution(9220227564265402569)
XLA Ops:
  0.6 4.3 %shard_map.68 = (f32[4,128,512]{2,1,0:T(8,128)}, f32[2,128,512]{2,1,0:T(8,128)}, f32[2,128,512]{2,1,0:T(8,128)}, f32[2,128,512]{2,1,0:T(8,128)}, f32[2,128,512]{2,1,0:T(8,128)}) custom-call(s32[28]{0:T(128)} %rows_ref.1, s32[28]{0:T(128)} %cols_ref.1, bf16[28,128,128]{2,1,0:T(8,128)(2,1)} %jac_ref.1, bf16[4,128,512]{2,1,0:T(8,128)(2,1)} %bitcast.30), custom_call_target="tpu_custom_call" | custom-call | tf_op jit(solution)/shard_map/pallas_call | solution.py:174
  4.9 1.3 %collective-permute-start = (f32[2,128,512]{2,1,0:T(8,128)}, f32[2,128,512]{2,1,0:T(8,128)S(1)}, u32[]{:S(2)}, u32[]{:S(2)}) collective-permute-start(f32[2,128,512]{2,1,0:T(8,128)} %get-tuple-element.10), channel_id=1, source_target_pairs={{2,0},{4,2},{6,4},{8,6},{10,8},{12,10},{14,12},{3,1},{5,3},{7,5},{... | collective-permute-start | bytes 1572872 | tf_op jit(solution)/shard_map/ppermute | solution.py:73
  6.2 5.5 %collective-permute-start.1 = (f32[2,128,512]{2,1,0:T(8,128)}, f32[2,128,512]{2,1,0:T(8,128)S(1)}, u32[]{:S(2)}, u32[]{:S(2)}) collective-permute-start(f32[2,128,512]{2,1,0:T(8,128)} %get-tuple-element.11), channel_id=1, source_target_pairs={{0,2},{2,4},{4,6},{6,8},{8,10},{10,12},{12,14},{1,3},{3,5},{5,7},{... | collective-permute-start | bytes 1572872 | tf_op jit(solution)/shard_map/ppermute | solution.py:73
  11.7 1.3 %collective-permute-start.2 = (f32[2,128,512]{2,1,0:T(8,128)}, f32[2,128,512]{2,1,0:T(8,128)S(1)}, u32[]{:S(2)}, u32[]{:S(2)}) collective-permute-start(f32[2,128,512]{2,1,0:T(8,128)} %get-tuple-element.12), channel_id=1, source_target_pairs={{1,0},{3,2},{5,4},{7,6},{9,8},{11,10},{13,12},{15,14},{17,16},{19,... | collective-permute-start | bytes 1572872 | tf_op jit(solution)/shard_map/ppermute | solution.py:73
  13.0 3.1 %collective-permute-start.3 = (f32[2,128,512]{2,1,0:T(8,128)}, f32[2,128,512]{2,1,0:T(8,128)S(1)}, u32[]{:S(2)}, u32[]{:S(2)}) collective-permute-start(f32[2,128,512]{2,1,0:T(8,128)} %get-tuple-element.13), channel_id=1, source_target_pairs={{0,1},{2,3},{4,5},{6,7},{8,9},{10,11},{12,13},{14,15},{16,17},{18,... | collective-permute-start | bytes 1572872 | tf_op jit(solution)/shard_map/ppermute | solution.py:73
  16.1 5.7 %collective-permute-done.refs_0_ = f32[2,128,512]{2,1,0:T(8,128)S(1)} collective-permute-done((f32[2,128,512]{2,1,0:T(8,128)}, f32[2,128,512]{2,1,0:T(8,128)S(1)}, u32[]{:S(2)}, u32[]{:S(2)}) %collective-permute-start) | collective-permute-done | bytes 524320 | tf_op jit(solution)/shard_map/ppermute | solution.py:73
  21.9 0.0 copy-start.1
  21.9 11.5 %collective-permute-done.1.refs_1_ = f32[2,128,512]{2,1,0:T(8,128)S(1)} collective-permute-done((f32[2,128,512]{2,1,0:T(8,128)}, f32[2,128,512]{2,1,0:T(8,128)S(1)}, u32[]{:S(2)}, u32[]{:S(2)}) %collective-permute-start.1) | collective-permute-done | bytes 524320 | tf_op jit(solution)/shard_map/ppermute | solution.py:73
  33.4 0.0 copy-start.2
  33.4 0.0 collective-permute-done.2.refs_2_
  33.4 0.0 copy-start.3
  33.4 0.0 collective-permute-done.3.refs_3_
  33.4 0.0 copy-start.4
  33.4 0.0 copy-done.1
  33.4 0.8 copy-done.2
  34.2 0.2 copy-done.3
  34.4 0.2 copy-done.4
  34.5 4.9 %shard_map.69 = (f32[512,512]{1,0:T(8,128)}, f32[10,128,128]{2,1,0:T(8,128)}) custom-call(s32[8]{0:T(128)} %landing_ref.1, f32[4,128,512]{2,1,0:T(8,128)} %get-tuple-element.9.base_ref, f32[2,128,512]{2,1,0:T(8,128)} %copy-done.1, f32[2,128,512]{2,1,0:T(8,128)} %copy-done.2, f32[2,128,512]{2,1,0:T(8,128)} %copy-done.3, f32[2,128,512]{2,1,0:T(8,128)} %copy-done.4), custom_call_target="tpu_custom_call" | custom-call | tf_op jit(solution)/shard_map/pallas_call | solution.py:213
  39.4 1.1 dynamic_slice.25
  40.5 0.1 collective-permute-start.4
  40.6 1.6 %collective-permute-done.4 = f32[81920]{0:T(1024)S(1)} collective-permute-done((f32[81920]{0:T(1024)S(1)}, f32[81920]{0:T(1024)S(1)}, u32[]{:S(2)}, u32[]{:S(2)}) %collective-permute-start.4) | collective-permute-done | bytes 327712 | tf_op jit(solution)/shard_map/ppermute | solution.py:132
  42.2 0.0 copy-done
  42.3 3.5 %collective-permute-start.7 = (f32[20480]{0:T(1024)S(1)}, f32[20480]{0:T(1024)S(1)}, u32[]{:S(2)}, u32[]{:S(2)}) collective-permute-start(f32[20480]{0:T(1024)S(1)} %get-tuple-element.32), channel_id=1, source_target_pairs={{0,6},{2,4},{4,2},{6,0},{8,14},{10,12},{12,10},{14,8},{1,7},{3,5},... | collective-permute-start | bytes 245768 | tf_op jit(solution)/shard_map/ppermute | solution.py:132
  45.7 0.4 collective-permute-start.6
  46.2 0.2 collective-permute-start.5
  46.4 2.6 %collective-permute-done.7 = f32[20480]{0:T(1024)S(1)} collective-permute-done((f32[20480]{0:T(1024)S(1)}, f32[20480]{0:T(1024)S(1)}, u32[]{:S(2)}, u32[]{:S(2)}) %collective-permute-start.7) | collective-permute-done | bytes 81952 | tf_op jit(solution)/shard_map/ppermute | solution.py:132
  48.9 1.4 %collective-permute-done.6 = f32[20480]{0:T(1024)S(1)} collective-permute-done((f32[20480]{0:T(1024)S(1)}, f32[20480]{0:T(1024)S(1)}, u32[]{:S(2)}, u32[]{:S(2)}) %collective-permute-start.6) | collective-permute-done | bytes 81952 | tf_op jit(solution)/shard_map/ppermute | solution.py:132
  50.4 0.2 collective-permute-done.5
  50.6 2.6 %collective-permute-start.8 = (f32[10240]{0:T(1024)S(1)}, f32[10240]{0:T(1024)S(1)}, u32[]{:S(2)}, u32[]{:S(2)}) collective-permute-start(f32[10240]{0:T(1024)S(1)} %dynamic_slice.31), channel_id=1, source_target_pairs={{0,8},{2,10},{4,12},{6,14},{8,0},{10,2},{12,4},{14,6},{1,9},{3,11}... | collective-permute-start | bytes 122888 | tf_op jit(solution)/shard_map/ppermute | solution.py:132
  53.3 2.3 %collective-permute-done.8 = f32[10240]{0:T(1024)S(1)} collective-permute-done((f32[10240]{0:T(1024)S(1)}, f32[10240]{0:T(1024)S(1)}, u32[]{:S(2)}, u32[]{:S(2)}) %collective-permute-start.8) | collective-permute-done | bytes 40992 | tf_op jit(solution)/shard_map/ppermute | solution.py:132
  55.6 2.6 %collective-permute-start.9 = (f32[10240]{0:T(1024)S(1)}, f32[10240]{0:T(1024)S(1)}, u32[]{:S(2)}, u32[]{:S(2)}) collective-permute-start(f32[10240]{0:T(1024)S(1)} %dynamic-slice_add_fusion.1), channel_id=1, source_target_pairs={{0,8},{2,10},{4,12},{6,14},{8,0},{10,2},{12,4},{14,6},{1,9},{3,11}... | collective-permute-start | bytes 122888 | tf_op jit(solution)/shard_map/ppermute | solution.py:139
  58.3 2.3 %collective-permute-done.9 = f32[10240]{0:T(1024)S(1)} collective-permute-done((f32[10240]{0:T(1024)S(1)}, f32[10240]{0:T(1024)S(1)}, u32[]{:S(2)}, u32[]{:S(2)}) %collective-permute-start.9) | collective-permute-done | bytes 40992 | tf_op jit(solution)/shard_map/ppermute | solution.py:139
  60.6 2.3 %collective-permute-start.10 = (f32[20480]{0:T(1024)S(1)}, f32[20480]{0:T(1024)S(1)}, u32[]{:S(2)}, u32[]{:S(2)}) collective-permute-start(f32[20480]{0:T(1024)S(1)} %pad_maximum_fusion.1), channel_id=1, source_target_pairs={{0,6},{2,4},{4,2},{6,0},{8,14},{10,12},{12,10},{14,8},{1,7},{3,5},... | collective-permute-start | bytes 245768 | tf_op jit(solution)/shard_map/ppermute | solution.py:139
  62.9 0.8 collective-permute-start.11
  63.8 0.4 collective-permute-start.12
  64.2 1.9 %collective-permute-done.10 = f32[20480]{0:T(1024)S(1)} collective-permute-done((f32[20480]{0:T(1024)S(1)}, f32[20480]{0:T(1024)S(1)}, u32[]{:S(2)}, u32[]{:S(2)}) %collective-permute-start.10) | collective-permute-done | bytes 81952 | tf_op jit(solution)/shard_map/ppermute | solution.py:139
  66.0 1.4 %collective-permute-done.11 = f32[20480]{0:T(1024)S(1)} collective-permute-done((f32[20480]{0:T(1024)S(1)}, f32[20480]{0:T(1024)S(1)}, u32[]{:S(2)}, u32[]{:S(2)}) %collective-permute-start.11) | collective-permute-done | bytes 81952 | tf_op jit(solution)/shard_map/ppermute | solution.py:139
  67.4 0.8 collective-permute-done.12
  68.3 0.1 collective-permute-start.13
  68.4 1.6 %collective-permute-done.13 = f32[81920]{0:T(1024)S(1)} collective-permute-done((f32[81920]{0:T(1024)S(1)}, f32[81920]{0:T(1024)S(1)}, u32[]{:S(2)}, u32[]{:S(2)}) %collective-permute-start.13) | collective-permute-done | bytes 327712 | tf_op jit(solution)/shard_map/ppermute | solution.py:139
  70.1 0.1 copy.20
  70.2 0.1 copy.19
  70.3 0.1 copy.18
  70.4 0.1 copy.17
  70.5 0.1 copy.16
  70.6 0.1 copy.15
  70.7 1.0 maximum_multiply_fusion.g_ref
  71.8 47.9 %shard_map.70 = (bf16[512,512]{1,0:T(8,128)(2,1)}, f32[512,512]{1,0:T(8,128)}) custom-call(f32[512,512]{1,0:T(8,128)} %maximum_multiply_fusion.g_ref, f32[512,512]{1,0:T(8,128)} %get-tuple-element.15.f_ref), custom_call_target="tpu_custom_call" | custom-call | tf_op jit(solution)/shard_map/pallas_call | solution.py:57
  (13 shorter events, 0.3 us)
Async XLA Ops:
  4.9 17.0 %collective-permute-start = (f32[2,128,512]{2,1,0:T(8,128)}, f32[2,128,512]{2,1,0:T(8,128)S(1)}, u32[]{:S(2)}, u32[]{:S(2)}) collective-permute-start(f32[2,128,512]{2,1,0:T(8,128)} %get-tuple-element.10), channel_id=1, source_target_pairs={{2,0},{4,2},{6,4},{8,6},{10,8},{12,10},{14,12},{3,1},{5,3},{7,5},{... | collective-permute-start | bytes 1572872 | tf_op jit(solution)/shard_map/ppermute | solution.py:73
  6.2 27.2 %collective-permute-start.1 = (f32[2,128,512]{2,1,0:T(8,128)}, f32[2,128,512]{2,1,0:T(8,128)S(1)}, u32[]{:S(2)}, u32[]{:S(2)}) collective-permute-start(f32[2,128,512]{2,1,0:T(8,128)} %get-tuple-element.11), channel_id=1, source_target_pairs={{0,2},{2,4},{4,6},{6,8},{8,10},{10,12},{12,14},{1,3},{3,5},{5,7},{... | collective-permute-start | bytes 1572872 | tf_op jit(solution)/shard_map/ppermute | solution.py:73
  11.7 21.7 %collective-permute-start.2 = (f32[2,128,512]{2,1,0:T(8,128)}, f32[2,128,512]{2,1,0:T(8,128)S(1)}, u32[]{:S(2)}, u32[]{:S(2)}) collective-permute-start(f32[2,128,512]{2,1,0:T(8,128)} %get-tuple-element.12), channel_id=1, source_target_pairs={{1,0},{3,2},{5,4},{7,6},{9,8},{11,10},{13,12},{15,14},{17,16},{19,... | collective-permute-start | bytes 1572872 | tf_op jit(solution)/shard_map/ppermute | solution.py:73
  13.0 20.4 %collective-permute-start.3 = (f32[2,128,512]{2,1,0:T(8,128)}, f32[2,128,512]{2,1,0:T(8,128)S(1)}, u32[]{:S(2)}, u32[]{:S(2)}) collective-permute-start(f32[2,128,512]{2,1,0:T(8,128)} %get-tuple-element.13), channel_id=1, source_target_pairs={{0,1},{2,3},{4,5},{6,7},{8,9},{10,11},{12,13},{14,15},{16,17},{18,... | collective-permute-start | bytes 1572872 | tf_op jit(solution)/shard_map/ppermute | solution.py:73
  21.9 11.5 %copy-start.1 = (f32[2,128,512]{2,1,0:T(8,128)}, f32[2,128,512]{2,1,0:T(8,128)S(1)}, u32[]{:S(2)}) copy-start(f32[2,128,512]{2,1,0:T(8,128)S(1)} %collective-permute-done.refs_0_) | copy-start | bytes 1572868
  33.4 0.8 copy-start.2
  33.4 1.0 copy-start.3
  33.4 1.1 copy-start.4
  39.4 2.8 %copy-start = (f32[10,128,128]{2,1,0:T(8,128)S(1)}, f32[10,128,128]{2,1,0:T(8,128)}, u32[]{:S(2)}) copy-start(f32[10,128,128]{2,1,0:T(8,128)} %get-tuple-element.14) | copy-start | bytes 1966084
  40.5 1.7 %collective-permute-start.4 = (f32[81920]{0:T(1024)S(1)}, f32[81920]{0:T(1024)S(1)}, u32[]{:S(2)}, u32[]{:S(2)}) collective-permute-start(f32[81920]{0:T(1024)S(1)} %dynamic_slice.25), channel_id=1, source_target_pairs={{0,1},{1,0},{2,3},{3,2},{4,5},{5,4},{6,7},{7,6},{8,9},{9,8},{10,11... | collective-permute-start | bytes 983048 | tf_op jit(solution)/shard_map/ppermute | solution.py:132
  42.3 6.7 %collective-permute-start.7 = (f32[20480]{0:T(1024)S(1)}, f32[20480]{0:T(1024)S(1)}, u32[]{:S(2)}, u32[]{:S(2)}) collective-permute-start(f32[20480]{0:T(1024)S(1)} %get-tuple-element.32), channel_id=1, source_target_pairs={{0,6},{2,4},{4,2},{6,0},{8,14},{10,12},{12,10},{14,8},{1,7},{3,5},... | collective-permute-start | bytes 245768 | tf_op jit(solution)/shard_map/ppermute | solution.py:132
  45.7 4.7 %collective-permute-start.6 = (f32[20480]{0:T(1024)S(1)}, f32[20480]{0:T(1024)S(1)}, u32[]{:S(2)}, u32[]{:S(2)}) collective-permute-start(f32[20480]{0:T(1024)S(1)} %get-tuple-element.33), channel_id=1, source_target_pairs={{0,4},{2,6},{4,0},{6,2},{8,12},{10,14},{12,8},{14,10},{1,5},{3,7},... | collective-permute-start | bytes 245768 | tf_op jit(solution)/shard_map/ppermute | solution.py:132
  46.2 4.4 %collective-permute-start.5 = (f32[20480]{0:T(1024)S(1)}, f32[20480]{0:T(1024)S(1)}, u32[]{:S(2)}, u32[]{:S(2)}) collective-permute-start(f32[20480]{0:T(1024)S(1)} %get-tuple-element.31), channel_id=1, source_target_pairs={{0,2},{2,0},{4,6},{6,4},{8,10},{10,8},{12,14},{14,12},{1,3},{3,1},... | collective-permute-start | bytes 245768 | tf_op jit(solution)/shard_map/ppermute | solution.py:132
  50.6 5.0 %collective-permute-start.8 = (f32[10240]{0:T(1024)S(1)}, f32[10240]{0:T(1024)S(1)}, u32[]{:S(2)}, u32[]{:S(2)}) collective-permute-start(f32[10240]{0:T(1024)S(1)} %dynamic_slice.31), channel_id=1, source_target_pairs={{0,8},{2,10},{4,12},{6,14},{8,0},{10,2},{12,4},{14,6},{1,9},{3,11}... | collective-permute-start | bytes 122888 | tf_op jit(solution)/shard_map/ppermute | solution.py:132
  55.6 5.0 %collective-permute-start.9 = (f32[10240]{0:T(1024)S(1)}, f32[10240]{0:T(1024)S(1)}, u32[]{:S(2)}, u32[]{:S(2)}) collective-permute-start(f32[10240]{0:T(1024)S(1)} %dynamic-slice_add_fusion.1), channel_id=1, source_target_pairs={{0,8},{2,10},{4,12},{6,14},{8,0},{10,2},{12,4},{14,6},{1,9},{3,11}... | collective-permute-start | bytes 122888 | tf_op jit(solution)/shard_map/ppermute | solution.py:139
  60.6 5.4 %collective-permute-start.10 = (f32[20480]{0:T(1024)S(1)}, f32[20480]{0:T(1024)S(1)}, u32[]{:S(2)}, u32[]{:S(2)}) collective-permute-start(f32[20480]{0:T(1024)S(1)} %pad_maximum_fusion.1), channel_id=1, source_target_pairs={{0,6},{2,4},{4,2},{6,0},{8,14},{10,12},{12,10},{14,8},{1,7},{3,5},... | collective-permute-start | bytes 245768 | tf_op jit(solution)/shard_map/ppermute | solution.py:139
  62.9 4.4 %collective-permute-start.11 = (f32[20480]{0:T(1024)S(1)}, f32[20480]{0:T(1024)S(1)}, u32[]{:S(2)}, u32[]{:S(2)}) collective-permute-start(f32[20480]{0:T(1024)S(1)} %pad_maximum_fusion.1), channel_id=1, source_target_pairs={{0,4},{2,6},{4,0},{6,2},{8,12},{10,14},{12,8},{14,10},{1,5},{3,7},... | collective-permute-start | bytes 245768 | tf_op jit(solution)/shard_map/ppermute | solution.py:139
  63.8 4.4 %collective-permute-start.12 = (f32[20480]{0:T(1024)S(1)}, f32[20480]{0:T(1024)S(1)}, u32[]{:S(2)}, u32[]{:S(2)}) collective-permute-start(f32[20480]{0:T(1024)S(1)} %pad_maximum_fusion.1), channel_id=1, source_target_pairs={{0,2},{2,0},{4,6},{6,4},{8,10},{10,8},{12,14},{14,12},{1,3},{3,1},... | collective-permute-start | bytes 245768 | tf_op jit(solution)/shard_map/ppermute | solution.py:139
  68.3 1.7 %collective-permute-start.13 = (f32[81920]{0:T(1024)S(1)}, f32[81920]{0:T(1024)S(1)}, u32[]{:S(2)}, u32[]{:S(2)}) collective-permute-start(f32[81920]{0:T(1024)S(1)} %pad_maximum_fusion), channel_id=1, source_target_pairs={{0,1},{1,0},{2,3},{3,2},{4,5},{5,4},{6,7},{7,6},{8,9},{9,8},{10,11... | collective-permute-start | bytes 983048 | tf_op jit(solution)/shard_map/ppermute | solution.py:139

commit v3 on v2

--- a/solution.py
+++ b/solution.py
@@ -1,3 +1,5 @@
+import functools
+
 import jax
 import jax.numpy as jnp
 from jax import lax
@@ -8,11 +10,18 @@
 HI = lax.Precision.HIGHEST
 
 
-def factor_kernel(g_ref, f_ref, x_ref, u_ref, w_ref, inv_ref, xs_ref):
-    n = g_ref.shape[0]
+def factor_kernel(total, g_ref, f_ref, x_ref, u_ref, w_ref, inv_ref, xs_ref):
+    n = f_ref.shape[1]
     b = inv_ref.shape[1]
     nb = n // b
-    w_ref[...] = g_ref[...]
+    t = 0
+    for first in range(nb):
+        for second in range(first, nb):
+            tile = g_ref[t] / total
+            w_ref[first * b:(first + 1) * b, second * b:(second + 1) * b] = tile
+            if second > first:
+                w_ref[second * b:(second + 1) * b, first * b:(first + 1) * b] = tile.T
+            t += 1
     u_ref[...] = jnp.zeros(u_ref.shape, jnp.float32)
     lane = lax.broadcasted_iota(jnp.int32, (1, b), 1)
     rows = lax.broadcasted_iota(jnp.int32, (b, 1), 0)
@@ -50,12 +59,12 @@
     x_ref[...] = xs_ref[...].astype(x_ref.dtype)
 
 
-def factor_solve(gram, forecast, block=128):
-    n = gram.shape[0]
+def factor_solve(tiles, forecast, total, block=128):
+    n = forecast.shape[1]
     m = forecast.shape[0]
     vmem = pl.BlockSpec(memory_space=pltpu.VMEM)
     return pl.pallas_call(
-        factor_kernel,
+        functools.partial(factor_kernel, float(total)),
         out_shape=(jax.ShapeDtypeStruct((m, n), jnp.bfloat16), jax.ShapeDtypeStruct((n, n), jnp.float32)),
         in_specs=[vmem, vmem],
         out_specs=(vmem, vmem),
@@ -64,7 +73,7 @@
             pltpu.VMEM((n // block, block, block), jnp.float32),
             pltpu.VMEM((m, n), jnp.float32),
         ],
-    )(gram, forecast)
+    )(tiles, forecast)
 
 
 def shifted(block, axis, distance):
@@ -147,37 +156,50 @@
     return flat
 
 
-def apply_kernel(rows_ref, cols_ref, jac_ref, root_ref, base_ref, *refs):
+def apply_kernel(own, rows_ref, cols_ref, jac_ref, root_ref, *refs):
     out_refs = refs[:-1]
     acc_ref = refs[-1]
     nblk = root_ref.shape[0]
-    rim = out_refs[0].shape[0]
+    first = 0 if own else nblk
     acc_ref[...] = jnp.zeros(acc_ref.shape, jnp.float32)
 
     def step(n, carry):
         slot = rows_ref[n]
-        acc_ref[slot] = acc_ref[slot] + jnp.dot(
-            jac_ref[n], root_ref[cols_ref[n]], preferred_element_type=jnp.float32)
+        inside = slot < nblk if own else slot >= nblk
+
+        @pl.when(inside)
+        def _():
+            acc_ref[slot - first] = acc_ref[slot - first] + jnp.dot(
+                jac_ref[n], root_ref[cols_ref[n]], preferred_element_type=jnp.float32)
+
         return carry
 
     lax.fori_loop(0, jac_ref.shape[0], step, 0, unroll=True)
-    base_ref[...] = root_ref[...].astype(jnp.float32) + acc_ref[:nblk]
-    for k, out_ref in enumerate(out_refs):
-        out_ref[...] = acc_ref[nblk + k * rim:nblk + (k + 1) * rim]
-
-
-def apply_blocks(jac_rows, jac_cols, jac_blocks, root_blocks, slot_count):
+    if own:
+        out_refs[0][...] = root_ref[...].astype(jnp.float32) + acc_ref[...]
+    else:
+        rim = out_refs[0].shape[0]
+        for k, out_ref in enumerate(out_refs):
+            out_ref[...] = acc_ref[k * rim:(k + 1) * rim]
+
+
+def apply_blocks(jac_rows, jac_cols, jac_blocks, root_blocks, slot_count, own):
     nblk, block, width = root_blocks.shape
     rim = (slot_count - nblk) // 4
     smem = pl.BlockSpec(memory_space=pltpu.SMEM)
     vmem = pl.BlockSpec(memory_space=pltpu.VMEM)
+    if own:
+        shapes = (jax.ShapeDtypeStruct((nblk, block, width), jnp.float32),)
+        held = nblk
+    else:
+        shapes = tuple(jax.ShapeDtypeStruct((rim, block, width), jnp.float32) for _ in range(4))
+        held = 4 * rim
     return pl.pallas_call(
-        apply_kernel,
-        out_shape=(jax.ShapeDtypeStruct((nblk, block, width), jnp.float32),)
-        + tuple(jax.ShapeDtypeStruct((rim, block, width), jnp.float32) for _ in range(4)),
+        functools.partial(apply_kernel, own),
+        out_shape=shapes,
         in_specs=[smem, smem, vmem, vmem],
-        out_specs=(vmem,) * 5,
-        scratch_shapes=[pltpu.VMEM((slot_count, block, width), jnp.float32)],
+        out_specs=(vmem,) * len(shapes),
+        scratch_shapes=[pltpu.VMEM((held, block, width), jnp.float32)],
     )(jac_rows, jac_cols, jac_blocks, root_blocks)
 
 
@@ -228,35 +250,19 @@
     rim = landing.shape[0] // 4
     slot_count = nblk + 4 * rim
     blocks = covariance_root.reshape(nblk, block, mode_columns)
-    base, to_prev_x, to_next_x, to_prev_y, to_next_y = apply_blocks(
-        jac_rows, jac_cols, jac_blocks, blocks, slot_count)
+    to_prev_x, to_next_x, to_prev_y, to_next_y = apply_blocks(
+        jac_rows, jac_cols, jac_blocks, blocks, slot_count, False)
     from_next_x = shifted(to_prev_x, "tx", -1)
     from_prev_x = shifted(to_next_x, "tx", 1)
     from_next_y = shifted(to_prev_y, "ty", -1)
     from_prev_y = shifted(to_next_y, "ty", 1)
+    (base,) = apply_blocks(jac_rows, jac_cols, jac_blocks, blocks, slot_count, True)
     predicted_root, local_tiles = land_and_gram(
         landing, base, [from_next_x, from_prev_x, from_next_y, from_prev_y])
     total_rows = state_rows * lax.axis_size("tx") * lax.axis_size("ty")
     tiles = mode_columns // block
     upper_sum = grouped_sum(local_tiles.reshape(-1)).reshape(local_tiles.shape)
-    position = {}
-    counter = 0
-    for first in range(tiles):
-        for second in range(first, tiles):
-            position[first, second] = counter
-            counter = counter + 1
-    band_rows = []
-    for first in range(tiles):
-        pieces = []
-        for second in range(tiles):
-            if first <= second:
-                pieces.append(upper_sum[position[first, second]])
-            else:
-                pieces.append(upper_sum[position[second, first]].T)
-        band_rows.append(jnp.concatenate(pieces, axis=1))
-    summed = jnp.concatenate(band_rows, axis=0)
-    inner_products_table = summed / total_rows
-    rescaled_orthogonal_root, r_factor = factor_solve(inner_products_table, predicted_root, block)
+    rescaled_orthogonal_root, r_factor = factor_solve(upper_sum, predicted_root, total_rows, block)
     return (rescaled_orthogonal_root, r_factor)
 
 

time: 120 us -> 121 us (level)
  Pallas kernels: 57.1 us -> 63.3 us
  waiting for transfers between devices: 33.4 us -> 27.4 us
  starting transfers between devices: 24.2 us -> 25.6 us
    pallas_call x2 -> x3, Pallas kernels: 52.2 us -> 58.4 us  [the longest x1 47.9 us: factor_solve(): pl.pallas_call(functools.partial(factor_kernel, float(total)), out_shape=...]
    ppermute x4, waiting for transfers between devices: 17.2 us -> 12.3 us  [shifted(): return lax.ppermute(block, axis, route)]
  transfers between devices with their start and end apart: 14 -> 14, of which waited for: 12 -> 12; matrix products, arithmetic and copies ran while one was open for 0% -> 0% of each run, Pallas kernels for 0% -> 3%
where the time goes in v3:
time: 121 us
  Pallas kernels  63.3 us (52%)
  waiting for transfers between devices  27.4 us (23%)
  starting transfers between devices  25.6 us (21%)
  local copies, waits for them, and re-layouts  2.88 us (2%)
    pallas_call x1, Pallas kernels, factor_solve(): pl.pallas_call(functools.partial(factor_kernel, float(total)), out_shape=...  47.9 us
    ppermute x4, waiting for transfers between devices, shifted(): return lax.ppermute(block, axis, route)  12.3 us
    ppermute x4, starting transfers between devices, shifted(): return lax.ppermute(block, axis, route)  11.3 us
    pallas_call x2, Pallas kernels, apply_blocks(): pl.pallas_call(functools.partial(apply_kernel, own), out_shape=shapes, in...  10.5 us
    ppermute x5, starting transfers between devices, grouped_sum(): kept = kept + lax.ppermute(sent, axis, route)  7.75 us
    ppermute x5, waiting for transfers between devices, grouped_sum(): got.append(lax.ppermute(flat, axis, route))  7.68 us
    ppermute x5, waiting for transfers between devices, grouped_sum(): kept = kept + lax.ppermute(sent, axis, route)  7.5 us
    ppermute x5, starting transfers between devices, grouped_sum(): got.append(lax.ppermute(flat, axis, route))  6.6 us
  transfers between devices with their start and end apart: 14, of which 12 were waited for; matrix products, arithmetic and copies ran while one was open for 0% of the time, Pallas kernels for 3%

profile of v3, /device:TPU:0, one launch (start us, length us, event | category | flops | bytes accessed | tf_op | source)
XLA Modules:
  0.0 121.2 jit_solution(3520980038268510092)
XLA Ops:
  0.6 6.3 %shard_map.69 = (f32[2,128,512]{2,1,0:T(8,128)}, f32[2,128,512]{2,1,0:T(8,128)}, f32[2,128,512]{2,1,0:T(8,128)}, f32[2,128,512]{2,1,0:T(8,128)}) custom-call(s32[28]{0:T(128)} %rows_ref.3, s32[28]{0:T(128)} %cols_ref.3, bf16[28,128,128]{2,1,0:T(8,128)(2,1)} %jac_ref.3, bf16[4,128,512]{2,1,0:T(8,128)(2,1)} %bitcast.4), custom_call_target="tpu_custom_call" | custom-call | tf_op jit(solution)/shard_map/pallas_call | solution.py:197
  6.9 1.3 %collective-permute-start = (f32[2,128,512]{2,1,0:T(8,128)}, f32[2,128,512]{2,1,0:T(8,128)S(1)}, u32[]{:S(2)}, u32[]{:S(2)}) collective-permute-start(f32[2,128,512]{2,1,0:T(8,128)} %get-tuple-element.8), channel_id=1, source_target_pairs={{2,0},{4,2},{6,4},{8,6},{10,8},{12,10},{14,12},{3,1},{5,3},{7,5},{... | collective-permute-start | bytes 1572872 | tf_op jit(solution)/shard_map/ppermute | solution.py:82
  8.2 5.6 %collective-permute-start.1 = (f32[2,128,512]{2,1,0:T(8,128)}, f32[2,128,512]{2,1,0:T(8,128)S(1)}, u32[]{:S(2)}, u32[]{:S(2)}) collective-permute-start(f32[2,128,512]{2,1,0:T(8,128)} %get-tuple-element.9), channel_id=1, source_target_pairs={{0,2},{2,4},{4,6},{6,8},{8,10},{10,12},{12,14},{1,3},{3,5},{5,7},{... | collective-permute-start | bytes 1572872 | tf_op jit(solution)/shard_map/ppermute | solution.py:82
  13.9 1.3 %collective-permute-start.2 = (f32[2,128,512]{2,1,0:T(8,128)}, f32[2,128,512]{2,1,0:T(8,128)S(1)}, u32[]{:S(2)}, u32[]{:S(2)}) collective-permute-start(f32[2,128,512]{2,1,0:T(8,128)} %get-tuple-element.10), channel_id=1, source_target_pairs={{1,0},{3,2},{5,4},{7,6},{9,8},{11,10},{13,12},{15,14},{17,16},{19,... | collective-permute-start | bytes 1572872 | tf_op jit(solution)/shard_map/ppermute | solution.py:82
  15.2 3.1 %collective-permute-start.3 = (f32[2,128,512]{2,1,0:T(8,128)}, f32[2,128,512]{2,1,0:T(8,128)S(1)}, u32[]{:S(2)}, u32[]{:S(2)}) collective-permute-start(f32[2,128,512]{2,1,0:T(8,128)} %get-tuple-element.11), channel_id=1, source_target_pairs={{0,1},{2,3},{4,5},{6,7},{8,9},{10,11},{12,13},{14,15},{16,17},{18,... | collective-permute-start | bytes 1572872 | tf_op jit(solution)/shard_map/ppermute | solution.py:82
  18.3 4.2 %shard_map.68.base_ref = f32[4,128,512]{2,1,0:T(8,128)} custom-call(s32[28]{0:T(128)} %rows_ref.3, s32[28]{0:T(128)} %cols_ref.3, bf16[28,128,128]{2,1,0:T(8,128)(2,1)} %jac_ref.3, bf16[4,128,512]{2,1,0:T(8,128)(2,1)} %bitcast.5), custom_call_target="tpu_custom_call" | custom-call | tf_op jit(solution)/shard_map/pallas_call | solution.py:197
  22.5 1.0 collective-permute-done.refs_0_
  23.5 0.0 copy-start.1
  23.5 11.2 %collective-permute-done.1.refs_1_ = f32[2,128,512]{2,1,0:T(8,128)S(1)} collective-permute-done((f32[2,128,512]{2,1,0:T(8,128)}, f32[2,128,512]{2,1,0:T(8,128)S(1)}, u32[]{:S(2)}, u32[]{:S(2)}) %collective-permute-start.1) | collective-permute-done | bytes 524320 | tf_op jit(solution)/shard_map/ppermute | solution.py:82
  34.7 0.0 copy-start.2
  34.7 0.0 collective-permute-done.2.refs_2_
  34.7 0.0 copy-start.3
  34.7 0.0 collective-permute-done.3.refs_3_
  34.7 0.0 copy-done.1
  34.7 0.8 copy-done.2
  35.5 0.2 copy-done.3
  35.7 0.0 copy-start.4
  35.7 0.8 copy-done.4
  36.5 4.9 %shard_map.70 = (f32[512,512]{1,0:T(8,128)}, f32[10,128,128]{2,1,0:T(8,128)}) custom-call(s32[8]{0:T(128)} %landing_ref.1, f32[4,128,512]{2,1,0:T(8,128)} %shard_map.68.base_ref, f32[2,128,512]{2,1,0:T(8,128)} %copy-done.1, f32[2,128,512]{2,1,0:T(8,128)} %copy-done.2, f32[2,128,512]{2,1,0:T(8,128)} %copy-done.3, f32[2,128,512]{2,1,0:T(8,128)} %copy-done.4), custom_call_target="tpu_custom_call" | custom-call | tf_op jit(solution)/shard_map/pallas_call | solution.py:235
  41.4 0.0 copy-start
  41.4 1.1 dynamic_slice.25
  42.5 0.1 collective-permute-start.4
  42.6 1.6 %collective-permute-done.4 = f32[81920]{0:T(1024)S(1)} collective-permute-done((f32[81920]{0:T(1024)S(1)}, f32[81920]{0:T(1024)S(1)}, u32[]{:S(2)}, u32[]{:S(2)}) %collective-permute-start.4) | collective-permute-done | bytes 327712 | tf_op jit(solution)/shard_map/ppermute | solution.py:141
  44.2 0.0 copy-done
  44.2 4.0 %collective-permute-start.7 = (f32[20480]{0:T(1024)S(1)}, f32[20480]{0:T(1024)S(1)}, u32[]{:S(2)}, u32[]{:S(2)}) collective-permute-start(f32[20480]{0:T(1024)S(1)} %get-tuple-element.20), channel_id=1, source_target_pairs={{0,6},{2,4},{4,2},{6,0},{8,14},{10,12},{12,10},{14,8},{1,7},{3,5},... | collective-permute-start | bytes 245768 | tf_op jit(solution)/shard_map/ppermute | solution.py:141
  48.2 0.0 collective-permute-start.6
  48.2 0.6 collective-permute-start.5
  48.8 2.6 %collective-permute-done.7 = f32[20480]{0:T(1024)S(1)} collective-permute-done((f32[20480]{0:T(1024)S(1)}, f32[20480]{0:T(1024)S(1)}, u32[]{:S(2)}, u32[]{:S(2)}) %collective-permute-start.7) | collective-permute-done | bytes 81952 | tf_op jit(solution)/shard_map/ppermute | solution.py:141
  51.4 1.2 collective-permute-done.6
  52.6 0.2 collective-permute-done.5
  52.8 3.1 %collective-permute-start.8 = (f32[10240]{0:T(1024)S(1)}, f32[10240]{0:T(1024)S(1)}, u32[]{:S(2)}, u32[]{:S(2)}) collective-permute-start(f32[10240]{0:T(1024)S(1)} %dynamic_slice.31), channel_id=1, source_target_pairs={{0,8},{2,10},{4,12},{6,14},{8,0},{10,2},{12,4},{14,6},{1,9},{3,11}... | collective-permute-start | bytes 122888 | tf_op jit(solution)/shard_map/ppermute | solution.py:141
  55.9 2.0 %collective-permute-done.8 = f32[10240]{0:T(1024)S(1)} collective-permute-done((f32[10240]{0:T(1024)S(1)}, f32[10240]{0:T(1024)S(1)}, u32[]{:S(2)}, u32[]{:S(2)}) %collective-permute-start.8) | collective-permute-done | bytes 40992 | tf_op jit(solution)/shard_map/ppermute | solution.py:141
  57.9 3.0 %collective-permute-start.9 = (f32[10240]{0:T(1024)S(1)}, f32[10240]{0:T(1024)S(1)}, u32[]{:S(2)}, u32[]{:S(2)}) collective-permute-start(f32[10240]{0:T(1024)S(1)} %dynamic-slice_add_fusion.1), channel_id=1, source_target_pairs={{0,8},{2,10},{4,12},{6,14},{8,0},{10,2},{12,4},{14,6},{1,9},{3,11}... | collective-permute-start | bytes 122888 | tf_op jit(solution)/shard_map/ppermute | solution.py:148
  60.9 2.0 %collective-permute-done.9 = f32[10240]{0:T(1024)S(1)} collective-permute-done((f32[10240]{0:T(1024)S(1)}, f32[10240]{0:T(1024)S(1)}, u32[]{:S(2)}, u32[]{:S(2)}) %collective-permute-start.9) | collective-permute-done | bytes 40992 | tf_op jit(solution)/shard_map/ppermute | solution.py:148
  62.9 2.5 %collective-permute-start.10 = (f32[20480]{0:T(1024)S(1)}, f32[20480]{0:T(1024)S(1)}, u32[]{:S(2)}, u32[]{:S(2)}) collective-permute-start(f32[20480]{0:T(1024)S(1)} %pad_maximum_fusion.2), channel_id=1, source_target_pairs={{0,6},{2,4},{4,2},{6,0},{8,14},{10,12},{12,10},{14,8},{1,7},{3,5},... | collective-permute-start | bytes 245768 | tf_op jit(solution)/shard_map/ppermute | solution.py:148
  65.4 0.7 collective-permute-start.11
  66.1 0.4 collective-permute-start.12
  66.4 1.9 %collective-permute-done.10 = f32[20480]{0:T(1024)S(1)} collective-permute-done((f32[20480]{0:T(1024)S(1)}, f32[20480]{0:T(1024)S(1)}, u32[]{:S(2)}, u32[]{:S(2)}) %collective-permute-start.10) | collective-permute-done | bytes 81952 | tf_op jit(solution)/shard_map/ppermute | solution.py:148
  68.3 1.6 %collective-permute-done.11 = f32[20480]{0:T(1024)S(1)} collective-permute-done((f32[20480]{0:T(1024)S(1)}, f32[20480]{0:T(1024)S(1)}, u32[]{:S(2)}, u32[]{:S(2)}) %collective-permute-start.11) | collective-permute-done | bytes 81952 | tf_op jit(solution)/shard_map/ppermute | solution.py:148
  69.9 0.7 collective-permute-done.12
  70.6 0.1 collective-permute-start.13
  70.7 1.6 %collective-permute-done.13 = f32[81920]{0:T(1024)S(1)} collective-permute-done((f32[81920]{0:T(1024)S(1)}, f32[81920]{0:T(1024)S(1)}, u32[]{:S(2)}, u32[]{:S(2)}) %collective-permute-start.13) | collective-permute-done | bytes 327712 | tf_op jit(solution)/shard_map/ppermute | solution.py:148
  72.4 0.9 pad_maximum_fusion.g_ref
  73.3 47.9 %shard_map.71 = (bf16[512,512]{1,0:T(8,128)(2,1)}, f32[512,512]{1,0:T(8,128)}) custom-call(f32[10,128,128]{2,1,0:T(8,128)} %pad_maximum_fusion.g_ref, f32[512,512]{1,0:T(8,128)} %get-tuple-element.13.f_ref), custom_call_target="tpu_custom_call" | custom-call | tf_op jit(solution)/shard_map/pallas_call | solution.py:66
  (11 shorter events, 0.2 us)
Async XLA Ops:
  6.9 16.5 %collective-permute-start = (f32[2,128,512]{2,1,0:T(8,128)}, f32[2,128,512]{2,1,0:T(8,128)S(1)}, u32[]{:S(2)}, u32[]{:S(2)}) collective-permute-start(f32[2,128,512]{2,1,0:T(8,128)} %get-tuple-element.8), channel_id=1, source_target_pairs={{2,0},{4,2},{6,4},{8,6},{10,8},{12,10},{14,12},{3,1},{5,3},{7,5},{... | collective-permute-start | bytes 1572872 | tf_op jit(solution)/shard_map/ppermute | solution.py:82
  8.2 26.5 %collective-permute-start.1 = (f32[2,128,512]{2,1,0:T(8,128)}, f32[2,128,512]{2,1,0:T(8,128)S(1)}, u32[]{:S(2)}, u32[]{:S(2)}) collective-permute-start(f32[2,128,512]{2,1,0:T(8,128)} %get-tuple-element.9), channel_id=1, source_target_pairs={{0,2},{2,4},{4,6},{6,8},{8,10},{10,12},{12,14},{1,3},{3,5},{5,7},{... | collective-permute-start | bytes 1572872 | tf_op jit(solution)/shard_map/ppermute | solution.py:82
  13.9 20.9 %collective-permute-start.2 = (f32[2,128,512]{2,1,0:T(8,128)}, f32[2,128,512]{2,1,0:T(8,128)S(1)}, u32[]{:S(2)}, u32[]{:S(2)}) collective-permute-start(f32[2,128,512]{2,1,0:T(8,128)} %get-tuple-element.10), channel_id=1, source_target_pairs={{1,0},{3,2},{5,4},{7,6},{9,8},{11,10},{13,12},{15,14},{17,16},{19,... | collective-permute-start | bytes 1572872 | tf_op jit(solution)/shard_map/ppermute | solution.py:82
  15.2 19.6 %collective-permute-start.3 = (f32[2,128,512]{2,1,0:T(8,128)}, f32[2,128,512]{2,1,0:T(8,128)S(1)}, u32[]{:S(2)}, u32[]{:S(2)}) collective-permute-start(f32[2,128,512]{2,1,0:T(8,128)} %get-tuple-element.11), channel_id=1, source_target_pairs={{0,1},{2,3},{4,5},{6,7},{8,9},{10,11},{12,13},{14,15},{16,17},{18,... | collective-permute-start | bytes 1572872 | tf_op jit(solution)/shard_map/ppermute | solution.py:82
  23.5 11.3 %copy-start.1 = (f32[2,128,512]{2,1,0:T(8,128)}, f32[2,128,512]{2,1,0:T(8,128)S(1)}, u32[]{:S(2)}) copy-start(f32[2,128,512]{2,1,0:T(8,128)S(1)} %collective-permute-done.refs_0_) | copy-start | bytes 1572868
  34.7 0.8 copy-start.2
  34.7 1.0 copy-start.3
  35.7 0.8 copy-start.4
  41.4 2.8 %copy-start = (f32[10,128,128]{2,1,0:T(8,128)S(1)}, f32[10,128,128]{2,1,0:T(8,128)}, u32[]{:S(2)}) copy-start(f32[10,128,128]{2,1,0:T(8,128)} %get-tuple-element.12) | copy-start | bytes 1966084
  42.5 1.7 %collective-permute-start.4 = (f32[81920]{0:T(1024)S(1)}, f32[81920]{0:T(1024)S(1)}, u32[]{:S(2)}, u32[]{:S(2)}) collective-permute-start(f32[81920]{0:T(1024)S(1)} %dynamic_slice.25), channel_id=1, source_target_pairs={{0,1},{1,0},{2,3},{3,2},{4,5},{5,4},{6,7},{7,6},{8,9},{9,8},{10,11... | collective-permute-start | bytes 983048 | tf_op jit(solution)/shard_map/ppermute | solution.py:141
  44.2 7.2 %collective-permute-start.7 = (f32[20480]{0:T(1024)S(1)}, f32[20480]{0:T(1024)S(1)}, u32[]{:S(2)}, u32[]{:S(2)}) collective-permute-start(f32[20480]{0:T(1024)S(1)} %get-tuple-element.20), channel_id=1, source_target_pairs={{0,6},{2,4},{4,2},{6,0},{8,14},{10,12},{12,10},{14,8},{1,7},{3,5},... | collective-permute-start | bytes 245768 | tf_op jit(solution)/shard_map/ppermute | solution.py:141
  48.2 4.4 %collective-permute-start.6 = (f32[20480]{0:T(1024)S(1)}, f32[20480]{0:T(1024)S(1)}, u32[]{:S(2)}, u32[]{:S(2)}) collective-permute-start(f32[20480]{0:T(1024)S(1)} %get-tuple-element.21), channel_id=1, source_target_pairs={{0,4},{2,6},{4,0},{6,2},{8,12},{10,14},{12,8},{14,10},{1,5},{3,7},... | collective-permute-start | bytes 245768 | tf_op jit(solution)/shard_map/ppermute | solution.py:141
  48.2 4.6 %collective-permute-start.5 = (f32[20480]{0:T(1024)S(1)}, f32[20480]{0:T(1024)S(1)}, u32[]{:S(2)}, u32[]{:S(2)}) collective-permute-start(f32[20480]{0:T(1024)S(1)} %get-tuple-element.19), channel_id=1, source_target_pairs={{0,2},{2,0},{4,6},{6,4},{8,10},{10,8},{12,14},{14,12},{1,3},{3,1},... | collective-permute-start | bytes 245768 | tf_op jit(solution)/shard_map/ppermute | solution.py:141
  52.8 5.1 %collective-permute-start.8 = (f32[10240]{0:T(1024)S(1)}, f32[10240]{0:T(1024)S(1)}, u32[]{:S(2)}, u32[]{:S(2)}) collective-permute-start(f32[10240]{0:T(1024)S(1)} %dynamic_slice.31), channel_id=1, source_target_pairs={{0,8},{2,10},{4,12},{6,14},{8,0},{10,2},{12,4},{14,6},{1,9},{3,11}... | collective-permute-start | bytes 122888 | tf_op jit(solution)/shard_map/ppermute | solution.py:141
  57.9 5.0 %collective-permute-start.9 = (f32[10240]{0:T(1024)S(1)}, f32[10240]{0:T(1024)S(1)}, u32[]{:S(2)}, u32[]{:S(2)}) collective-permute-start(f32[10240]{0:T(1024)S(1)} %dynamic-slice_add_fusion.1), channel_id=1, source_target_pairs={{0,8},{2,10},{4,12},{6,14},{8,0},{10,2},{12,4},{14,6},{1,9},{3,11}... | collective-permute-start | bytes 122888 | tf_op jit(solution)/shard_map/ppermute | solution.py:148
  62.9 5.4 %collective-permute-start.10 = (f32[20480]{0:T(1024)S(1)}, f32[20480]{0:T(1024)S(1)}, u32[]{:S(2)}, u32[]{:S(2)}) collective-permute-start(f32[20480]{0:T(1024)S(1)} %pad_maximum_fusion.2), channel_id=1, source_target_pairs={{0,6},{2,4},{4,2},{6,0},{8,14},{10,12},{12,10},{14,8},{1,7},{3,5},... | collective-permute-start | bytes 245768 | tf_op jit(solution)/shard_map/ppermute | solution.py:148
  65.4 4.4 %collective-permute-start.11 = (f32[20480]{0:T(1024)S(1)}, f32[20480]{0:T(1024)S(1)}, u32[]{:S(2)}, u32[]{:S(2)}) collective-permute-start(f32[20480]{0:T(1024)S(1)} %pad_maximum_fusion.2), channel_id=1, source_target_pairs={{0,4},{2,6},{4,0},{6,2},{8,12},{10,14},{12,8},{14,10},{1,5},{3,7},... | collective-permute-start | bytes 245768 | tf_op jit(solution)/shard_map/ppermute | solution.py:148
  66.1 4.4 %collective-permute-start.12 = (f32[20480]{0:T(1024)S(1)}, f32[20480]{0:T(1024)S(1)}, u32[]{:S(2)}, u32[]{:S(2)}) collective-permute-start(f32[20480]{0:T(1024)S(1)} %pad_maximum_fusion.2), channel_id=1, source_target_pairs={{0,2},{2,0},{4,6},{6,4},{8,10},{10,8},{12,14},{14,12},{1,3},{3,1},... | collective-permute-start | bytes 245768 | tf_op jit(solution)/shard_map/ppermute | solution.py:148
  70.6 1.7 %collective-permute-start.13 = (f32[81920]{0:T(1024)S(1)}, f32[81920]{0:T(1024)S(1)}, u32[]{:S(2)}, u32[]{:S(2)}) collective-permute-start(f32[81920]{0:T(1024)S(1)} %pad_maximum_fusion.1), channel_id=1, source_target_pairs={{0,1},{1,0},{2,3},{3,2},{4,5},{5,4},{6,7},{7,6},{8,9},{9,8},{10,11... | collective-permute-start | bytes 983048 | tf_op jit(solution)/shard_map/ppermute | solution.py:148

commit v4 on v2

--- a/solution.py
+++ b/solution.py
@@ -1,3 +1,5 @@
+import functools
+
 import jax
 import jax.numpy as jnp
 from jax import lax
@@ -8,11 +10,18 @@
 HI = lax.Precision.HIGHEST
 
 
-def factor_kernel(g_ref, f_ref, x_ref, u_ref, w_ref, inv_ref, xs_ref):
-    n = g_ref.shape[0]
+def factor_kernel(total, g_ref, f_ref, x_ref, u_ref, w_ref, inv_ref, xs_ref):
+    n = f_ref.shape[1]
     b = inv_ref.shape[1]
     nb = n // b
-    w_ref[...] = g_ref[...]
+    t = 0
+    for first in range(nb):
+        for second in range(first, nb):
+            tile = g_ref[t] / total
+            w_ref[first * b:(first + 1) * b, second * b:(second + 1) * b] = tile
+            if second > first:
+                w_ref[second * b:(second + 1) * b, first * b:(first + 1) * b] = tile.T
+            t += 1
     u_ref[...] = jnp.zeros(u_ref.shape, jnp.float32)
     lane = lax.broadcasted_iota(jnp.int32, (1, b), 1)
     rows = lax.broadcasted_iota(jnp.int32, (b, 1), 0)
@@ -50,12 +59,12 @@
     x_ref[...] = xs_ref[...].astype(x_ref.dtype)
 
 
-def factor_solve(gram, forecast, block=128):
-    n = gram.shape[0]
+def factor_solve(tiles, forecast, total, block=128):
+    n = forecast.shape[1]
     m = forecast.shape[0]
     vmem = pl.BlockSpec(memory_space=pltpu.VMEM)
     return pl.pallas_call(
-        factor_kernel,
+        functools.partial(factor_kernel, float(total)),
         out_shape=(jax.ShapeDtypeStruct((m, n), jnp.bfloat16), jax.ShapeDtypeStruct((n, n), jnp.float32)),
         in_specs=[vmem, vmem],
         out_specs=(vmem, vmem),
@@ -64,7 +73,7 @@
             pltpu.VMEM((n // block, block, block), jnp.float32),
             pltpu.VMEM((m, n), jnp.float32),
         ],
-    )(gram, forecast)
+    )(tiles, forecast)
 
 
 def shifted(block, axis, distance):
@@ -239,24 +248,7 @@
     total_rows = state_rows * lax.axis_size("tx") * lax.axis_size("ty")
     tiles = mode_columns // block
     upper_sum = grouped_sum(local_tiles.reshape(-1)).reshape(local_tiles.shape)
-    position = {}
-    counter = 0
-    for first in range(tiles):
-        for second in range(first, tiles):
-            position[first, second] = counter
-            counter = counter + 1
-    band_rows = []
-    for first in range(tiles):
-        pieces = []
-        for second in range(tiles):
-            if first <= second:
-                pieces.append(upper_sum[position[first, second]])
-            else:
-                pieces.append(upper_sum[position[second, first]].T)
-        band_rows.append(jnp.concatenate(pieces, axis=1))
-    summed = jnp.concatenate(band_rows, axis=0)
-    inner_products_table = summed / total_rows
-    rescaled_orthogonal_root, r_factor = factor_solve(inner_products_table, predicted_root, block)
+    rescaled_orthogonal_root, r_factor = factor_solve(upper_sum, predicted_root, total_rows, block)
     return (rescaled_orthogonal_root, r_factor)
 
 

time: 120 us -> 119 us (level)
  no operation moved by 1% of the time
where the time goes in v4:
time: 119 us
  Pallas kernels  57 us (48%)
  waiting for transfers between devices  33.3 us (28%)
  starting transfers between devices  24.3 us (20%)
  local copies, waits for them, and re-layouts  2.23 us (2%)
    pallas_call x1, Pallas kernels, factor_solve(): pl.pallas_call(functools.partial(factor_kernel, float(total)), out_shape=...  47.8 us
    ppermute x4, waiting for transfers between devices, shifted(): return lax.ppermute(block, axis, route)  17.2 us
    ppermute x4, starting transfers between devices, shifted(): return lax.ppermute(block, axis, route)  11.2 us
    ppermute x5, waiting for transfers between devices, grouped_sum(): kept = kept + lax.ppermute(sent, axis, route)  8.13 us
    ppermute x5, waiting for transfers between devices, grouped_sum(): got.append(lax.ppermute(flat, axis, route))  7.98 us
    ppermute x5, starting transfers between devices, grouped_sum(): kept = kept + lax.ppermute(sent, axis, route)  6.82 us
    ppermute x5, starting transfers between devices, grouped_sum(): got.append(lax.ppermute(flat, axis, route))  6.26 us
    pallas_call x1, Pallas kernels, land_and_gram(): pl.pallas_call(land_kernel, out_shape=(jax.ShapeDtypeStruct((nblk * block...  4.9 us
  transfers between devices with their start and end apart: 14, of which 12 were waited for; matrix products, arithmetic and copies ran while one was open for 0% of the time, Pallas kernels for 0%

profile of v4, /device:TPU:0, one launch (start us, length us, event | category | flops | bytes accessed | tf_op | source)
XLA Modules:
  0.0 118.8 jit_solution(13499911263370227933)
XLA Ops:
  0.6 4.3 %shard_map.68 = (f32[4,128,512]{2,1,0:T(8,128)}, f32[2,128,512]{2,1,0:T(8,128)}, f32[2,128,512]{2,1,0:T(8,128)}, f32[2,128,512]{2,1,0:T(8,128)}, f32[2,128,512]{2,1,0:T(8,128)}) custom-call(s32[28]{0:T(128)} %rows_ref.1, s32[28]{0:T(128)} %cols_ref.1, bf16[28,128,128]{2,1,0:T(8,128)(2,1)} %jac_ref.1, bf16[4,128,512]{2,1,0:T(8,128)(2,1)} %bitcast.8), custom_call_target="tpu_custom_call" | custom-call | tf_op jit(solution)/shard_map/pallas_call | solution.py:183
  4.9 1.3 %collective-permute-start = (f32[2,128,512]{2,1,0:T(8,128)}, f32[2,128,512]{2,1,0:T(8,128)S(1)}, u32[]{:S(2)}, u32[]{:S(2)}) collective-permute-start(f32[2,128,512]{2,1,0:T(8,128)} %get-tuple-element.10), channel_id=1, source_target_pairs={{2,0},{4,2},{6,4},{8,6},{10,8},{12,10},{14,12},{3,1},{5,3},{7,5},{... | collective-permute-start | bytes 1572872 | tf_op jit(solution)/shard_map/ppermute | solution.py:82
  6.2 5.5 %collective-permute-start.1 = (f32[2,128,512]{2,1,0:T(8,128)}, f32[2,128,512]{2,1,0:T(8,128)S(1)}, u32[]{:S(2)}, u32[]{:S(2)}) collective-permute-start(f32[2,128,512]{2,1,0:T(8,128)} %get-tuple-element.11), channel_id=1, source_target_pairs={{0,2},{2,4},{4,6},{6,8},{8,10},{10,12},{12,14},{1,3},{3,5},{5,7},{... | collective-permute-start | bytes 1572872 | tf_op jit(solution)/shard_map/ppermute | solution.py:82
  11.7 1.3 %collective-permute-start.2 = (f32[2,128,512]{2,1,0:T(8,128)}, f32[2,128,512]{2,1,0:T(8,128)S(1)}, u32[]{:S(2)}, u32[]{:S(2)}) collective-permute-start(f32[2,128,512]{2,1,0:T(8,128)} %get-tuple-element.12), channel_id=1, source_target_pairs={{1,0},{3,2},{5,4},{7,6},{9,8},{11,10},{13,12},{15,14},{17,16},{19,... | collective-permute-start | bytes 1572872 | tf_op jit(solution)/shard_map/ppermute | solution.py:82
  13.0 3.1 %collective-permute-start.3 = (f32[2,128,512]{2,1,0:T(8,128)}, f32[2,128,512]{2,1,0:T(8,128)S(1)}, u32[]{:S(2)}, u32[]{:S(2)}) collective-permute-start(f32[2,128,512]{2,1,0:T(8,128)} %get-tuple-element.13), channel_id=1, source_target_pairs={{0,1},{2,3},{4,5},{6,7},{8,9},{10,11},{12,13},{14,15},{16,17},{18,... | collective-permute-start | bytes 1572872 | tf_op jit(solution)/shard_map/ppermute | solution.py:82
  16.2 5.7 %collective-permute-done.refs_0_ = f32[2,128,512]{2,1,0:T(8,128)S(1)} collective-permute-done((f32[2,128,512]{2,1,0:T(8,128)}, f32[2,128,512]{2,1,0:T(8,128)S(1)}, u32[]{:S(2)}, u32[]{:S(2)}) %collective-permute-start) | collective-permute-done | bytes 524320 | tf_op jit(solution)/shard_map/ppermute | solution.py:82
  21.9 0.0 copy-start.1
  21.9 11.5 %collective-permute-done.1.refs_1_ = f32[2,128,512]{2,1,0:T(8,128)S(1)} collective-permute-done((f32[2,128,512]{2,1,0:T(8,128)}, f32[2,128,512]{2,1,0:T(8,128)S(1)}, u32[]{:S(2)}, u32[]{:S(2)}) %collective-permute-start.1) | collective-permute-done | bytes 524320 | tf_op jit(solution)/shard_map/ppermute | solution.py:82
  33.4 0.0 copy-start.2
  33.4 0.0 collective-permute-done.2.refs_2_
  33.4 0.0 copy-start.3
  33.4 0.0 collective-permute-done.3.refs_3_
  33.4 0.0 copy-start.4
  33.4 0.0 copy-done.1
  33.4 0.8 copy-done.2
  34.2 0.2 copy-done.3
  34.4 0.1 copy-done.4
  34.5 4.9 %shard_map.69 = (f32[512,512]{1,0:T(8,128)}, f32[10,128,128]{2,1,0:T(8,128)}) custom-call(s32[8]{0:T(128)} %landing_ref.1, f32[4,128,512]{2,1,0:T(8,128)} %get-tuple-element.9.base_ref, f32[2,128,512]{2,1,0:T(8,128)} %copy-done.1, f32[2,128,512]{2,1,0:T(8,128)} %copy-done.2, f32[2,128,512]{2,1,0:T(8,128)} %copy-done.3, f32[2,128,512]{2,1,0:T(8,128)} %copy-done.4), custom_call_target="tpu_custom_call" | custom-call | tf_op jit(solution)/shard_map/pallas_call | solution.py:222
  39.4 0.0 copy-start
  39.4 1.1 dynamic_slice.25
  40.5 0.1 collective-permute-start.4
  40.6 1.6 %collective-permute-done.4 = f32[81920]{0:T(1024)S(1)} collective-permute-done((f32[81920]{0:T(1024)S(1)}, f32[81920]{0:T(1024)S(1)}, u32[]{:S(2)}, u32[]{:S(2)}) %collective-permute-start.4) | collective-permute-done | bytes 327712 | tf_op jit(solution)/shard_map/ppermute | solution.py:141
  42.2 0.0 copy-done
  42.3 3.5 %collective-permute-start.7 = (f32[20480]{0:T(1024)S(1)}, f32[20480]{0:T(1024)S(1)}, u32[]{:S(2)}, u32[]{:S(2)}) collective-permute-start(f32[20480]{0:T(1024)S(1)} %get-tuple-element.22), channel_id=1, source_target_pairs={{0,6},{2,4},{4,2},{6,0},{8,14},{10,12},{12,10},{14,8},{1,7},{3,5},... | collective-permute-start | bytes 245768 | tf_op jit(solution)/shard_map/ppermute | solution.py:141
  45.7 0.4 collective-permute-start.6
  46.2 0.2 collective-permute-start.5
  46.4 2.6 %collective-permute-done.7 = f32[20480]{0:T(1024)S(1)} collective-permute-done((f32[20480]{0:T(1024)S(1)}, f32[20480]{0:T(1024)S(1)}, u32[]{:S(2)}, u32[]{:S(2)}) %collective-permute-start.7) | collective-permute-done | bytes 81952 | tf_op jit(solution)/shard_map/ppermute | solution.py:141
  49.0 1.4 %collective-permute-done.6 = f32[20480]{0:T(1024)S(1)} collective-permute-done((f32[20480]{0:T(1024)S(1)}, f32[20480]{0:T(1024)S(1)}, u32[]{:S(2)}, u32[]{:S(2)}) %collective-permute-start.6) | collective-permute-done | bytes 81952 | tf_op jit(solution)/shard_map/ppermute | solution.py:141
  50.4 0.2 collective-permute-done.5
  50.7 2.6 %collective-permute-start.8 = (f32[10240]{0:T(1024)S(1)}, f32[10240]{0:T(1024)S(1)}, u32[]{:S(2)}, u32[]{:S(2)}) collective-permute-start(f32[10240]{0:T(1024)S(1)} %dynamic_slice.31), channel_id=1, source_target_pairs={{0,8},{2,10},{4,12},{6,14},{8,0},{10,2},{12,4},{14,6},{1,9},{3,11}... | collective-permute-start | bytes 122888 | tf_op jit(solution)/shard_map/ppermute | solution.py:141
  53.3 2.3 %collective-permute-done.8 = f32[10240]{0:T(1024)S(1)} collective-permute-done((f32[10240]{0:T(1024)S(1)}, f32[10240]{0:T(1024)S(1)}, u32[]{:S(2)}, u32[]{:S(2)}) %collective-permute-start.8) | collective-permute-done | bytes 40992 | tf_op jit(solution)/shard_map/ppermute | solution.py:141
  55.6 2.6 %collective-permute-start.9 = (f32[10240]{0:T(1024)S(1)}, f32[10240]{0:T(1024)S(1)}, u32[]{:S(2)}, u32[]{:S(2)}) collective-permute-start(f32[10240]{0:T(1024)S(1)} %dynamic-slice_add_fusion.1), channel_id=1, source_target_pairs={{0,8},{2,10},{4,12},{6,14},{8,0},{10,2},{12,4},{14,6},{1,9},{3,11}... | collective-permute-start | bytes 122888 | tf_op jit(solution)/shard_map/ppermute | solution.py:148
  58.3 2.3 %collective-permute-done.9 = f32[10240]{0:T(1024)S(1)} collective-permute-done((f32[10240]{0:T(1024)S(1)}, f32[10240]{0:T(1024)S(1)}, u32[]{:S(2)}, u32[]{:S(2)}) %collective-permute-start.9) | collective-permute-done | bytes 40992 | tf_op jit(solution)/shard_map/ppermute | solution.py:148
  60.6 2.3 %collective-permute-start.10 = (f32[20480]{0:T(1024)S(1)}, f32[20480]{0:T(1024)S(1)}, u32[]{:S(2)}, u32[]{:S(2)}) collective-permute-start(f32[20480]{0:T(1024)S(1)} %pad_maximum_fusion.2), channel_id=1, source_target_pairs={{0,6},{2,4},{4,2},{6,0},{8,14},{10,12},{12,10},{14,8},{1,7},{3,5},... | collective-permute-start | bytes 245768 | tf_op jit(solution)/shard_map/ppermute | solution.py:148
  62.9 0.8 collective-permute-start.11
  63.8 0.4 collective-permute-start.12
  64.2 1.9 %collective-permute-done.10 = f32[20480]{0:T(1024)S(1)} collective-permute-done((f32[20480]{0:T(1024)S(1)}, f32[20480]{0:T(1024)S(1)}, u32[]{:S(2)}, u32[]{:S(2)}) %collective-permute-start.10) | collective-permute-done | bytes 81952 | tf_op jit(solution)/shard_map/ppermute | solution.py:148
  66.0 1.4 %collective-permute-done.11 = f32[20480]{0:T(1024)S(1)} collective-permute-done((f32[20480]{0:T(1024)S(1)}, f32[20480]{0:T(1024)S(1)}, u32[]{:S(2)}, u32[]{:S(2)}) %collective-permute-start.11) | collective-permute-done | bytes 81952 | tf_op jit(solution)/shard_map/ppermute | solution.py:148
  67.4 0.8 collective-permute-done.12
  68.3 0.1 collective-permute-start.13
  68.4 1.6 %collective-permute-done.13 = f32[81920]{0:T(1024)S(1)} collective-permute-done((f32[81920]{0:T(1024)S(1)}, f32[81920]{0:T(1024)S(1)}, u32[]{:S(2)}, u32[]{:S(2)}) %collective-permute-start.13) | collective-permute-done | bytes 327712 | tf_op jit(solution)/shard_map/ppermute | solution.py:148
  70.1 0.9 pad_maximum_fusion.g_ref
  71.0 47.8 %shard_map.70 = (bf16[512,512]{1,0:T(8,128)(2,1)}, f32[512,512]{1,0:T(8,128)}) custom-call(f32[10,128,128]{2,1,0:T(8,128)} %pad_maximum_fusion.g_ref, f32[512,512]{1,0:T(8,128)} %get-tuple-element.15.f_ref), custom_call_target="tpu_custom_call" | custom-call | tf_op jit(solution)/shard_map/pallas_call | solution.py:66
  (11 shorter events, 0.2 us)
Async XLA Ops:
  4.9 17.0 %collective-permute-start = (f32[2,128,512]{2,1,0:T(8,128)}, f32[2,128,512]{2,1,0:T(8,128)S(1)}, u32[]{:S(2)}, u32[]{:S(2)}) collective-permute-start(f32[2,128,512]{2,1,0:T(8,128)} %get-tuple-element.10), channel_id=1, source_target_pairs={{2,0},{4,2},{6,4},{8,6},{10,8},{12,10},{14,12},{3,1},{5,3},{7,5},{... | collective-permute-start | bytes 1572872 | tf_op jit(solution)/shard_map/ppermute | solution.py:82
  6.2 27.2 %collective-permute-start.1 = (f32[2,128,512]{2,1,0:T(8,128)}, f32[2,128,512]{2,1,0:T(8,128)S(1)}, u32[]{:S(2)}, u32[]{:S(2)}) collective-permute-start(f32[2,128,512]{2,1,0:T(8,128)} %get-tuple-element.11), channel_id=1, source_target_pairs={{0,2},{2,4},{4,6},{6,8},{8,10},{10,12},{12,14},{1,3},{3,5},{5,7},{... | collective-permute-start | bytes 1572872 | tf_op jit(solution)/shard_map/ppermute | solution.py:82
  11.7 21.7 %collective-permute-start.2 = (f32[2,128,512]{2,1,0:T(8,128)}, f32[2,128,512]{2,1,0:T(8,128)S(1)}, u32[]{:S(2)}, u32[]{:S(2)}) collective-permute-start(f32[2,128,512]{2,1,0:T(8,128)} %get-tuple-element.12), channel_id=1, source_target_pairs={{1,0},{3,2},{5,4},{7,6},{9,8},{11,10},{13,12},{15,14},{17,16},{19,... | collective-permute-start | bytes 1572872 | tf_op jit(solution)/shard_map/ppermute | solution.py:82
  13.0 20.4 %collective-permute-start.3 = (f32[2,128,512]{2,1,0:T(8,128)}, f32[2,128,512]{2,1,0:T(8,128)S(1)}, u32[]{:S(2)}, u32[]{:S(2)}) collective-permute-start(f32[2,128,512]{2,1,0:T(8,128)} %get-tuple-element.13), channel_id=1, source_target_pairs={{0,1},{2,3},{4,5},{6,7},{8,9},{10,11},{12,13},{14,15},{16,17},{18,... | collective-permute-start | bytes 1572872 | tf_op jit(solution)/shard_map/ppermute | solution.py:82
  21.9 11.5 %copy-start.1 = (f32[2,128,512]{2,1,0:T(8,128)}, f32[2,128,512]{2,1,0:T(8,128)S(1)}, u32[]{:S(2)}) copy-start(f32[2,128,512]{2,1,0:T(8,128)S(1)} %collective-permute-done.refs_0_) | copy-start | bytes 1572868
  33.4 0.8 copy-start.2
  33.4 1.0 copy-start.3
  33.4 1.1 copy-start.4
  39.4 2.8 %copy-start = (f32[10,128,128]{2,1,0:T(8,128)S(1)}, f32[10,128,128]{2,1,0:T(8,128)}, u32[]{:S(2)}) copy-start(f32[10,128,128]{2,1,0:T(8,128)} %get-tuple-element.14) | copy-start | bytes 1966084
  40.5 1.7 %collective-permute-start.4 = (f32[81920]{0:T(1024)S(1)}, f32[81920]{0:T(1024)S(1)}, u32[]{:S(2)}, u32[]{:S(2)}) collective-permute-start(f32[81920]{0:T(1024)S(1)} %dynamic_slice.25), channel_id=1, source_target_pairs={{0,1},{1,0},{2,3},{3,2},{4,5},{5,4},{6,7},{7,6},{8,9},{9,8},{10,11... | collective-permute-start | bytes 983048 | tf_op jit(solution)/shard_map/ppermute | solution.py:141
  42.3 6.7 %collective-permute-start.7 = (f32[20480]{0:T(1024)S(1)}, f32[20480]{0:T(1024)S(1)}, u32[]{:S(2)}, u32[]{:S(2)}) collective-permute-start(f32[20480]{0:T(1024)S(1)} %get-tuple-element.22), channel_id=1, source_target_pairs={{0,6},{2,4},{4,2},{6,0},{8,14},{10,12},{12,10},{14,8},{1,7},{3,5},... | collective-permute-start | bytes 245768 | tf_op jit(solution)/shard_map/ppermute | solution.py:141
  45.7 4.7 %collective-permute-start.6 = (f32[20480]{0:T(1024)S(1)}, f32[20480]{0:T(1024)S(1)}, u32[]{:S(2)}, u32[]{:S(2)}) collective-permute-start(f32[20480]{0:T(1024)S(1)} %get-tuple-element.23), channel_id=1, source_target_pairs={{0,4},{2,6},{4,0},{6,2},{8,12},{10,14},{12,8},{14,10},{1,5},{3,7},... | collective-permute-start | bytes 245768 | tf_op jit(solution)/shard_map/ppermute | solution.py:141
  46.2 4.4 %collective-permute-start.5 = (f32[20480]{0:T(1024)S(1)}, f32[20480]{0:T(1024)S(1)}, u32[]{:S(2)}, u32[]{:S(2)}) collective-permute-start(f32[20480]{0:T(1024)S(1)} %get-tuple-element.21), channel_id=1, source_target_pairs={{0,2},{2,0},{4,6},{6,4},{8,10},{10,8},{12,14},{14,12},{1,3},{3,1},... | collective-permute-start | bytes 245768 | tf_op jit(solution)/shard_map/ppermute | solution.py:141
  50.7 5.0 %collective-permute-start.8 = (f32[10240]{0:T(1024)S(1)}, f32[10240]{0:T(1024)S(1)}, u32[]{:S(2)}, u32[]{:S(2)}) collective-permute-start(f32[10240]{0:T(1024)S(1)} %dynamic_slice.31), channel_id=1, source_target_pairs={{0,8},{2,10},{4,12},{6,14},{8,0},{10,2},{12,4},{14,6},{1,9},{3,11}... | collective-permute-start | bytes 122888 | tf_op jit(solution)/shard_map/ppermute | solution.py:141
  55.6 5.0 %collective-permute-start.9 = (f32[10240]{0:T(1024)S(1)}, f32[10240]{0:T(1024)S(1)}, u32[]{:S(2)}, u32[]{:S(2)}) collective-permute-start(f32[10240]{0:T(1024)S(1)} %dynamic-slice_add_fusion.1), channel_id=1, source_target_pairs={{0,8},{2,10},{4,12},{6,14},{8,0},{10,2},{12,4},{14,6},{1,9},{3,11}... | collective-permute-start | bytes 122888 | tf_op jit(solution)/shard_map/ppermute | solution.py:148
  60.6 5.4 %collective-permute-start.10 = (f32[20480]{0:T(1024)S(1)}, f32[20480]{0:T(1024)S(1)}, u32[]{:S(2)}, u32[]{:S(2)}) collective-permute-start(f32[20480]{0:T(1024)S(1)} %pad_maximum_fusion.2), channel_id=1, source_target_pairs={{0,6},{2,4},{4,2},{6,0},{8,14},{10,12},{12,10},{14,8},{1,7},{3,5},... | collective-permute-start | bytes 245768 | tf_op jit(solution)/shard_map/ppermute | solution.py:148
  62.9 4.4 %collective-permute-start.11 = (f32[20480]{0:T(1024)S(1)}, f32[20480]{0:T(1024)S(1)}, u32[]{:S(2)}, u32[]{:S(2)}) collective-permute-start(f32[20480]{0:T(1024)S(1)} %pad_maximum_fusion.2), channel_id=1, source_target_pairs={{0,4},{2,6},{4,0},{6,2},{8,12},{10,14},{12,8},{14,10},{1,5},{3,7},... | collective-permute-start | bytes 245768 | tf_op jit(solution)/shard_map/ppermute | solution.py:148
  63.8 4.4 %collective-permute-start.12 = (f32[20480]{0:T(1024)S(1)}, f32[20480]{0:T(1024)S(1)}, u32[]{:S(2)}, u32[]{:S(2)}) collective-permute-start(f32[20480]{0:T(1024)S(1)} %pad_maximum_fusion.2), channel_id=1, source_target_pairs={{0,2},{2,0},{4,6},{6,4},{8,10},{10,8},{12,14},{14,12},{1,3},{3,1},... | collective-permute-start | bytes 245768 | tf_op jit(solution)/shard_map/ppermute | solution.py:148
  68.3 1.7 %collective-permute-start.13 = (f32[81920]{0:T(1024)S(1)}, f32[81920]{0:T(1024)S(1)}, u32[]{:S(2)}, u32[]{:S(2)}) collective-permute-start(f32[81920]{0:T(1024)S(1)} %pad_maximum_fusion.1), channel_id=1, source_target_pairs={{0,1},{1,0},{2,3},{3,2},{4,5},{5,4},{6,7},{7,6},{8,9},{9,8},{10,11... | collective-permute-start | bytes 983048 | tf_op jit(solution)/shard_map/ppermute | solution.py:148

commit v5 on v4

--- a/solution.py
+++ b/solution.py
@@ -247,7 +247,7 @@
         landing, base, [from_next_x, from_prev_x, from_next_y, from_prev_y])
     total_rows = state_rows * lax.axis_size("tx") * lax.axis_size("ty")
     tiles = mode_columns // block
-    upper_sum = grouped_sum(local_tiles.reshape(-1)).reshape(local_tiles.shape)
+    upper_sum = grouped_sum(local_tiles.reshape(-1, block)).reshape(local_tiles.shape)
     rescaled_orthogonal_root, r_factor = factor_solve(upper_sum, predicted_root, total_rows, block)
     return (rescaled_orthogonal_root, r_factor)
 

time: 119 us -> 119 us (level)
  no operation moved by 1% of the time
where the time goes in v5:
time: 119 us
  Pallas kernels  57 us (48%)
  waiting for transfers between devices  33.3 us (28%)
  starting transfers between devices  24.3 us (20%)
  local copies, waits for them, and re-layouts  2.23 us (2%)
    pallas_call x1, Pallas kernels, factor_solve(): pl.pallas_call(functools.partial(factor_kernel, float(total)), out_shape=...  47.8 us
    ppermute x4, waiting for transfers between devices, shifted(): return lax.ppermute(block, axis, route)  17.2 us
    ppermute x4, starting transfers between devices, shifted(): return lax.ppermute(block, axis, route)  11.2 us
    ppermute x5, waiting for transfers between devices, grouped_sum(): kept = kept + lax.ppermute(sent, axis, route)  8.13 us
    ppermute x5, waiting for transfers between devices, grouped_sum(): got.append(lax.ppermute(flat, axis, route))  7.98 us
    ppermute x5, starting transfers between devices, grouped_sum(): kept = kept + lax.ppermute(sent, axis, route)  6.82 us
    ppermute x5, starting transfers between devices, grouped_sum(): got.append(lax.ppermute(flat, axis, route))  6.26 us
    pallas_call x1, Pallas kernels, land_and_gram(): pl.pallas_call(land_kernel, out_shape=(jax.ShapeDtypeStruct((nblk * block...  4.9 us
  transfers between devices with their start and end apart: 14, of which 12 were waited for; matrix products, arithmetic and copies ran while one was open for 0% of the time, Pallas kernels for 0%

profile of v5, /device:TPU:0, one launch (start us, length us, event | category | flops | bytes accessed | tf_op | source)
XLA Modules:
  0.0 118.8 jit_solution(9014781238398680294)
XLA Ops:
  0.6 4.3 %shard_map.68 = (f32[4,128,512]{2,1,0:T(8,128)}, f32[2,128,512]{2,1,0:T(8,128)}, f32[2,128,512]{2,1,0:T(8,128)}, f32[2,128,512]{2,1,0:T(8,128)}, f32[2,128,512]{2,1,0:T(8,128)}) custom-call(s32[28]{0:T(128)} %rows_ref.1, s32[28]{0:T(128)} %cols_ref.1, bf16[28,128,128]{2,1,0:T(8,128)(2,1)} %jac_ref.1, bf16[4,128,512]{2,1,0:T(8,128)(2,1)} %bitcast.6), custom_call_target="tpu_custom_call" | custom-call | tf_op jit(solution)/shard_map/pallas_call | solution.py:183
  4.9 1.3 %collective-permute-start = (f32[2,128,512]{2,1,0:T(8,128)}, f32[2,128,512]{2,1,0:T(8,128)S(1)}, u32[]{:S(2)}, u32[]{:S(2)}) collective-permute-start(f32[2,128,512]{2,1,0:T(8,128)} %get-tuple-element.10), channel_id=1, source_target_pairs={{2,0},{4,2},{6,4},{8,6},{10,8},{12,10},{14,12},{3,1},{5,3},{7,5},{... | collective-permute-start | bytes 1572872 | tf_op jit(solution)/shard_map/ppermute | solution.py:82
  6.2 5.5 %collective-permute-start.1 = (f32[2,128,512]{2,1,0:T(8,128)}, f32[2,128,512]{2,1,0:T(8,128)S(1)}, u32[]{:S(2)}, u32[]{:S(2)}) collective-permute-start(f32[2,128,512]{2,1,0:T(8,128)} %get-tuple-element.11), channel_id=1, source_target_pairs={{0,2},{2,4},{4,6},{6,8},{8,10},{10,12},{12,14},{1,3},{3,5},{5,7},{... | collective-permute-start | bytes 1572872 | tf_op jit(solution)/shard_map/ppermute | solution.py:82
  11.7 1.3 %collective-permute-start.2 = (f32[2,128,512]{2,1,0:T(8,128)}, f32[2,128,512]{2,1,0:T(8,128)S(1)}, u32[]{:S(2)}, u32[]{:S(2)}) collective-permute-start(f32[2,128,512]{2,1,0:T(8,128)} %get-tuple-element.12), channel_id=1, source_target_pairs={{1,0},{3,2},{5,4},{7,6},{9,8},{11,10},{13,12},{15,14},{17,16},{19,... | collective-permute-start | bytes 1572872 | tf_op jit(solution)/shard_map/ppermute | solution.py:82
  13.0 3.1 %collective-permute-start.3 = (f32[2,128,512]{2,1,0:T(8,128)}, f32[2,128,512]{2,1,0:T(8,128)S(1)}, u32[]{:S(2)}, u32[]{:S(2)}) collective-permute-start(f32[2,128,512]{2,1,0:T(8,128)} %get-tuple-element.13), channel_id=1, source_target_pairs={{0,1},{2,3},{4,5},{6,7},{8,9},{10,11},{12,13},{14,15},{16,17},{18,... | collective-permute-start | bytes 1572872 | tf_op jit(solution)/shard_map/ppermute | solution.py:82
  16.2 5.7 %collective-permute-done.refs_0_ = f32[2,128,512]{2,1,0:T(8,128)S(1)} collective-permute-done((f32[2,128,512]{2,1,0:T(8,128)}, f32[2,128,512]{2,1,0:T(8,128)S(1)}, u32[]{:S(2)}, u32[]{:S(2)}) %collective-permute-start) | collective-permute-done | bytes 524320 | tf_op jit(solution)/shard_map/ppermute | solution.py:82
  21.9 0.0 copy-start.1
  21.9 11.5 %collective-permute-done.1.refs_1_ = f32[2,128,512]{2,1,0:T(8,128)S(1)} collective-permute-done((f32[2,128,512]{2,1,0:T(8,128)}, f32[2,128,512]{2,1,0:T(8,128)S(1)}, u32[]{:S(2)}, u32[]{:S(2)}) %collective-permute-start.1) | collective-permute-done | bytes 524320 | tf_op jit(solution)/shard_map/ppermute | solution.py:82
  33.4 0.0 copy-start.2
  33.4 0.0 collective-permute-done.2.refs_2_
  33.4 0.0 copy-start.3
  33.4 0.0 collective-permute-done.3.refs_3_
  33.4 0.0 copy-start.4
  33.4 0.0 copy-done.1
  33.4 0.8 copy-done.2
  34.2 0.2 copy-done.3
  34.4 0.1 copy-done.4
  34.5 4.9 %shard_map.69 = (f32[512,512]{1,0:T(8,128)}, f32[10,128,128]{2,1,0:T(8,128)}) custom-call(s32[8]{0:T(128)} %landing_ref.1, f32[4,128,512]{2,1,0:T(8,128)} %get-tuple-element.9.base_ref, f32[2,128,512]{2,1,0:T(8,128)} %copy-done.1, f32[2,128,512]{2,1,0:T(8,128)} %copy-done.2, f32[2,128,512]{2,1,0:T(8,128)} %copy-done.3, f32[2,128,512]{2,1,0:T(8,128)} %copy-done.4), custom_call_target="tpu_custom_call" | custom-call | tf_op jit(solution)/shard_map/pallas_call | solution.py:222
  39.4 0.0 copy-start
  39.4 1.1 constant_dynamic-slice_fusion.4
  40.5 0.1 collective-permute-start.4
  40.6 1.6 %collective-permute-done.4 = f32[640,128]{1,0:T(8,128)S(1)} collective-permute-done((f32[640,128]{1,0:T(8,128)S(1)}, f32[640,128]{1,0:T(8,128)S(1)}, u32[]{:S(2)}, u32[]{:S(2)}) %collective-permute-start.4) | collective-permute-done | bytes 327712 | tf_op jit(solution)/shard_map/ppermute | solution.py:141
  42.2 0.0 copy-done
  42.3 3.5 %collective-permute-start.7 = (f32[160,128]{1,0:T(8,128)S(1)}, f32[160,128]{1,0:T(8,128)S(1)}, u32[]{:S(2)}, u32[]{:S(2)}) collective-permute-start(f32[160,128]{1,0:T(8,128)S(1)} %get-tuple-element.22), channel_id=1, source_target_pairs={{0,6},{2,4},{4,2},{6,0},{8,14},{10,12},{12,10},{14,8},{1,7},{3,5},... | collective-permute-start | bytes 245768 | tf_op jit(solution)/shard_map/ppermute | solution.py:141
  45.7 0.4 collective-permute-start.6
  46.2 0.2 collective-permute-start.5
  46.4 2.6 %collective-permute-done.7 = f32[160,128]{1,0:T(8,128)S(1)} collective-permute-done((f32[160,128]{1,0:T(8,128)S(1)}, f32[160,128]{1,0:T(8,128)S(1)}, u32[]{:S(2)}, u32[]{:S(2)}) %collective-permute-start.7) | collective-permute-done | bytes 81952 | tf_op jit(solution)/shard_map/ppermute | solution.py:141
  49.0 1.4 %collective-permute-done.6 = f32[160,128]{1,0:T(8,128)S(1)} collective-permute-done((f32[160,128]{1,0:T(8,128)S(1)}, f32[160,128]{1,0:T(8,128)S(1)}, u32[]{:S(2)}, u32[]{:S(2)}) %collective-permute-start.6) | collective-permute-done | bytes 81952 | tf_op jit(solution)/shard_map/ppermute | solution.py:141
  50.4 0.2 collective-permute-done.5
  50.7 2.6 %collective-permute-start.8 = (f32[80,128]{1,0:T(8,128)S(1)}, f32[80,128]{1,0:T(8,128)S(1)}, u32[]{:S(2)}, u32[]{:S(2)}) collective-permute-start(f32[80,128]{1,0:T(8,128)S(1)} %constant_dynamic-slice_fusion), channel_id=1, source_target_pairs={{0,8},{2,10},{4,12},{6,14},{8,0},{10,2},{12,4},{14,6},{1,9},{3,11}... | collective-permute-start | bytes 122888 | tf_op jit(solution)/shard_map/ppermute | solution.py:141
  53.3 2.3 %collective-permute-done.8 = f32[80,128]{1,0:T(8,128)S(1)} collective-permute-done((f32[80,128]{1,0:T(8,128)S(1)}, f32[80,128]{1,0:T(8,128)S(1)}, u32[]{:S(2)}, u32[]{:S(2)}) %collective-permute-start.8) | collective-permute-done | bytes 40992 | tf_op jit(solution)/shard_map/ppermute | solution.py:141
  55.6 2.6 %collective-permute-start.9 = (f32[80,128]{1,0:T(8,128)S(1)}, f32[80,128]{1,0:T(8,128)S(1)}, u32[]{:S(2)}, u32[]{:S(2)}) collective-permute-start(f32[80,128]{1,0:T(8,128)S(1)} %dynamic-slice_add_fusion.1), channel_id=1, source_target_pairs={{0,8},{2,10},{4,12},{6,14},{8,0},{10,2},{12,4},{14,6},{1,9},{3,11}... | collective-permute-start | bytes 122888 | tf_op jit(solution)/shard_map/ppermute | solution.py:148
  58.3 2.3 %collective-permute-done.9 = f32[80,128]{1,0:T(8,128)S(1)} collective-permute-done((f32[80,128]{1,0:T(8,128)S(1)}, f32[80,128]{1,0:T(8,128)S(1)}, u32[]{:S(2)}, u32[]{:S(2)}) %collective-permute-start.9) | collective-permute-done | bytes 40992 | tf_op jit(solution)/shard_map/ppermute | solution.py:148
  60.6 2.3 %collective-permute-start.10 = (f32[160,128]{1,0:T(8,128)S(1)}, f32[160,128]{1,0:T(8,128)S(1)}, u32[]{:S(2)}, u32[]{:S(2)}) collective-permute-start(f32[160,128]{1,0:T(8,128)S(1)} %pad_maximum_fusion.2), channel_id=1, source_target_pairs={{0,6},{2,4},{4,2},{6,0},{8,14},{10,12},{12,10},{14,8},{1,7},{3,5},... | collective-permute-start | bytes 245768 | tf_op jit(solution)/shard_map/ppermute | solution.py:148
  62.9 0.8 collective-permute-start.11
  63.8 0.4 collective-permute-start.12
  64.2 1.9 %collective-permute-done.10 = f32[160,128]{1,0:T(8,128)S(1)} collective-permute-done((f32[160,128]{1,0:T(8,128)S(1)}, f32[160,128]{1,0:T(8,128)S(1)}, u32[]{:S(2)}, u32[]{:S(2)}) %collective-permute-start.10) | collective-permute-done | bytes 81952 | tf_op jit(solution)/shard_map/ppermute | solution.py:148
  66.0 1.4 %collective-permute-done.11 = f32[160,128]{1,0:T(8,128)S(1)} collective-permute-done((f32[160,128]{1,0:T(8,128)S(1)}, f32[160,128]{1,0:T(8,128)S(1)}, u32[]{:S(2)}, u32[]{:S(2)}) %collective-permute-start.11) | collective-permute-done | bytes 81952 | tf_op jit(solution)/shard_map/ppermute | solution.py:148
  67.4 0.8 collective-permute-done.12
  68.3 0.1 collective-permute-start.13
  68.4 1.6 %collective-permute-done.13 = f32[640,128]{1,0:T(8,128)S(1)} collective-permute-done((f32[640,128]{1,0:T(8,128)S(1)}, f32[640,128]{1,0:T(8,128)S(1)}, u32[]{:S(2)}, u32[]{:S(2)}) %collective-permute-start.13) | collective-permute-done | bytes 327712 | tf_op jit(solution)/shard_map/ppermute | solution.py:148
  70.1 0.9 pad_maximum_fusion
  71.0 47.8 %shard_map.70 = (bf16[512,512]{1,0:T(8,128)(2,1)}, f32[512,512]{1,0:T(8,128)}) custom-call(f32[10,128,128]{2,1,0:T(8,128)} %bitcast.3, f32[512,512]{1,0:T(8,128)} %get-tuple-element.15.f_ref), custom_call_target="tpu_custom_call" | custom-call | tf_op jit(solution)/shard_map/pallas_call | solution.py:66
  (11 shorter events, 0.2 us)
Async XLA Ops:
  4.9 17.0 %collective-permute-start = (f32[2,128,512]{2,1,0:T(8,128)}, f32[2,128,512]{2,1,0:T(8,128)S(1)}, u32[]{:S(2)}, u32[]{:S(2)}) collective-permute-start(f32[2,128,512]{2,1,0:T(8,128)} %get-tuple-element.10), channel_id=1, source_target_pairs={{2,0},{4,2},{6,4},{8,6},{10,8},{12,10},{14,12},{3,1},{5,3},{7,5},{... | collective-permute-start | bytes 1572872 | tf_op jit(solution)/shard_map/ppermute | solution.py:82
  6.2 27.2 %collective-permute-start.1 = (f32[2,128,512]{2,1,0:T(8,128)}, f32[2,128,512]{2,1,0:T(8,128)S(1)}, u32[]{:S(2)}, u32[]{:S(2)}) collective-permute-start(f32[2,128,512]{2,1,0:T(8,128)} %get-tuple-element.11), channel_id=1, source_target_pairs={{0,2},{2,4},{4,6},{6,8},{8,10},{10,12},{12,14},{1,3},{3,5},{5,7},{... | collective-permute-start | bytes 1572872 | tf_op jit(solution)/shard_map/ppermute | solution.py:82
  11.7 21.7 %collective-permute-start.2 = (f32[2,128,512]{2,1,0:T(8,128)}, f32[2,128,512]{2,1,0:T(8,128)S(1)}, u32[]{:S(2)}, u32[]{:S(2)}) collective-permute-start(f32[2,128,512]{2,1,0:T(8,128)} %get-tuple-element.12), channel_id=1, source_target_pairs={{1,0},{3,2},{5,4},{7,6},{9,8},{11,10},{13,12},{15,14},{17,16},{19,... | collective-permute-start | bytes 1572872 | tf_op jit(solution)/shard_map/ppermute | solution.py:82
  13.0 20.4 %collective-permute-start.3 = (f32[2,128,512]{2,1,0:T(8,128)}, f32[2,128,512]{2,1,0:T(8,128)S(1)}, u32[]{:S(2)}, u32[]{:S(2)}) collective-permute-start(f32[2,128,512]{2,1,0:T(8,128)} %get-tuple-element.13), channel_id=1, source_target_pairs={{0,1},{2,3},{4,5},{6,7},{8,9},{10,11},{12,13},{14,15},{16,17},{18,... | collective-permute-start | bytes 1572872 | tf_op jit(solution)/shard_map/ppermute | solution.py:82
  21.9 11.5 %copy-start.1 = (f32[2,128,512]{2,1,0:T(8,128)}, f32[2,128,512]{2,1,0:T(8,128)S(1)}, u32[]{:S(2)}) copy-start(f32[2,128,512]{2,1,0:T(8,128)S(1)} %collective-permute-done.refs_0_) | copy-start | bytes 1572868
  33.4 0.8 copy-start.2
  33.4 1.0 copy-start.3
  33.4 1.1 copy-start.4
  39.4 2.8 %copy-start = (f32[10,128,128]{2,1,0:T(8,128)S(1)}, f32[10,128,128]{2,1,0:T(8,128)}, u32[]{:S(2)}) copy-start(f32[10,128,128]{2,1,0:T(8,128)} %get-tuple-element.14) | copy-start | bytes 1966084
  40.5 1.7 %collective-permute-start.4 = (f32[640,128]{1,0:T(8,128)S(1)}, f32[640,128]{1,0:T(8,128)S(1)}, u32[]{:S(2)}, u32[]{:S(2)}) collective-permute-start(f32[640,128]{1,0:T(8,128)S(1)} %constant_dynamic-slice_fusion.4), channel_id=1, source_target_pairs={{0,1},{1,0},{2,3},{3,2},{4,5},{5,4},{6,7},{7,6},{8,9},{9,8},{10,11... | collective-permute-start | bytes 983048 | tf_op jit(solution)/shard_map/ppermute | solution.py:141
  42.3 6.7 %collective-permute-start.7 = (f32[160,128]{1,0:T(8,128)S(1)}, f32[160,128]{1,0:T(8,128)S(1)}, u32[]{:S(2)}, u32[]{:S(2)}) collective-permute-start(f32[160,128]{1,0:T(8,128)S(1)} %get-tuple-element.22), channel_id=1, source_target_pairs={{0,6},{2,4},{4,2},{6,0},{8,14},{10,12},{12,10},{14,8},{1,7},{3,5},... | collective-permute-start | bytes 245768 | tf_op jit(solution)/shard_map/ppermute | solution.py:141
  45.7 4.7 %collective-permute-start.6 = (f32[160,128]{1,0:T(8,128)S(1)}, f32[160,128]{1,0:T(8,128)S(1)}, u32[]{:S(2)}, u32[]{:S(2)}) collective-permute-start(f32[160,128]{1,0:T(8,128)S(1)} %get-tuple-element.23), channel_id=1, source_target_pairs={{0,4},{2,6},{4,0},{6,2},{8,12},{10,14},{12,8},{14,10},{1,5},{3,7},... | collective-permute-start | bytes 245768 | tf_op jit(solution)/shard_map/ppermute | solution.py:141
  46.2 4.4 %collective-permute-start.5 = (f32[160,128]{1,0:T(8,128)S(1)}, f32[160,128]{1,0:T(8,128)S(1)}, u32[]{:S(2)}, u32[]{:S(2)}) collective-permute-start(f32[160,128]{1,0:T(8,128)S(1)} %get-tuple-element.21), channel_id=1, source_target_pairs={{0,2},{2,0},{4,6},{6,4},{8,10},{10,8},{12,14},{14,12},{1,3},{3,1},... | collective-permute-start | bytes 245768 | tf_op jit(solution)/shard_map/ppermute | solution.py:141
  50.7 5.0 %collective-permute-start.8 = (f32[80,128]{1,0:T(8,128)S(1)}, f32[80,128]{1,0:T(8,128)S(1)}, u32[]{:S(2)}, u32[]{:S(2)}) collective-permute-start(f32[80,128]{1,0:T(8,128)S(1)} %constant_dynamic-slice_fusion), channel_id=1, source_target_pairs={{0,8},{2,10},{4,12},{6,14},{8,0},{10,2},{12,4},{14,6},{1,9},{3,11}... | collective-permute-start | bytes 122888 | tf_op jit(solution)/shard_map/ppermute | solution.py:141
  55.6 5.0 %collective-permute-start.9 = (f32[80,128]{1,0:T(8,128)S(1)}, f32[80,128]{1,0:T(8,128)S(1)}, u32[]{:S(2)}, u32[]{:S(2)}) collective-permute-start(f32[80,128]{1,0:T(8,128)S(1)} %dynamic-slice_add_fusion.1), channel_id=1, source_target_pairs={{0,8},{2,10},{4,12},{6,14},{8,0},{10,2},{12,4},{14,6},{1,9},{3,11}... | collective-permute-start | bytes 122888 | tf_op jit(solution)/shard_map/ppermute | solution.py:148
  60.6 5.4 %collective-permute-start.10 = (f32[160,128]{1,0:T(8,128)S(1)}, f32[160,128]{1,0:T(8,128)S(1)}, u32[]{:S(2)}, u32[]{:S(2)}) collective-permute-start(f32[160,128]{1,0:T(8,128)S(1)} %pad_maximum_fusion.2), channel_id=1, source_target_pairs={{0,6},{2,4},{4,2},{6,0},{8,14},{10,12},{12,10},{14,8},{1,7},{3,5},... | collective-permute-start | bytes 245768 | tf_op jit(solution)/shard_map/ppermute | solution.py:148
  62.9 4.4 %collective-permute-start.11 = (f32[160,128]{1,0:T(8,128)S(1)}, f32[160,128]{1,0:T(8,128)S(1)}, u32[]{:S(2)}, u32[]{:S(2)}) collective-permute-start(f32[160,128]{1,0:T(8,128)S(1)} %pad_maximum_fusion.2), channel_id=1, source_target_pairs={{0,4},{2,6},{4,0},{6,2},{8,12},{10,14},{12,8},{14,10},{1,5},{3,7},... | collective-permute-start | bytes 245768 | tf_op jit(solution)/shard_map/ppermute | solution.py:148
  63.8 4.4 %collective-permute-start.12 = (f32[160,128]{1,0:T(8,128)S(1)}, f32[160,128]{1,0:T(8,128)S(1)}, u32[]{:S(2)}, u32[]{:S(2)}) collective-permute-start(f32[160,128]{1,0:T(8,128)S(1)} %pad_maximum_fusion.2), channel_id=1, source_target_pairs={{0,2},{2,0},{4,6},{6,4},{8,10},{10,8},{12,14},{14,12},{1,3},{3,1},... | collective-permute-start | bytes 245768 | tf_op jit(solution)/shard_map/ppermute | solution.py:148
  68.3 1.7 %collective-permute-start.13 = (f32[640,128]{1,0:T(8,128)S(1)}, f32[640,128]{1,0:T(8,128)S(1)}, u32[]{:S(2)}, u32[]{:S(2)}) collective-permute-start(f32[640,128]{1,0:T(8,128)S(1)} %pad_maximum_fusion.1), channel_id=1, source_target_pairs={{0,1},{1,0},{2,3},{3,2},{4,5},{5,4},{6,7},{7,6},{8,9},{9,8},{10,11... | collective-permute-start | bytes 983048 | tf_op jit(solution)/shard_map/ppermute | solution.py:148

commit v6 on v5

--- a/solution.py
+++ b/solution.py
@@ -45,12 +45,18 @@
             inv_ref[k, s:, :] = inv_ref[k, s:, :] - v * brow
         if k < nb - 1:
             e = o + b
+            dims = (((0,), (0,)), ((), ()))
             panel = jnp.dot(inv_ref[k], w_ref[o:e, e:], precision=HI, preferred_element_type=jnp.float32)
             u_ref[o:e, e:] = panel
-            w_ref[e:, e:] = w_ref[e:, e:] - lax.dot_general(
-                panel, panel, (((0,), (0,)), ((), ())), precision=HI, preferred_element_type=jnp.float32)
-    for k in range(nb):
-        o = k * b
+            near = panel[:, :b]
+            w_ref[e:e + b, e:e + b] = w_ref[e:e + b, e:e + b] - lax.dot_general(
+                near, near, dims, precision=HI, preferred_element_type=jnp.float32)
+            if e + b < n:
+                far = panel[:, b:]
+                w_ref[e:e + b, e + b:] = w_ref[e:e + b, e + b:] - lax.dot_general(
+                    near, far, dims, precision=HI, preferred_element_type=jnp.float32)
+                w_ref[e + b:, e + b:] = w_ref[e + b:, e + b:] - lax.dot_general(
+                    far, far, dims, precision=HI, preferred_element_type=jnp.float32)
         y = f_ref[:, o:o + b]
         if k > 0:
             y = y - jnp.dot(xs_ref[:, :o], u_ref[:o, o:o + b], precision=HI, preferred_element_type=jnp.float32)

time: 119 us -> 118 us (level)
  no operation moved by 1% of the time
where the time goes in v6:
time: 118 us
  Pallas kernels  56.4 us (48%)
  waiting for transfers between devices  33.3 us (28%)
  starting transfers between devices  24.3 us (21%)
  local copies, waits for them, and re-layouts  2.23 us (2%)
    pallas_call x1, Pallas kernels, factor_solve(): pl.pallas_call(functools.partial(factor_kernel, float(total)), out_shape=...  47.2 us
    ppermute x4, waiting for transfers between devices, shifted(): return lax.ppermute(block, axis, route)  17.2 us
    ppermute x4, starting transfers between devices, shifted(): return lax.ppermute(block, axis, route)  11.2 us
    ppermute x5, waiting for transfers between devices, grouped_sum(): kept = kept + lax.ppermute(sent, axis, route)  8.13 us
    ppermute x5, waiting for transfers between devices, grouped_sum(): got.append(lax.ppermute(flat, axis, route))  7.98 us
    ppermute x5, starting transfers between devices, grouped_sum(): kept = kept + lax.ppermute(sent, axis, route)  6.82 us
    ppermute x5, starting transfers between devices, grouped_sum(): got.append(lax.ppermute(flat, axis, route))  6.26 us
    pallas_call x1, Pallas kernels, land_and_gram(): pl.pallas_call(land_kernel, out_shape=(jax.ShapeDtypeStruct((nblk * block...  4.9 us
  transfers between devices with their start and end apart: 14, of which 12 were waited for; matrix products, arithmetic and copies ran while one was open for 0% of the time, Pallas kernels for 0%

profile of v6, /device:TPU:0, one launch (start us, length us, event | category | flops | bytes accessed | tf_op | source)
XLA Modules:
  0.0 118.2 jit_solution(16070741179528064168)
XLA Ops:
  0.6 4.3 %shard_map.68 = (f32[4,128,512]{2,1,0:T(8,128)}, f32[2,128,512]{2,1,0:T(8,128)}, f32[2,128,512]{2,1,0:T(8,128)}, f32[2,128,512]{2,1,0:T(8,128)}, f32[2,128,512]{2,1,0:T(8,128)}) custom-call(s32[28]{0:T(128)} %rows_ref.1, s32[28]{0:T(128)} %cols_ref.1, bf16[28,128,128]{2,1,0:T(8,128)(2,1)} %jac_ref.1, bf16[4,128,512]{2,1,0:T(8,128)(2,1)} %bitcast.6), custom_call_target="tpu_custom_call" | custom-call | tf_op jit(solution)/shard_map/pallas_call | solution.py:189
  4.9 1.3 %collective-permute-start = (f32[2,128,512]{2,1,0:T(8,128)}, f32[2,128,512]{2,1,0:T(8,128)S(1)}, u32[]{:S(2)}, u32[]{:S(2)}) collective-permute-start(f32[2,128,512]{2,1,0:T(8,128)} %get-tuple-element.10), channel_id=1, source_target_pairs={{2,0},{4,2},{6,4},{8,6},{10,8},{12,10},{14,12},{3,1},{5,3},{7,5},{... | collective-permute-start | bytes 1572872 | tf_op jit(solution)/shard_map/ppermute | solution.py:88
  6.2 5.5 %collective-permute-start.1 = (f32[2,128,512]{2,1,0:T(8,128)}, f32[2,128,512]{2,1,0:T(8,128)S(1)}, u32[]{:S(2)}, u32[]{:S(2)}) collective-permute-start(f32[2,128,512]{2,1,0:T(8,128)} %get-tuple-element.11), channel_id=1, source_target_pairs={{0,2},{2,4},{4,6},{6,8},{8,10},{10,12},{12,14},{1,3},{3,5},{5,7},{... | collective-permute-start | bytes 1572872 | tf_op jit(solution)/shard_map/ppermute | solution.py:88
  11.7 1.3 %collective-permute-start.2 = (f32[2,128,512]{2,1,0:T(8,128)}, f32[2,128,512]{2,1,0:T(8,128)S(1)}, u32[]{:S(2)}, u32[]{:S(2)}) collective-permute-start(f32[2,128,512]{2,1,0:T(8,128)} %get-tuple-element.12), channel_id=1, source_target_pairs={{1,0},{3,2},{5,4},{7,6},{9,8},{11,10},{13,12},{15,14},{17,16},{19,... | collective-permute-start | bytes 1572872 | tf_op jit(solution)/shard_map/ppermute | solution.py:88
  13.0 3.1 %collective-permute-start.3 = (f32[2,128,512]{2,1,0:T(8,128)}, f32[2,128,512]{2,1,0:T(8,128)S(1)}, u32[]{:S(2)}, u32[]{:S(2)}) collective-permute-start(f32[2,128,512]{2,1,0:T(8,128)} %get-tuple-element.13), channel_id=1, source_target_pairs={{0,1},{2,3},{4,5},{6,7},{8,9},{10,11},{12,13},{14,15},{16,17},{18,... | collective-permute-start | bytes 1572872 | tf_op jit(solution)/shard_map/ppermute | solution.py:88
  16.2 5.7 %collective-permute-done.refs_0_ = f32[2,128,512]{2,1,0:T(8,128)S(1)} collective-permute-done((f32[2,128,512]{2,1,0:T(8,128)}, f32[2,128,512]{2,1,0:T(8,128)S(1)}, u32[]{:S(2)}, u32[]{:S(2)}) %collective-permute-start) | collective-permute-done | bytes 524320 | tf_op jit(solution)/shard_map/ppermute | solution.py:88
  21.9 0.0 copy-start.1
  21.9 11.5 %collective-permute-done.1.refs_1_ = f32[2,128,512]{2,1,0:T(8,128)S(1)} collective-permute-done((f32[2,128,512]{2,1,0:T(8,128)}, f32[2,128,512]{2,1,0:T(8,128)S(1)}, u32[]{:S(2)}, u32[]{:S(2)}) %collective-permute-start.1) | collective-permute-done | bytes 524320 | tf_op jit(solution)/shard_map/ppermute | solution.py:88
  33.4 0.0 copy-start.2
  33.4 0.0 collective-permute-done.2.refs_2_
  33.4 0.0 copy-start.3
  33.4 0.0 collective-permute-done.3.refs_3_
  33.4 0.0 copy-start.4
  33.4 0.0 copy-done.1
  33.4 0.8 copy-done.2
  34.2 0.2 copy-done.3
  34.4 0.1 copy-done.4
  34.5 4.9 %shard_map.69 = (f32[512,512]{1,0:T(8,128)}, f32[10,128,128]{2,1,0:T(8,128)}) custom-call(s32[8]{0:T(128)} %landing_ref.1, f32[4,128,512]{2,1,0:T(8,128)} %get-tuple-element.9.base_ref, f32[2,128,512]{2,1,0:T(8,128)} %copy-done.1, f32[2,128,512]{2,1,0:T(8,128)} %copy-done.2, f32[2,128,512]{2,1,0:T(8,128)} %copy-done.3, f32[2,128,512]{2,1,0:T(8,128)} %copy-done.4), custom_call_target="tpu_custom_call" | custom-call | tf_op jit(solution)/shard_map/pallas_call | solution.py:228
  39.4 0.0 copy-start
  39.4 1.1 constant_dynamic-slice_fusion.4
  40.5 0.1 collective-permute-start.4
  40.6 1.6 %collective-permute-done.4 = f32[640,128]{1,0:T(8,128)S(1)} collective-permute-done((f32[640,128]{1,0:T(8,128)S(1)}, f32[640,128]{1,0:T(8,128)S(1)}, u32[]{:S(2)}, u32[]{:S(2)}) %collective-permute-start.4) | collective-permute-done | bytes 327712 | tf_op jit(solution)/shard_map/ppermute | solution.py:147
  42.2 0.0 copy-done
  42.3 3.5 %collective-permute-start.7 = (f32[160,128]{1,0:T(8,128)S(1)}, f32[160,128]{1,0:T(8,128)S(1)}, u32[]{:S(2)}, u32[]{:S(2)}) collective-permute-start(f32[160,128]{1,0:T(8,128)S(1)} %get-tuple-element.22), channel_id=1, source_target_pairs={{0,6},{2,4},{4,2},{6,0},{8,14},{10,12},{12,10},{14,8},{1,7},{3,5},... | collective-permute-start | bytes 245768 | tf_op jit(solution)/shard_map/ppermute | solution.py:147
  45.7 0.4 collective-permute-start.6
  46.2 0.2 collective-permute-start.5
  46.4 2.6 %collective-permute-done.7 = f32[160,128]{1,0:T(8,128)S(1)} collective-permute-done((f32[160,128]{1,0:T(8,128)S(1)}, f32[160,128]{1,0:T(8,128)S(1)}, u32[]{:S(2)}, u32[]{:S(2)}) %collective-permute-start.7) | collective-permute-done | bytes 81952 | tf_op jit(solution)/shard_map/ppermute | solution.py:147
  49.0 1.4 %collective-permute-done.6 = f32[160,128]{1,0:T(8,128)S(1)} collective-permute-done((f32[160,128]{1,0:T(8,128)S(1)}, f32[160,128]{1,0:T(8,128)S(1)}, u32[]{:S(2)}, u32[]{:S(2)}) %collective-permute-start.6) | collective-permute-done | bytes 81952 | tf_op jit(solution)/shard_map/ppermute | solution.py:147
  50.4 0.2 collective-permute-done.5
  50.7 2.6 %collective-permute-start.8 = (f32[80,128]{1,0:T(8,128)S(1)}, f32[80,128]{1,0:T(8,128)S(1)}, u32[]{:S(2)}, u32[]{:S(2)}) collective-permute-start(f32[80,128]{1,0:T(8,128)S(1)} %constant_dynamic-slice_fusion), channel_id=1, source_target_pairs={{0,8},{2,10},{4,12},{6,14},{8,0},{10,2},{12,4},{14,6},{1,9},{3,11}... | collective-permute-start | bytes 122888 | tf_op jit(solution)/shard_map/ppermute | solution.py:147
  53.3 2.3 %collective-permute-done.8 = f32[80,128]{1,0:T(8,128)S(1)} collective-permute-done((f32[80,128]{1,0:T(8,128)S(1)}, f32[80,128]{1,0:T(8,128)S(1)}, u32[]{:S(2)}, u32[]{:S(2)}) %collective-permute-start.8) | collective-permute-done | bytes 40992 | tf_op jit(solution)/shard_map/ppermute | solution.py:147
  55.6 2.6 %collective-permute-start.9 = (f32[80,128]{1,0:T(8,128)S(1)}, f32[80,128]{1,0:T(8,128)S(1)}, u32[]{:S(2)}, u32[]{:S(2)}) collective-permute-start(f32[80,128]{1,0:T(8,128)S(1)} %dynamic-slice_add_fusion.1), channel_id=1, source_target_pairs={{0,8},{2,10},{4,12},{6,14},{8,0},{10,2},{12,4},{14,6},{1,9},{3,11}... | collective-permute-start | bytes 122888 | tf_op jit(solution)/shard_map/ppermute | solution.py:154
  58.3 2.3 %collective-permute-done.9 = f32[80,128]{1,0:T(8,128)S(1)} collective-permute-done((f32[80,128]{1,0:T(8,128)S(1)}, f32[80,128]{1,0:T(8,128)S(1)}, u32[]{:S(2)}, u32[]{:S(2)}) %collective-permute-start.9) | collective-permute-done | bytes 40992 | tf_op jit(solution)/shard_map/ppermute | solution.py:154
  60.6 2.3 %collective-permute-start.10 = (f32[160,128]{1,0:T(8,128)S(1)}, f32[160,128]{1,0:T(8,128)S(1)}, u32[]{:S(2)}, u32[]{:S(2)}) collective-permute-start(f32[160,128]{1,0:T(8,128)S(1)} %pad_maximum_fusion.2), channel_id=1, source_target_pairs={{0,6},{2,4},{4,2},{6,0},{8,14},{10,12},{12,10},{14,8},{1,7},{3,5},... | collective-permute-start | bytes 245768 | tf_op jit(solution)/shard_map/ppermute | solution.py:154
  62.9 0.8 collective-permute-start.11
  63.8 0.4 collective-permute-start.12
  64.2 1.9 %collective-permute-done.10 = f32[160,128]{1,0:T(8,128)S(1)} collective-permute-done((f32[160,128]{1,0:T(8,128)S(1)}, f32[160,128]{1,0:T(8,128)S(1)}, u32[]{:S(2)}, u32[]{:S(2)}) %collective-permute-start.10) | collective-permute-done | bytes 81952 | tf_op jit(solution)/shard_map/ppermute | solution.py:154
  66.0 1.4 %collective-permute-done.11 = f32[160,128]{1,0:T(8,128)S(1)} collective-permute-done((f32[160,128]{1,0:T(8,128)S(1)}, f32[160,128]{1,0:T(8,128)S(1)}, u32[]{:S(2)}, u32[]{:S(2)}) %collective-permute-start.11) | collective-permute-done | bytes 81952 | tf_op jit(solution)/shard_map/ppermute | solution.py:154
  67.4 0.8 collective-permute-done.12
  68.3 0.1 collective-permute-start.13
  68.4 1.6 %collective-permute-done.13 = f32[640,128]{1,0:T(8,128)S(1)} collective-permute-done((f32[640,128]{1,0:T(8,128)S(1)}, f32[640,128]{1,0:T(8,128)S(1)}, u32[]{:S(2)}, u32[]{:S(2)}) %collective-permute-start.13) | collective-permute-done | bytes 327712 | tf_op jit(solution)/shard_map/ppermute | solution.py:154
  70.1 0.9 pad_maximum_fusion
  71.0 47.2 %shard_map.70 = (bf16[512,512]{1,0:T(8,128)(2,1)}, f32[512,512]{1,0:T(8,128)}) custom-call(f32[10,128,128]{2,1,0:T(8,128)} %bitcast.3, f32[512,512]{1,0:T(8,128)} %get-tuple-element.15.f_ref), custom_call_target="tpu_custom_call" | custom-call | tf_op jit(solution)/shard_map/pallas_call | solution.py:72
  (11 shorter events, 0.2 us)
Async XLA Ops:
  4.9 17.0 %collective-permute-start = (f32[2,128,512]{2,1,0:T(8,128)}, f32[2,128,512]{2,1,0:T(8,128)S(1)}, u32[]{:S(2)}, u32[]{:S(2)}) collective-permute-start(f32[2,128,512]{2,1,0:T(8,128)} %get-tuple-element.10), channel_id=1, source_target_pairs={{2,0},{4,2},{6,4},{8,6},{10,8},{12,10},{14,12},{3,1},{5,3},{7,5},{... | collective-permute-start | bytes 1572872 | tf_op jit(solution)/shard_map/ppermute | solution.py:88
  6.2 27.2 %collective-permute-start.1 = (f32[2,128,512]{2,1,0:T(8,128)}, f32[2,128,512]{2,1,0:T(8,128)S(1)}, u32[]{:S(2)}, u32[]{:S(2)}) collective-permute-start(f32[2,128,512]{2,1,0:T(8,128)} %get-tuple-element.11), channel_id=1, source_target_pairs={{0,2},{2,4},{4,6},{6,8},{8,10},{10,12},{12,14},{1,3},{3,5},{5,7},{... | collective-permute-start | bytes 1572872 | tf_op jit(solution)/shard_map/ppermute | solution.py:88
  11.7 21.7 %collective-permute-start.2 = (f32[2,128,512]{2,1,0:T(8,128)}, f32[2,128,512]{2,1,0:T(8,128)S(1)}, u32[]{:S(2)}, u32[]{:S(2)}) collective-permute-start(f32[2,128,512]{2,1,0:T(8,128)} %get-tuple-element.12), channel_id=1, source_target_pairs={{1,0},{3,2},{5,4},{7,6},{9,8},{11,10},{13,12},{15,14},{17,16},{19,... | collective-permute-start | bytes 1572872 | tf_op jit(solution)/shard_map/ppermute | solution.py:88
  13.0 20.4 %collective-permute-start.3 = (f32[2,128,512]{2,1,0:T(8,128)}, f32[2,128,512]{2,1,0:T(8,128)S(1)}, u32[]{:S(2)}, u32[]{:S(2)}) collective-permute-start(f32[2,128,512]{2,1,0:T(8,128)} %get-tuple-element.13), channel_id=1, source_target_pairs={{0,1},{2,3},{4,5},{6,7},{8,9},{10,11},{12,13},{14,15},{16,17},{18,... | collective-permute-start | bytes 1572872 | tf_op jit(solution)/shard_map/ppermute | solution.py:88
  21.9 11.5 %copy-start.1 = (f32[2,128,512]{2,1,0:T(8,128)}, f32[2,128,512]{2,1,0:T(8,128)S(1)}, u32[]{:S(2)}) copy-start(f32[2,128,512]{2,1,0:T(8,128)S(1)} %collective-permute-done.refs_0_) | copy-start | bytes 1572868
  33.4 0.8 copy-start.2
  33.4 1.0 copy-start.3
  33.4 1.1 copy-start.4
  39.4 2.8 %copy-start = (f32[10,128,128]{2,1,0:T(8,128)S(1)}, f32[10,128,128]{2,1,0:T(8,128)}, u32[]{:S(2)}) copy-start(f32[10,128,128]{2,1,0:T(8,128)} %get-tuple-element.14) | copy-start | bytes 1966084
  40.5 1.7 %collective-permute-start.4 = (f32[640,128]{1,0:T(8,128)S(1)}, f32[640,128]{1,0:T(8,128)S(1)}, u32[]{:S(2)}, u32[]{:S(2)}) collective-permute-start(f32[640,128]{1,0:T(8,128)S(1)} %constant_dynamic-slice_fusion.4), channel_id=1, source_target_pairs={{0,1},{1,0},{2,3},{3,2},{4,5},{5,4},{6,7},{7,6},{8,9},{9,8},{10,11... | collective-permute-start | bytes 983048 | tf_op jit(solution)/shard_map/ppermute | solution.py:147
  42.3 6.7 %collective-permute-start.7 = (f32[160,128]{1,0:T(8,128)S(1)}, f32[160,128]{1,0:T(8,128)S(1)}, u32[]{:S(2)}, u32[]{:S(2)}) collective-permute-start(f32[160,128]{1,0:T(8,128)S(1)} %get-tuple-element.22), channel_id=1, source_target_pairs={{0,6},{2,4},{4,2},{6,0},{8,14},{10,12},{12,10},{14,8},{1,7},{3,5},... | collective-permute-start | bytes 245768 | tf_op jit(solution)/shard_map/ppermute | solution.py:147
  45.7 4.7 %collective-permute-start.6 = (f32[160,128]{1,0:T(8,128)S(1)}, f32[160,128]{1,0:T(8,128)S(1)}, u32[]{:S(2)}, u32[]{:S(2)}) collective-permute-start(f32[160,128]{1,0:T(8,128)S(1)} %get-tuple-element.23), channel_id=1, source_target_pairs={{0,4},{2,6},{4,0},{6,2},{8,12},{10,14},{12,8},{14,10},{1,5},{3,7},... | collective-permute-start | bytes 245768 | tf_op jit(solution)/shard_map/ppermute | solution.py:147
  46.2 4.4 %collective-permute-start.5 = (f32[160,128]{1,0:T(8,128)S(1)}, f32[160,128]{1,0:T(8,128)S(1)}, u32[]{:S(2)}, u32[]{:S(2)}) collective-permute-start(f32[160,128]{1,0:T(8,128)S(1)} %get-tuple-element.21), channel_id=1, source_target_pairs={{0,2},{2,0},{4,6},{6,4},{8,10},{10,8},{12,14},{14,12},{1,3},{3,1},... | collective-permute-start | bytes 245768 | tf_op jit(solution)/shard_map/ppermute | solution.py:147
  50.7 5.0 %collective-permute-start.8 = (f32[80,128]{1,0:T(8,128)S(1)}, f32[80,128]{1,0:T(8,128)S(1)}, u32[]{:S(2)}, u32[]{:S(2)}) collective-permute-start(f32[80,128]{1,0:T(8,128)S(1)} %constant_dynamic-slice_fusion), channel_id=1, source_target_pairs={{0,8},{2,10},{4,12},{6,14},{8,0},{10,2},{12,4},{14,6},{1,9},{3,11}... | collective-permute-start | bytes 122888 | tf_op jit(solution)/shard_map/ppermute | solution.py:147
  55.6 5.0 %collective-permute-start.9 = (f32[80,128]{1,0:T(8,128)S(1)}, f32[80,128]{1,0:T(8,128)S(1)}, u32[]{:S(2)}, u32[]{:S(2)}) collective-permute-start(f32[80,128]{1,0:T(8,128)S(1)} %dynamic-slice_add_fusion.1), channel_id=1, source_target_pairs={{0,8},{2,10},{4,12},{6,14},{8,0},{10,2},{12,4},{14,6},{1,9},{3,11}... | collective-permute-start | bytes 122888 | tf_op jit(solution)/shard_map/ppermute | solution.py:154
  60.6 5.4 %collective-permute-start.10 = (f32[160,128]{1,0:T(8,128)S(1)}, f32[160,128]{1,0:T(8,128)S(1)}, u32[]{:S(2)}, u32[]{:S(2)}) collective-permute-start(f32[160,128]{1,0:T(8,128)S(1)} %pad_maximum_fusion.2), channel_id=1, source_target_pairs={{0,6},{2,4},{4,2},{6,0},{8,14},{10,12},{12,10},{14,8},{1,7},{3,5},... | collective-permute-start | bytes 245768 | tf_op jit(solution)/shard_map/ppermute | solution.py:154
  62.9 4.4 %collective-permute-start.11 = (f32[160,128]{1,0:T(8,128)S(1)}, f32[160,128]{1,0:T(8,128)S(1)}, u32[]{:S(2)}, u32[]{:S(2)}) collective-permute-start(f32[160,128]{1,0:T(8,128)S(1)} %pad_maximum_fusion.2), channel_id=1, source_target_pairs={{0,4},{2,6},{4,0},{6,2},{8,12},{10,14},{12,8},{14,10},{1,5},{3,7},... | collective-permute-start | bytes 245768 | tf_op jit(solution)/shard_map/ppermute | solution.py:154
  63.8 4.4 %collective-permute-start.12 = (f32[160,128]{1,0:T(8,128)S(1)}, f32[160,128]{1,0:T(8,128)S(1)}, u32[]{:S(2)}, u32[]{:S(2)}) collective-permute-start(f32[160,128]{1,0:T(8,128)S(1)} %pad_maximum_fusion.2), channel_id=1, source_target_pairs={{0,2},{2,0},{4,6},{6,4},{8,10},{10,8},{12,14},{14,12},{1,3},{3,1},... | collective-permute-start | bytes 245768 | tf_op jit(solution)/shard_map/ppermute | solution.py:154
  68.3 1.7 %collective-permute-start.13 = (f32[640,128]{1,0:T(8,128)S(1)}, f32[640,128]{1,0:T(8,128)S(1)}, u32[]{:S(2)}, u32[]{:S(2)}) collective-permute-start(f32[640,128]{1,0:T(8,128)S(1)} %pad_maximum_fusion.1), channel_id=1, source_target_pairs={{0,1},{1,0},{2,3},{3,2},{4,5},{5,4},{6,7},{7,6},{8,9},{9,8},{10,11... | collective-permute-start | bytes 983048 | tf_op jit(solution)/shard_map/ppermute | solution.py:154

commit v7 on v6

--- a/solution.py
+++ b/solution.py
@@ -208,14 +208,15 @@
             acc_ref[target] = acc_ref[target] + pieces[k][h]
     for i in range(nblk):
         forecast_ref[i * block:(i + 1) * block, :] = acc_ref[i]
-    whole = forecast_ref[...]
-    gram = lax.dot_general(whole, whole, (((0,), (0,)), ((), ())), precision=HI,
-                           preferred_element_type=jnp.float32)
     tiles = width // block
     t = 0
     for a in range(tiles):
+        left = forecast_ref[:, a * block:(a + 1) * block]
+        right = forecast_ref[:, a * block:]
+        band = lax.dot_general(left, right, (((0,), (0,)), ((), ())), precision=HI,
+                               preferred_element_type=jnp.float32)
         for b in range(a, tiles):
-            tiles_ref[t] = gram[a * block:(a + 1) * block, b * block:(b + 1) * block]
+            tiles_ref[t] = band[:, (b - a) * block:(b - a + 1) * block]
             t += 1
 
 

time: 118 us -> 118 us (level)
  no operation moved by 1% of the time
where the time goes in v7:
time: 118 us
  Pallas kernels  56.2 us (48%)
  waiting for transfers between devices  33.4 us (28%)
  starting transfers between devices  24.3 us (21%)
  local copies, waits for them, and re-layouts  2.23 us (2%)
    pallas_call x1, Pallas kernels, factor_solve(): pl.pallas_call(functools.partial(factor_kernel, float(total)), out_shape=...  47.2 us
    ppermute x4, waiting for transfers between devices, shifted(): return lax.ppermute(block, axis, route)  17.2 us
    ppermute x4, starting transfers between devices, shifted(): return lax.ppermute(block, axis, route)  11.2 us
    ppermute x5, waiting for transfers between devices, grouped_sum(): kept = kept + lax.ppermute(sent, axis, route)  8.14 us
    ppermute x5, waiting for transfers between devices, grouped_sum(): got.append(lax.ppermute(flat, axis, route))  7.98 us
    ppermute x5, starting transfers between devices, grouped_sum(): kept = kept + lax.ppermute(sent, axis, route)  6.82 us
    ppermute x5, starting transfers between devices, grouped_sum(): got.append(lax.ppermute(flat, axis, route))  6.26 us
    pallas_call x1, Pallas kernels, land_and_gram(): pl.pallas_call(land_kernel, out_shape=(jax.ShapeDtypeStruct((nblk * block...  4.66 us
  transfers between devices with their start and end apart: 14, of which 12 were waited for; matrix products, arithmetic and copies ran while one was open for 0% of the time, Pallas kernels for 0%

profile of v7, /device:TPU:0, one launch (start us, length us, event | category | flops | bytes accessed | tf_op | source)
XLA Modules:
  0.0 117.9 jit_solution(17878390444251435684)
XLA Ops:
  0.6 4.3 %shard_map.68 = (f32[4,128,512]{2,1,0:T(8,128)}, f32[2,128,512]{2,1,0:T(8,128)}, f32[2,128,512]{2,1,0:T(8,128)}, f32[2,128,512]{2,1,0:T(8,128)}, f32[2,128,512]{2,1,0:T(8,128)}) custom-call(s32[28]{0:T(128)} %rows_ref.1, s32[28]{0:T(128)} %cols_ref.1, bf16[28,128,128]{2,1,0:T(8,128)(2,1)} %jac_ref.1, bf16[4,128,512]{2,1,0:T(8,128)(2,1)} %bitcast.6), custom_call_target="tpu_custom_call" | custom-call | tf_op jit(solution)/shard_map/pallas_call | solution.py:189
  4.9 1.3 %collective-permute-start = (f32[2,128,512]{2,1,0:T(8,128)}, f32[2,128,512]{2,1,0:T(8,128)S(1)}, u32[]{:S(2)}, u32[]{:S(2)}) collective-permute-start(f32[2,128,512]{2,1,0:T(8,128)} %get-tuple-element.10), channel_id=1, source_target_pairs={{2,0},{4,2},{6,4},{8,6},{10,8},{12,10},{14,12},{3,1},{5,3},{7,5},{... | collective-permute-start | bytes 1572872 | tf_op jit(solution)/shard_map/ppermute | solution.py:88
  6.2 5.5 %collective-permute-start.1 = (f32[2,128,512]{2,1,0:T(8,128)}, f32[2,128,512]{2,1,0:T(8,128)S(1)}, u32[]{:S(2)}, u32[]{:S(2)}) collective-permute-start(f32[2,128,512]{2,1,0:T(8,128)} %get-tuple-element.11), channel_id=1, source_target_pairs={{0,2},{2,4},{4,6},{6,8},{8,10},{10,12},{12,14},{1,3},{3,5},{5,7},{... | collective-permute-start | bytes 1572872 | tf_op jit(solution)/shard_map/ppermute | solution.py:88
  11.7 1.3 %collective-permute-start.2 = (f32[2,128,512]{2,1,0:T(8,128)}, f32[2,128,512]{2,1,0:T(8,128)S(1)}, u32[]{:S(2)}, u32[]{:S(2)}) collective-permute-start(f32[2,128,512]{2,1,0:T(8,128)} %get-tuple-element.12), channel_id=1, source_target_pairs={{1,0},{3,2},{5,4},{7,6},{9,8},{11,10},{13,12},{15,14},{17,16},{19,... | collective-permute-start | bytes 1572872 | tf_op jit(solution)/shard_map/ppermute | solution.py:88
  13.0 3.1 %collective-permute-start.3 = (f32[2,128,512]{2,1,0:T(8,128)}, f32[2,128,512]{2,1,0:T(8,128)S(1)}, u32[]{:S(2)}, u32[]{:S(2)}) collective-permute-start(f32[2,128,512]{2,1,0:T(8,128)} %get-tuple-element.13), channel_id=1, source_target_pairs={{0,1},{2,3},{4,5},{6,7},{8,9},{10,11},{12,13},{14,15},{16,17},{18,... | collective-permute-start | bytes 1572872 | tf_op jit(solution)/shard_map/ppermute | solution.py:88
  16.2 5.7 %collective-permute-done.refs_0_ = f32[2,128,512]{2,1,0:T(8,128)S(1)} collective-permute-done((f32[2,128,512]{2,1,0:T(8,128)}, f32[2,128,512]{2,1,0:T(8,128)S(1)}, u32[]{:S(2)}, u32[]{:S(2)}) %collective-permute-start) | collective-permute-done | bytes 524320 | tf_op jit(solution)/shard_map/ppermute | solution.py:88
  21.9 0.0 copy-start.1
  21.9 11.5 %collective-permute-done.1.refs_1_ = f32[2,128,512]{2,1,0:T(8,128)S(1)} collective-permute-done((f32[2,128,512]{2,1,0:T(8,128)}, f32[2,128,512]{2,1,0:T(8,128)S(1)}, u32[]{:S(2)}, u32[]{:S(2)}) %collective-permute-start.1) | collective-permute-done | bytes 524320 | tf_op jit(solution)/shard_map/ppermute | solution.py:88
  33.4 0.0 copy-start.2
  33.4 0.0 collective-permute-done.2.refs_2_
  33.4 0.0 copy-start.3
  33.4 0.0 collective-permute-done.3.refs_3_
  33.4 0.0 copy-start.4
  33.4 0.0 copy-done.1
  33.4 0.8 copy-done.2
  34.2 0.2 copy-done.3
  34.4 0.1 copy-done.4
  34.5 4.7 %shard_map.69 = (f32[512,512]{1,0:T(8,128)}, f32[10,128,128]{2,1,0:T(8,128)}) custom-call(s32[8]{0:T(128)} %landing_ref.1, f32[4,128,512]{2,1,0:T(8,128)} %get-tuple-element.9.base_ref, f32[2,128,512]{2,1,0:T(8,128)} %copy-done.1, f32[2,128,512]{2,1,0:T(8,128)} %copy-done.2, f32[2,128,512]{2,1,0:T(8,128)} %copy-done.3, f32[2,128,512]{2,1,0:T(8,128)} %copy-done.4), custom_call_target="tpu_custom_call" | custom-call | tf_op jit(solution)/shard_map/pallas_call | solution.py:229
  39.2 0.0 copy-start
  39.2 1.1 constant_dynamic-slice_fusion.4
  40.3 0.1 collective-permute-start.4
  40.4 1.6 %collective-permute-done.4 = f32[640,128]{1,0:T(8,128)S(1)} collective-permute-done((f32[640,128]{1,0:T(8,128)S(1)}, f32[640,128]{1,0:T(8,128)S(1)}, u32[]{:S(2)}, u32[]{:S(2)}) %collective-permute-start.4) | collective-permute-done | bytes 327712 | tf_op jit(solution)/shard_map/ppermute | solution.py:147
  42.0 0.0 copy-done
  42.0 3.5 %collective-permute-start.7 = (f32[160,128]{1,0:T(8,128)S(1)}, f32[160,128]{1,0:T(8,128)S(1)}, u32[]{:S(2)}, u32[]{:S(2)}) collective-permute-start(f32[160,128]{1,0:T(8,128)S(1)} %get-tuple-element.22), channel_id=1, source_target_pairs={{0,6},{2,4},{4,2},{6,0},{8,14},{10,12},{12,10},{14,8},{1,7},{3,5},... | collective-permute-start | bytes 245768 | tf_op jit(solution)/shard_map/ppermute | solution.py:147
  45.5 0.4 collective-permute-start.6
  45.9 0.2 collective-permute-start.5
  46.1 2.6 %collective-permute-done.7 = f32[160,128]{1,0:T(8,128)S(1)} collective-permute-done((f32[160,128]{1,0:T(8,128)S(1)}, f32[160,128]{1,0:T(8,128)S(1)}, u32[]{:S(2)}, u32[]{:S(2)}) %collective-permute-start.7) | collective-permute-done | bytes 81952 | tf_op jit(solution)/shard_map/ppermute | solution.py:147
  48.7 1.4 %collective-permute-done.6 = f32[160,128]{1,0:T(8,128)S(1)} collective-permute-done((f32[160,128]{1,0:T(8,128)S(1)}, f32[160,128]{1,0:T(8,128)S(1)}, u32[]{:S(2)}, u32[]{:S(2)}) %collective-permute-start.6) | collective-permute-done | bytes 81952 | tf_op jit(solution)/shard_map/ppermute | solution.py:147
  50.2 0.2 collective-permute-done.5
  50.4 2.6 %collective-permute-start.8 = (f32[80,128]{1,0:T(8,128)S(1)}, f32[80,128]{1,0:T(8,128)S(1)}, u32[]{:S(2)}, u32[]{:S(2)}) collective-permute-start(f32[80,128]{1,0:T(8,128)S(1)} %constant_dynamic-slice_fusion), channel_id=1, source_target_pairs={{0,8},{2,10},{4,12},{6,14},{8,0},{10,2},{12,4},{14,6},{1,9},{3,11}... | collective-permute-start | bytes 122888 | tf_op jit(solution)/shard_map/ppermute | solution.py:147
  53.1 2.3 %collective-permute-done.8 = f32[80,128]{1,0:T(8,128)S(1)} collective-permute-done((f32[80,128]{1,0:T(8,128)S(1)}, f32[80,128]{1,0:T(8,128)S(1)}, u32[]{:S(2)}, u32[]{:S(2)}) %collective-permute-start.8) | collective-permute-done | bytes 40992 | tf_op jit(solution)/shard_map/ppermute | solution.py:147
  55.4 2.6 %collective-permute-start.9 = (f32[80,128]{1,0:T(8,128)S(1)}, f32[80,128]{1,0:T(8,128)S(1)}, u32[]{:S(2)}, u32[]{:S(2)}) collective-permute-start(f32[80,128]{1,0:T(8,128)S(1)} %dynamic-slice_add_fusion.1), channel_id=1, source_target_pairs={{0,8},{2,10},{4,12},{6,14},{8,0},{10,2},{12,4},{14,6},{1,9},{3,11}... | collective-permute-start | bytes 122888 | tf_op jit(solution)/shard_map/ppermute | solution.py:154
  58.0 2.3 %collective-permute-done.9 = f32[80,128]{1,0:T(8,128)S(1)} collective-permute-done((f32[80,128]{1,0:T(8,128)S(1)}, f32[80,128]{1,0:T(8,128)S(1)}, u32[]{:S(2)}, u32[]{:S(2)}) %collective-permute-start.9) | collective-permute-done | bytes 40992 | tf_op jit(solution)/shard_map/ppermute | solution.py:154
  60.4 2.3 %collective-permute-start.10 = (f32[160,128]{1,0:T(8,128)S(1)}, f32[160,128]{1,0:T(8,128)S(1)}, u32[]{:S(2)}, u32[]{:S(2)}) collective-permute-start(f32[160,128]{1,0:T(8,128)S(1)} %pad_maximum_fusion.2), channel_id=1, source_target_pairs={{0,6},{2,4},{4,2},{6,0},{8,14},{10,12},{12,10},{14,8},{1,7},{3,5},... | collective-permute-start | bytes 245768 | tf_op jit(solution)/shard_map/ppermute | solution.py:154
  62.7 0.8 collective-permute-start.11
  63.5 0.4 collective-permute-start.12
  63.9 1.9 %collective-permute-done.10 = f32[160,128]{1,0:T(8,128)S(1)} collective-permute-done((f32[160,128]{1,0:T(8,128)S(1)}, f32[160,128]{1,0:T(8,128)S(1)}, u32[]{:S(2)}, u32[]{:S(2)}) %collective-permute-start.10) | collective-permute-done | bytes 81952 | tf_op jit(solution)/shard_map/ppermute | solution.py:154
  65.8 1.4 %collective-permute-done.11 = f32[160,128]{1,0:T(8,128)S(1)} collective-permute-done((f32[160,128]{1,0:T(8,128)S(1)}, f32[160,128]{1,0:T(8,128)S(1)}, u32[]{:S(2)}, u32[]{:S(2)}) %collective-permute-start.11) | collective-permute-done | bytes 81952 | tf_op jit(solution)/shard_map/ppermute | solution.py:154
  67.1 0.8 collective-permute-done.12
  68.1 0.1 collective-permute-start.13
  68.2 1.6 %collective-permute-done.13 = f32[640,128]{1,0:T(8,128)S(1)} collective-permute-done((f32[640,128]{1,0:T(8,128)S(1)}, f32[640,128]{1,0:T(8,128)S(1)}, u32[]{:S(2)}, u32[]{:S(2)}) %collective-permute-start.13) | collective-permute-done | bytes 327712 | tf_op jit(solution)/shard_map/ppermute | solution.py:154
  69.8 0.9 pad_maximum_fusion
  70.7 47.2 %shard_map.70 = (bf16[512,512]{1,0:T(8,128)(2,1)}, f32[512,512]{1,0:T(8,128)}) custom-call(f32[10,128,128]{2,1,0:T(8,128)} %bitcast.3, f32[512,512]{1,0:T(8,128)} %get-tuple-element.15.f_ref), custom_call_target="tpu_custom_call" | custom-call | tf_op jit(solution)/shard_map/pallas_call | solution.py:72
  (11 shorter events, 0.2 us)
Async XLA Ops:
  4.9 17.0 %collective-permute-start = (f32[2,128,512]{2,1,0:T(8,128)}, f32[2,128,512]{2,1,0:T(8,128)S(1)}, u32[]{:S(2)}, u32[]{:S(2)}) collective-permute-start(f32[2,128,512]{2,1,0:T(8,128)} %get-tuple-element.10), channel_id=1, source_target_pairs={{2,0},{4,2},{6,4},{8,6},{10,8},{12,10},{14,12},{3,1},{5,3},{7,5},{... | collective-permute-start | bytes 1572872 | tf_op jit(solution)/shard_map/ppermute | solution.py:88
  6.2 27.2 %collective-permute-start.1 = (f32[2,128,512]{2,1,0:T(8,128)}, f32[2,128,512]{2,1,0:T(8,128)S(1)}, u32[]{:S(2)}, u32[]{:S(2)}) collective-permute-start(f32[2,128,512]{2,1,0:T(8,128)} %get-tuple-element.11), channel_id=1, source_target_pairs={{0,2},{2,4},{4,6},{6,8},{8,10},{10,12},{12,14},{1,3},{3,5},{5,7},{... | collective-permute-start | bytes 1572872 | tf_op jit(solution)/shard_map/ppermute | solution.py:88
  11.7 21.7 %collective-permute-start.2 = (f32[2,128,512]{2,1,0:T(8,128)}, f32[2,128,512]{2,1,0:T(8,128)S(1)}, u32[]{:S(2)}, u32[]{:S(2)}) collective-permute-start(f32[2,128,512]{2,1,0:T(8,128)} %get-tuple-element.12), channel_id=1, source_target_pairs={{1,0},{3,2},{5,4},{7,6},{9,8},{11,10},{13,12},{15,14},{17,16},{19,... | collective-permute-start | bytes 1572872 | tf_op jit(solution)/shard_map/ppermute | solution.py:88
  13.0 20.4 %collective-permute-start.3 = (f32[2,128,512]{2,1,0:T(8,128)}, f32[2,128,512]{2,1,0:T(8,128)S(1)}, u32[]{:S(2)}, u32[]{:S(2)}) collective-permute-start(f32[2,128,512]{2,1,0:T(8,128)} %get-tuple-element.13), channel_id=1, source_target_pairs={{0,1},{2,3},{4,5},{6,7},{8,9},{10,11},{12,13},{14,15},{16,17},{18,... | collective-permute-start | bytes 1572872 | tf_op jit(solution)/shard_map/ppermute | solution.py:88
  21.9 11.5 %copy-start.1 = (f32[2,128,512]{2,1,0:T(8,128)}, f32[2,128,512]{2,1,0:T(8,128)S(1)}, u32[]{:S(2)}) copy-start(f32[2,128,512]{2,1,0:T(8,128)S(1)} %collective-permute-done.refs_0_) | copy-start | bytes 1572868
  33.4 0.8 copy-start.2
  33.4 1.0 copy-start.3
  33.4 1.1 copy-start.4
  39.2 2.8 %copy-start = (f32[10,128,128]{2,1,0:T(8,128)S(1)}, f32[10,128,128]{2,1,0:T(8,128)}, u32[]{:S(2)}) copy-start(f32[10,128,128]{2,1,0:T(8,128)} %get-tuple-element.14) | copy-start | bytes 1966084
  40.3 1.7 %collective-permute-start.4 = (f32[640,128]{1,0:T(8,128)S(1)}, f32[640,128]{1,0:T(8,128)S(1)}, u32[]{:S(2)}, u32[]{:S(2)}) collective-permute-start(f32[640,128]{1,0:T(8,128)S(1)} %constant_dynamic-slice_fusion.4), channel_id=1, source_target_pairs={{0,1},{1,0},{2,3},{3,2},{4,5},{5,4},{6,7},{7,6},{8,9},{9,8},{10,11... | collective-permute-start | bytes 983048 | tf_op jit(solution)/shard_map/ppermute | solution.py:147
  42.0 6.7 %collective-permute-start.7 = (f32[160,128]{1,0:T(8,128)S(1)}, f32[160,128]{1,0:T(8,128)S(1)}, u32[]{:S(2)}, u32[]{:S(2)}) collective-permute-start(f32[160,128]{1,0:T(8,128)S(1)} %get-tuple-element.22), channel_id=1, source_target_pairs={{0,6},{2,4},{4,2},{6,0},{8,14},{10,12},{12,10},{14,8},{1,7},{3,5},... | collective-permute-start | bytes 245768 | tf_op jit(solution)/shard_map/ppermute | solution.py:147
  45.5 4.7 %collective-permute-start.6 = (f32[160,128]{1,0:T(8,128)S(1)}, f32[160,128]{1,0:T(8,128)S(1)}, u32[]{:S(2)}, u32[]{:S(2)}) collective-permute-start(f32[160,128]{1,0:T(8,128)S(1)} %get-tuple-element.23), channel_id=1, source_target_pairs={{0,4},{2,6},{4,0},{6,2},{8,12},{10,14},{12,8},{14,10},{1,5},{3,7},... | collective-permute-start | bytes 245768 | tf_op jit(solution)/shard_map/ppermute | solution.py:147
  45.9 4.4 %collective-permute-start.5 = (f32[160,128]{1,0:T(8,128)S(1)}, f32[160,128]{1,0:T(8,128)S(1)}, u32[]{:S(2)}, u32[]{:S(2)}) collective-permute-start(f32[160,128]{1,0:T(8,128)S(1)} %get-tuple-element.21), channel_id=1, source_target_pairs={{0,2},{2,0},{4,6},{6,4},{8,10},{10,8},{12,14},{14,12},{1,3},{3,1},... | collective-permute-start | bytes 245768 | tf_op jit(solution)/shard_map/ppermute | solution.py:147
  50.4 5.0 %collective-permute-start.8 = (f32[80,128]{1,0:T(8,128)S(1)}, f32[80,128]{1,0:T(8,128)S(1)}, u32[]{:S(2)}, u32[]{:S(2)}) collective-permute-start(f32[80,128]{1,0:T(8,128)S(1)} %constant_dynamic-slice_fusion), channel_id=1, source_target_pairs={{0,8},{2,10},{4,12},{6,14},{8,0},{10,2},{12,4},{14,6},{1,9},{3,11}... | collective-permute-start | bytes 122888 | tf_op jit(solution)/shard_map/ppermute | solution.py:147
  55.4 5.0 %collective-permute-start.9 = (f32[80,128]{1,0:T(8,128)S(1)}, f32[80,128]{1,0:T(8,128)S(1)}, u32[]{:S(2)}, u32[]{:S(2)}) collective-permute-start(f32[80,128]{1,0:T(8,128)S(1)} %dynamic-slice_add_fusion.1), channel_id=1, source_target_pairs={{0,8},{2,10},{4,12},{6,14},{8,0},{10,2},{12,4},{14,6},{1,9},{3,11}... | collective-permute-start | bytes 122888 | tf_op jit(solution)/shard_map/ppermute | solution.py:154
  60.4 5.4 %collective-permute-start.10 = (f32[160,128]{1,0:T(8,128)S(1)}, f32[160,128]{1,0:T(8,128)S(1)}, u32[]{:S(2)}, u32[]{:S(2)}) collective-permute-start(f32[160,128]{1,0:T(8,128)S(1)} %pad_maximum_fusion.2), channel_id=1, source_target_pairs={{0,6},{2,4},{4,2},{6,0},{8,14},{10,12},{12,10},{14,8},{1,7},{3,5},... | collective-permute-start | bytes 245768 | tf_op jit(solution)/shard_map/ppermute | solution.py:154
  62.7 4.4 %collective-permute-start.11 = (f32[160,128]{1,0:T(8,128)S(1)}, f32[160,128]{1,0:T(8,128)S(1)}, u32[]{:S(2)}, u32[]{:S(2)}) collective-permute-start(f32[160,128]{1,0:T(8,128)S(1)} %pad_maximum_fusion.2), channel_id=1, source_target_pairs={{0,4},{2,6},{4,0},{6,2},{8,12},{10,14},{12,8},{14,10},{1,5},{3,7},... | collective-permute-start | bytes 245768 | tf_op jit(solution)/shard_map/ppermute | solution.py:154
  63.5 4.4 %collective-permute-start.12 = (f32[160,128]{1,0:T(8,128)S(1)}, f32[160,128]{1,0:T(8,128)S(1)}, u32[]{:S(2)}, u32[]{:S(2)}) collective-permute-start(f32[160,128]{1,0:T(8,128)S(1)} %pad_maximum_fusion.2), channel_id=1, source_target_pairs={{0,2},{2,0},{4,6},{6,4},{8,10},{10,8},{12,14},{14,12},{1,3},{3,1},... | collective-permute-start | bytes 245768 | tf_op jit(solution)/shard_map/ppermute | solution.py:154
  68.1 1.7 %collective-permute-start.13 = (f32[640,128]{1,0:T(8,128)S(1)}, f32[640,128]{1,0:T(8,128)S(1)}, u32[]{:S(2)}, u32[]{:S(2)}) collective-permute-start(f32[640,128]{1,0:T(8,128)S(1)} %pad_maximum_fusion.1), channel_id=1, source_target_pairs={{0,1},{1,0},{2,3},{3,2},{4,5},{5,4},{6,7},{7,6},{8,9},{9,8},{10,11... | collective-permute-start | bytes 983048 | tf_op jit(solution)/shard_map/ppermute | solution.py:154

commit v8 on v7

--- a/solution.py
+++ b/solution.py
@@ -19,9 +19,9 @@
         for second in range(first, nb):
             tile = g_ref[t] / total
             w_ref[first * b:(first + 1) * b, second * b:(second + 1) * b] = tile
-            if second > first:
-                w_ref[second * b:(second + 1) * b, first * b:(first + 1) * b] = tile.T
             t += 1
+    for first in range(1, nb):
+        w_ref[first * b:, (first - 1) * b:first * b] = jnp.zeros(((nb - first) * b, b), jnp.float32)
     u_ref[...] = jnp.zeros(u_ref.shape, jnp.float32)
     lane = lax.broadcasted_iota(jnp.int32, (1, b), 1)
     rows = lax.broadcasted_iota(jnp.int32, (b, 1), 0)

time: 118 us -> 118 us (level)
  no operation moved by 1% of the time
where the time goes in v8:
time: 118 us
  Pallas kernels  56.2 us (48%)
  waiting for transfers between devices  33.4 us (28%)
  starting transfers between devices  24.3 us (21%)
  local copies, waits for them, and re-layouts  2.23 us (2%)
    pallas_call x1, Pallas kernels, factor_solve(): pl.pallas_call(functools.partial(factor_kernel, float(total)), out_shape=...  47.2 us
    ppermute x4, waiting for transfers between devices, shifted(): return lax.ppermute(block, axis, route)  17.2 us
    ppermute x4, starting transfers between devices, shifted(): return lax.ppermute(block, axis, route)  11.2 us
    ppermute x5, waiting for transfers between devices, grouped_sum(): kept = kept + lax.ppermute(sent, axis, route)  8.14 us
    ppermute x5, waiting for transfers between devices, grouped_sum(): got.append(lax.ppermute(flat, axis, route))  7.98 us
    ppermute x5, starting transfers between devices, grouped_sum(): kept = kept + lax.ppermute(sent, axis, route)  6.82 us
    ppermute x5, starting transfers between devices, grouped_sum(): got.append(lax.ppermute(flat, axis, route))  6.26 us
    pallas_call x1, Pallas kernels, land_and_gram(): pl.pallas_call(land_kernel, out_shape=(jax.ShapeDtypeStruct((nblk * block...  4.66 us
  transfers between devices with their start and end apart: 14, of which 12 were waited for; matrix products, arithmetic and copies ran while one was open for 0% of the time, Pallas kernels for 0%

profile of v8, /device:TPU:0, one launch (start us, length us, event | category | flops | bytes accessed | tf_op | source)
XLA Modules:
  0.0 117.9 jit_solution(11118091508495073259)
XLA Ops:
  0.6 4.3 %shard_map.68 = (f32[4,128,512]{2,1,0:T(8,128)}, f32[2,128,512]{2,1,0:T(8,128)}, f32[2,128,512]{2,1,0:T(8,128)}, f32[2,128,512]{2,1,0:T(8,128)}, f32[2,128,512]{2,1,0:T(8,128)}) custom-call(s32[28]{0:T(128)} %rows_ref.1, s32[28]{0:T(128)} %cols_ref.1, bf16[28,128,128]{2,1,0:T(8,128)(2,1)} %jac_ref.1, bf16[4,128,512]{2,1,0:T(8,128)(2,1)} %bitcast.6), custom_call_target="tpu_custom_call" | custom-call | tf_op jit(solution)/shard_map/pallas_call | solution.py:189
  4.9 1.3 %collective-permute-start = (f32[2,128,512]{2,1,0:T(8,128)}, f32[2,128,512]{2,1,0:T(8,128)S(1)}, u32[]{:S(2)}, u32[]{:S(2)}) collective-permute-start(f32[2,128,512]{2,1,0:T(8,128)} %get-tuple-element.10), channel_id=1, source_target_pairs={{2,0},{4,2},{6,4},{8,6},{10,8},{12,10},{14,12},{3,1},{5,3},{7,5},{... | collective-permute-start | bytes 1572872 | tf_op jit(solution)/shard_map/ppermute | solution.py:88
  6.2 5.5 %collective-permute-start.1 = (f32[2,128,512]{2,1,0:T(8,128)}, f32[2,128,512]{2,1,0:T(8,128)S(1)}, u32[]{:S(2)}, u32[]{:S(2)}) collective-permute-start(f32[2,128,512]{2,1,0:T(8,128)} %get-tuple-element.11), channel_id=1, source_target_pairs={{0,2},{2,4},{4,6},{6,8},{8,10},{10,12},{12,14},{1,3},{3,5},{5,7},{... | collective-permute-start | bytes 1572872 | tf_op jit(solution)/shard_map/ppermute | solution.py:88
  11.7 1.3 %collective-permute-start.2 = (f32[2,128,512]{2,1,0:T(8,128)}, f32[2,128,512]{2,1,0:T(8,128)S(1)}, u32[]{:S(2)}, u32[]{:S(2)}) collective-permute-start(f32[2,128,512]{2,1,0:T(8,128)} %get-tuple-element.12), channel_id=1, source_target_pairs={{1,0},{3,2},{5,4},{7,6},{9,8},{11,10},{13,12},{15,14},{17,16},{19,... | collective-permute-start | bytes 1572872 | tf_op jit(solution)/shard_map/ppermute | solution.py:88
  13.0 3.1 %collective-permute-start.3 = (f32[2,128,512]{2,1,0:T(8,128)}, f32[2,128,512]{2,1,0:T(8,128)S(1)}, u32[]{:S(2)}, u32[]{:S(2)}) collective-permute-start(f32[2,128,512]{2,1,0:T(8,128)} %get-tuple-element.13), channel_id=1, source_target_pairs={{0,1},{2,3},{4,5},{6,7},{8,9},{10,11},{12,13},{14,15},{16,17},{18,... | collective-permute-start | bytes 1572872 | tf_op jit(solution)/shard_map/ppermute | solution.py:88
  16.2 5.7 %collective-permute-done.refs_0_ = f32[2,128,512]{2,1,0:T(8,128)S(1)} collective-permute-done((f32[2,128,512]{2,1,0:T(8,128)}, f32[2,128,512]{2,1,0:T(8,128)S(1)}, u32[]{:S(2)}, u32[]{:S(2)}) %collective-permute-start) | collective-permute-done | bytes 524320 | tf_op jit(solution)/shard_map/ppermute | solution.py:88
  21.9 0.0 copy-start.1
  21.9 11.5 %collective-permute-done.1.refs_1_ = f32[2,128,512]{2,1,0:T(8,128)S(1)} collective-permute-done((f32[2,128,512]{2,1,0:T(8,128)}, f32[2,128,512]{2,1,0:T(8,128)S(1)}, u32[]{:S(2)}, u32[]{:S(2)}) %collective-permute-start.1) | collective-permute-done | bytes 524320 | tf_op jit(solution)/shard_map/ppermute | solution.py:88
  33.4 0.0 copy-start.2
  33.4 0.0 collective-permute-done.2.refs_2_
  33.4 0.0 copy-start.3
  33.4 0.0 collective-permute-done.3.refs_3_
  33.4 0.0 copy-start.4
  33.4 0.0 copy-done.1
  33.4 0.8 copy-done.2
  34.2 0.2 copy-done.3
  34.4 0.1 copy-done.4
  34.5 4.7 %shard_map.69 = (f32[512,512]{1,0:T(8,128)}, f32[10,128,128]{2,1,0:T(8,128)}) custom-call(s32[8]{0:T(128)} %landing_ref.1, f32[4,128,512]{2,1,0:T(8,128)} %get-tuple-element.9.base_ref, f32[2,128,512]{2,1,0:T(8,128)} %copy-done.1, f32[2,128,512]{2,1,0:T(8,128)} %copy-done.2, f32[2,128,512]{2,1,0:T(8,128)} %copy-done.3, f32[2,128,512]{2,1,0:T(8,128)} %copy-done.4), custom_call_target="tpu_custom_call" | custom-call | tf_op jit(solution)/shard_map/pallas_call | solution.py:229
  39.2 0.0 copy-start
  39.2 1.1 constant_dynamic-slice_fusion.4
  40.3 0.1 collective-permute-start.4
  40.4 1.6 %collective-permute-done.4 = f32[640,128]{1,0:T(8,128)S(1)} collective-permute-done((f32[640,128]{1,0:T(8,128)S(1)}, f32[640,128]{1,0:T(8,128)S(1)}, u32[]{:S(2)}, u32[]{:S(2)}) %collective-permute-start.4) | collective-permute-done | bytes 327712 | tf_op jit(solution)/shard_map/ppermute | solution.py:147
  42.0 0.0 copy-done
  42.0 3.5 %collective-permute-start.7 = (f32[160,128]{1,0:T(8,128)S(1)}, f32[160,128]{1,0:T(8,128)S(1)}, u32[]{:S(2)}, u32[]{:S(2)}) collective-permute-start(f32[160,128]{1,0:T(8,128)S(1)} %get-tuple-element.22), channel_id=1, source_target_pairs={{0,6},{2,4},{4,2},{6,0},{8,14},{10,12},{12,10},{14,8},{1,7},{3,5},... | collective-permute-start | bytes 245768 | tf_op jit(solution)/shard_map/ppermute | solution.py:147
  45.5 0.4 collective-permute-start.6
  45.9 0.2 collective-permute-start.5
  46.1 2.6 %collective-permute-done.7 = f32[160,128]{1,0:T(8,128)S(1)} collective-permute-done((f32[160,128]{1,0:T(8,128)S(1)}, f32[160,128]{1,0:T(8,128)S(1)}, u32[]{:S(2)}, u32[]{:S(2)}) %collective-permute-start.7) | collective-permute-done | bytes 81952 | tf_op jit(solution)/shard_map/ppermute | solution.py:147
  48.7 1.4 %collective-permute-done.6 = f32[160,128]{1,0:T(8,128)S(1)} collective-permute-done((f32[160,128]{1,0:T(8,128)S(1)}, f32[160,128]{1,0:T(8,128)S(1)}, u32[]{:S(2)}, u32[]{:S(2)}) %collective-permute-start.6) | collective-permute-done | bytes 81952 | tf_op jit(solution)/shard_map/ppermute | solution.py:147
  50.2 0.2 collective-permute-done.5
  50.4 2.6 %collective-permute-start.8 = (f32[80,128]{1,0:T(8,128)S(1)}, f32[80,128]{1,0:T(8,128)S(1)}, u32[]{:S(2)}, u32[]{:S(2)}) collective-permute-start(f32[80,128]{1,0:T(8,128)S(1)} %constant_dynamic-slice_fusion), channel_id=1, source_target_pairs={{0,8},{2,10},{4,12},{6,14},{8,0},{10,2},{12,4},{14,6},{1,9},{3,11}... | collective-permute-start | bytes 122888 | tf_op jit(solution)/shard_map/ppermute | solution.py:147
  53.1 2.3 %collective-permute-done.8 = f32[80,128]{1,0:T(8,128)S(1)} collective-permute-done((f32[80,128]{1,0:T(8,128)S(1)}, f32[80,128]{1,0:T(8,128)S(1)}, u32[]{:S(2)}, u32[]{:S(2)}) %collective-permute-start.8) | collective-permute-done | bytes 40992 | tf_op jit(solution)/shard_map/ppermute | solution.py:147
  55.4 2.6 %collective-permute-start.9 = (f32[80,128]{1,0:T(8,128)S(1)}, f32[80,128]{1,0:T(8,128)S(1)}, u32[]{:S(2)}, u32[]{:S(2)}) collective-permute-start(f32[80,128]{1,0:T(8,128)S(1)} %dynamic-slice_add_fusion.1), channel_id=1, source_target_pairs={{0,8},{2,10},{4,12},{6,14},{8,0},{10,2},{12,4},{14,6},{1,9},{3,11}... | collective-permute-start | bytes 122888 | tf_op jit(solution)/shard_map/ppermute | solution.py:154
  58.0 2.3 %collective-permute-done.9 = f32[80,128]{1,0:T(8,128)S(1)} collective-permute-done((f32[80,128]{1,0:T(8,128)S(1)}, f32[80,128]{1,0:T(8,128)S(1)}, u32[]{:S(2)}, u32[]{:S(2)}) %collective-permute-start.9) | collective-permute-done | bytes 40992 | tf_op jit(solution)/shard_map/ppermute | solution.py:154
  60.4 2.3 %collective-permute-start.10 = (f32[160,128]{1,0:T(8,128)S(1)}, f32[160,128]{1,0:T(8,128)S(1)}, u32[]{:S(2)}, u32[]{:S(2)}) collective-permute-start(f32[160,128]{1,0:T(8,128)S(1)} %pad_maximum_fusion.2), channel_id=1, source_target_pairs={{0,6},{2,4},{4,2},{6,0},{8,14},{10,12},{12,10},{14,8},{1,7},{3,5},... | collective-permute-start | bytes 245768 | tf_op jit(solution)/shard_map/ppermute | solution.py:154
  62.7 0.8 collective-permute-start.11
  63.5 0.4 collective-permute-start.12
  63.9 1.9 %collective-permute-done.10 = f32[160,128]{1,0:T(8,128)S(1)} collective-permute-done((f32[160,128]{1,0:T(8,128)S(1)}, f32[160,128]{1,0:T(8,128)S(1)}, u32[]{:S(2)}, u32[]{:S(2)}) %collective-permute-start.10) | collective-permute-done | bytes 81952 | tf_op jit(solution)/shard_map/ppermute | solution.py:154
  65.8 1.4 %collective-permute-done.11 = f32[160,128]{1,0:T(8,128)S(1)} collective-permute-done((f32[160,128]{1,0:T(8,128)S(1)}, f32[160,128]{1,0:T(8,128)S(1)}, u32[]{:S(2)}, u32[]{:S(2)}) %collective-permute-start.11) | collective-permute-done | bytes 81952 | tf_op jit(solution)/shard_map/ppermute | solution.py:154
  67.1 0.8 collective-permute-done.12
  68.1 0.1 collective-permute-start.13
  68.2 1.6 %collective-permute-done.13 = f32[640,128]{1,0:T(8,128)S(1)} collective-permute-done((f32[640,128]{1,0:T(8,128)S(1)}, f32[640,128]{1,0:T(8,128)S(1)}, u32[]{:S(2)}, u32[]{:S(2)}) %collective-permute-start.13) | collective-permute-done | bytes 327712 | tf_op jit(solution)/shard_map/ppermute | solution.py:154
  69.8 0.9 pad_maximum_fusion
  70.7 47.2 %shard_map.70 = (bf16[512,512]{1,0:T(8,128)(2,1)}, f32[512,512]{1,0:T(8,128)}) custom-call(f32[10,128,128]{2,1,0:T(8,128)} %bitcast.3, f32[512,512]{1,0:T(8,128)} %get-tuple-element.15.f_ref), custom_call_target="tpu_custom_call" | custom-call | tf_op jit(solution)/shard_map/pallas_call | solution.py:72
  (11 shorter events, 0.2 us)
Async XLA Ops:
  4.9 17.0 %collective-permute-start = (f32[2,128,512]{2,1,0:T(8,128)}, f32[2,128,512]{2,1,0:T(8,128)S(1)}, u32[]{:S(2)}, u32[]{:S(2)}) collective-permute-start(f32[2,128,512]{2,1,0:T(8,128)} %get-tuple-element.10), channel_id=1, source_target_pairs={{2,0},{4,2},{6,4},{8,6},{10,8},{12,10},{14,12},{3,1},{5,3},{7,5},{... | collective-permute-start | bytes 1572872 | tf_op jit(solution)/shard_map/ppermute | solution.py:88
  6.2 27.2 %collective-permute-start.1 = (f32[2,128,512]{2,1,0:T(8,128)}, f32[2,128,512]{2,1,0:T(8,128)S(1)}, u32[]{:S(2)}, u32[]{:S(2)}) collective-permute-start(f32[2,128,512]{2,1,0:T(8,128)} %get-tuple-element.11), channel_id=1, source_target_pairs={{0,2},{2,4},{4,6},{6,8},{8,10},{10,12},{12,14},{1,3},{3,5},{5,7},{... | collective-permute-start | bytes 1572872 | tf_op jit(solution)/shard_map/ppermute | solution.py:88
  11.7 21.7 %collective-permute-start.2 = (f32[2,128,512]{2,1,0:T(8,128)}, f32[2,128,512]{2,1,0:T(8,128)S(1)}, u32[]{:S(2)}, u32[]{:S(2)}) collective-permute-start(f32[2,128,512]{2,1,0:T(8,128)} %get-tuple-element.12), channel_id=1, source_target_pairs={{1,0},{3,2},{5,4},{7,6},{9,8},{11,10},{13,12},{15,14},{17,16},{19,... | collective-permute-start | bytes 1572872 | tf_op jit(solution)/shard_map/ppermute | solution.py:88
  13.0 20.4 %collective-permute-start.3 = (f32[2,128,512]{2,1,0:T(8,128)}, f32[2,128,512]{2,1,0:T(8,128)S(1)}, u32[]{:S(2)}, u32[]{:S(2)}) collective-permute-start(f32[2,128,512]{2,1,0:T(8,128)} %get-tuple-element.13), channel_id=1, source_target_pairs={{0,1},{2,3},{4,5},{6,7},{8,9},{10,11},{12,13},{14,15},{16,17},{18,... | collective-permute-start | bytes 1572872 | tf_op jit(solution)/shard_map/ppermute | solution.py:88
  21.9 11.5 %copy-start.1 = (f32[2,128,512]{2,1,0:T(8,128)}, f32[2,128,512]{2,1,0:T(8,128)S(1)}, u32[]{:S(2)}) copy-start(f32[2,128,512]{2,1,0:T(8,128)S(1)} %collective-permute-done.refs_0_) | copy-start | bytes 1572868
  33.4 0.8 copy-start.2
  33.4 1.0 copy-start.3
  33.4 1.1 copy-start.4
  39.2 2.8 %copy-start = (f32[10,128,128]{2,1,0:T(8,128)S(1)}, f32[10,128,128]{2,1,0:T(8,128)}, u32[]{:S(2)}) copy-start(f32[10,128,128]{2,1,0:T(8,128)} %get-tuple-element.14) | copy-start | bytes 1966084
  40.3 1.7 %collective-permute-start.4 = (f32[640,128]{1,0:T(8,128)S(1)}, f32[640,128]{1,0:T(8,128)S(1)}, u32[]{:S(2)}, u32[]{:S(2)}) collective-permute-start(f32[640,128]{1,0:T(8,128)S(1)} %constant_dynamic-slice_fusion.4), channel_id=1, source_target_pairs={{0,1},{1,0},{2,3},{3,2},{4,5},{5,4},{6,7},{7,6},{8,9},{9,8},{10,11... | collective-permute-start | bytes 983048 | tf_op jit(solution)/shard_map/ppermute | solution.py:147
  42.0 6.7 %collective-permute-start.7 = (f32[160,128]{1,0:T(8,128)S(1)}, f32[160,128]{1,0:T(8,128)S(1)}, u32[]{:S(2)}, u32[]{:S(2)}) collective-permute-start(f32[160,128]{1,0:T(8,128)S(1)} %get-tuple-element.22), channel_id=1, source_target_pairs={{0,6},{2,4},{4,2},{6,0},{8,14},{10,12},{12,10},{14,8},{1,7},{3,5},... | collective-permute-start | bytes 245768 | tf_op jit(solution)/shard_map/ppermute | solution.py:147
  45.5 4.7 %collective-permute-start.6 = (f32[160,128]{1,0:T(8,128)S(1)}, f32[160,128]{1,0:T(8,128)S(1)}, u32[]{:S(2)}, u32[]{:S(2)}) collective-permute-start(f32[160,128]{1,0:T(8,128)S(1)} %get-tuple-element.23), channel_id=1, source_target_pairs={{0,4},{2,6},{4,0},{6,2},{8,12},{10,14},{12,8},{14,10},{1,5},{3,7},... | collective-permute-start | bytes 245768 | tf_op jit(solution)/shard_map/ppermute | solution.py:147
  45.9 4.4 %collective-permute-start.5 = (f32[160,128]{1,0:T(8,128)S(1)}, f32[160,128]{1,0:T(8,128)S(1)}, u32[]{:S(2)}, u32[]{:S(2)}) collective-permute-start(f32[160,128]{1,0:T(8,128)S(1)} %get-tuple-element.21), channel_id=1, source_target_pairs={{0,2},{2,0},{4,6},{6,4},{8,10},{10,8},{12,14},{14,12},{1,3},{3,1},... | collective-permute-start | bytes 245768 | tf_op jit(solution)/shard_map/ppermute | solution.py:147
  50.4 5.0 %collective-permute-start.8 = (f32[80,128]{1,0:T(8,128)S(1)}, f32[80,128]{1,0:T(8,128)S(1)}, u32[]{:S(2)}, u32[]{:S(2)}) collective-permute-start(f32[80,128]{1,0:T(8,128)S(1)} %constant_dynamic-slice_fusion), channel_id=1, source_target_pairs={{0,8},{2,10},{4,12},{6,14},{8,0},{10,2},{12,4},{14,6},{1,9},{3,11}... | collective-permute-start | bytes 122888 | tf_op jit(solution)/shard_map/ppermute | solution.py:147
  55.4 5.0 %collective-permute-start.9 = (f32[80,128]{1,0:T(8,128)S(1)}, f32[80,128]{1,0:T(8,128)S(1)}, u32[]{:S(2)}, u32[]{:S(2)}) collective-permute-start(f32[80,128]{1,0:T(8,128)S(1)} %dynamic-slice_add_fusion.1), channel_id=1, source_target_pairs={{0,8},{2,10},{4,12},{6,14},{8,0},{10,2},{12,4},{14,6},{1,9},{3,11}... | collective-permute-start | bytes 122888 | tf_op jit(solution)/shard_map/ppermute | solution.py:154
  60.4 5.4 %collective-permute-start.10 = (f32[160,128]{1,0:T(8,128)S(1)}, f32[160,128]{1,0:T(8,128)S(1)}, u32[]{:S(2)}, u32[]{:S(2)}) collective-permute-start(f32[160,128]{1,0:T(8,128)S(1)} %pad_maximum_fusion.2), channel_id=1, source_target_pairs={{0,6},{2,4},{4,2},{6,0},{8,14},{10,12},{12,10},{14,8},{1,7},{3,5},... | collective-permute-start | bytes 245768 | tf_op jit(solution)/shard_map/ppermute | solution.py:154
  62.7 4.4 %collective-permute-start.11 = (f32[160,128]{1,0:T(8,128)S(1)}, f32[160,128]{1,0:T(8,128)S(1)}, u32[]{:S(2)}, u32[]{:S(2)}) collective-permute-start(f32[160,128]{1,0:T(8,128)S(1)} %pad_maximum_fusion.2), channel_id=1, source_target_pairs={{0,4},{2,6},{4,0},{6,2},{8,12},{10,14},{12,8},{14,10},{1,5},{3,7},... | collective-permute-start | bytes 245768 | tf_op jit(solution)/shard_map/ppermute | solution.py:154
  63.5 4.4 %collective-permute-start.12 = (f32[160,128]{1,0:T(8,128)S(1)}, f32[160,128]{1,0:T(8,128)S(1)}, u32[]{:S(2)}, u32[]{:S(2)}) collective-permute-start(f32[160,128]{1,0:T(8,128)S(1)} %pad_maximum_fusion.2), channel_id=1, source_target_pairs={{0,2},{2,0},{4,6},{6,4},{8,10},{10,8},{12,14},{14,12},{1,3},{3,1},... | collective-permute-start | bytes 245768 | tf_op jit(solution)/shard_map/ppermute | solution.py:154
  68.1 1.7 %collective-permute-start.13 = (f32[640,128]{1,0:T(8,128)S(1)}, f32[640,128]{1,0:T(8,128)S(1)}, u32[]{:S(2)}, u32[]{:S(2)}) collective-permute-start(f32[640,128]{1,0:T(8,128)S(1)} %pad_maximum_fusion.1), channel_id=1, source_target_pairs={{0,1},{1,0},{2,3},{3,2},{4,5},{5,4},{6,7},{7,6},{8,9},{9,8},{10,11... | collective-permute-start | bytes 983048 | tf_op jit(solution)/shard_map/ppermute | solution.py:154

commit v9 on v7

--- a/solution.py
+++ b/solution.py
@@ -127,7 +127,7 @@
     return levels
 
 
-def grouped_sum(flat):
+def grouped_sum(flat, rolled=False):
     levels = group_levels()
     if levels is None:
         return doubling_sum(doubling_sum(flat, "tx"), "ty")
@@ -140,6 +140,11 @@
     for axis, size, stride, group in levels:
         digit = lax.axis_index(axis) // stride % group
         chunk = flat.shape[0] // group
+        if rolled and not digits:
+            kept = flat[:chunk] + lax.ppermute(flat[chunk:], axis, [(i, i ^ stride) for i in range(size)])
+            flat = kept
+            digits.append(digit)
+            continue
         kept = lax.dynamic_slice_in_dim(flat, digit * chunk, chunk)
         for offset in range(1, group):
             route = [(i, i ^ (offset * stride)) for i in range(size)]
@@ -196,7 +201,7 @@
     )(jac_rows, jac_cols, jac_blocks, root_blocks)
 
 
-def land_kernel(landing_ref, base_ref, *refs):
+def land_kernel(landing_ref, shift_ref, base_ref, *refs):
     pieces = refs[:4]
     forecast_ref, tiles_ref, acc_ref = refs[4:]
     nblk, block, width = base_ref.shape
@@ -216,11 +221,11 @@
         band = lax.dot_general(left, right, (((0,), (0,)), ((), ())), precision=HI,
                                preferred_element_type=jnp.float32)
         for b in range(a, tiles):
-            tiles_ref[t] = band[:, (b - a) * block:(b - a + 1) * block]
+            tiles_ref[(t + shift_ref[0]) % tiles_ref.shape[0]] = band[:, (b - a) * block:(b - a + 1) * block]
             t += 1
 
 
-def land_and_gram(landing, base, pieces):
+def land_and_gram(landing, shift, base, pieces):
     nblk, block, width = base.shape
     tiles = width // block
     count = tiles * (tiles + 1) // 2
@@ -232,10 +237,10 @@
             jax.ShapeDtypeStruct((nblk * block, width), jnp.float32),
             jax.ShapeDtypeStruct((count, block, block), jnp.float32),
         ),
-        in_specs=[smem, vmem] + [vmem] * len(pieces),
+        in_specs=[smem, smem, vmem] + [vmem] * len(pieces),
         out_specs=(vmem, vmem),
         scratch_shapes=[pltpu.VMEM((nblk, block, width), jnp.float32)],
-    )(landing, base, *pieces)
+    )(landing, shift, base, *pieces)
 
 def per_device(jac_blocks, jac_rows, jac_cols, landing, covariance_root):
     nnz, block, _ = jac_blocks.shape
@@ -250,11 +255,17 @@
     from_prev_x = shifted(to_next_x, "tx", 1)
     from_next_y = shifted(to_prev_y, "ty", -1)
     from_prev_y = shifted(to_next_y, "ty", 1)
+    tiles = mode_columns // block
+    count = tiles * (tiles + 1) // 2
+    levels = group_levels()
+    rolled = bool(levels) and levels[0][0] == "ty" and levels[0][3] == 2 and count % 2 == 0
+    shift = lax.axis_index("ty") * (count // 2) if rolled else 0
+    shift = jnp.full((1,), shift, jnp.int32)
     predicted_root, local_tiles = land_and_gram(
-        landing, base, [from_next_x, from_prev_x, from_next_y, from_prev_y])
+        landing, shift, base, [from_next_x, from_prev_x, from_next_y, from_prev_y])
     total_rows = state_rows * lax.axis_size("tx") * lax.axis_size("ty")
     tiles = mode_columns // block
-    upper_sum = grouped_sum(local_tiles.reshape(-1, block)).reshape(local_tiles.shape)
+    upper_sum = grouped_sum(local_tiles.reshape(-1, block), rolled).reshape(local_tiles.shape)
     rescaled_orthogonal_root, r_factor = factor_solve(upper_sum, predicted_root, total_rows, block)
     return (rescaled_orthogonal_root, r_factor)
 

time: 118 us -> 118 us (level)
    ppermute x0 -> x1, waiting for transfers between devices: none -> 1.58 us  [grouped_sum(): lax.ppermute(flat[chunk:], axis, [(i, i ^ stride) for i in range(size)])]
    ppermute x5 -> x4, waiting for transfers between devices: 8.14 us -> 6.56 us  [grouped_sum(): kept = kept + lax.ppermute(sent, axis, route)]
    ppermute x5 -> x4, starting transfers between devices: 6.82 us -> 6.74 us  [grouped_sum(): kept = kept + lax.ppermute(sent, axis, route)]
where the time goes in v9:
time: 118 us
  Pallas kernels  56.2 us (48%)
  waiting for transfers between devices  33.4 us (28%)
  starting transfers between devices  24.3 us (21%)
  local copies, waits for them, and re-layouts  2.28 us (2%)
    pallas_call x1, Pallas kernels, factor_solve(): pl.pallas_call(functools.partial(factor_kernel, float(total)), out_shape=...  47.2 us
    ppermute x4, waiting for transfers between devices, shifted(): return lax.ppermute(block, axis, route)  17.3 us
    ppermute x4, starting transfers between devices, shifted(): return lax.ppermute(block, axis, route)  11.2 us
    ppermute x5, waiting for transfers between devices, grouped_sum(): got.append(lax.ppermute(flat, axis, route))  7.97 us
    ppermute x4, starting transfers between devices, grouped_sum(): kept = kept + lax.ppermute(sent, axis, route)  6.74 us
    ppermute x4, waiting for transfers between devices, grouped_sum(): kept = kept + lax.ppermute(sent, axis, route)  6.56 us
    ppermute x5, starting transfers between devices, grouped_sum(): got.append(lax.ppermute(flat, axis, route))  6.27 us
    pallas_call x1, Pallas kernels, land_and_gram(): pl.pallas_call(land_kernel, out_shape=(jax.ShapeDtypeStruct((nblk * block...  4.68 us
  transfers between devices with their start and end apart: 14, of which 12 were waited for; matrix products, arithmetic and copies ran while one was open for 0% of the time, Pallas kernels for 0%

profile of v9, /device:TPU:0, one launch (start us, length us, event | category | flops | bytes accessed | tf_op | source)
XLA Modules:
  0.0 118.0 jit_solution(12307570810745070355)
XLA Ops:
  0.6 4.3 %shard_map.68 = (f32[4,128,512]{2,1,0:T(8,128)}, f32[2,128,512]{2,1,0:T(8,128)}, f32[2,128,512]{2,1,0:T(8,128)}, f32[2,128,512]{2,1,0:T(8,128)}, f32[2,128,512]{2,1,0:T(8,128)}) custom-call(s32[28]{0:T(128)} %rows_ref.1, s32[28]{0:T(128)} %cols_ref.1, bf16[28,128,128]{2,1,0:T(8,128)(2,1)} %jac_ref.1, bf16[4,128,512]{2,1,0:T(8,128)(2,1)} %bitcast.7), custom_call_target="tpu_custom_call" | custom-call | tf_op jit(solution)/shard_map/pallas_call | solution.py:194
  4.9 1.3 %collective-permute-start = (f32[2,128,512]{2,1,0:T(8,128)}, f32[2,128,512]{2,1,0:T(8,128)S(1)}, u32[]{:S(2)}, u32[]{:S(2)}) collective-permute-start(f32[2,128,512]{2,1,0:T(8,128)} %get-tuple-element.10), channel_id=1, source_target_pairs={{2,0},{4,2},{6,4},{8,6},{10,8},{12,10},{14,12},{3,1},{5,3},{7,5},{... | collective-permute-start | bytes 1572872 | tf_op jit(solution)/shard_map/ppermute | solution.py:88
  6.2 5.5 %collective-permute-start.1 = (f32[2,128,512]{2,1,0:T(8,128)}, f32[2,128,512]{2,1,0:T(8,128)S(1)}, u32[]{:S(2)}, u32[]{:S(2)}) collective-permute-start(f32[2,128,512]{2,1,0:T(8,128)} %get-tuple-element.11), channel_id=1, source_target_pairs={{0,2},{2,4},{4,6},{6,8},{8,10},{10,12},{12,14},{1,3},{3,5},{5,7},{... | collective-permute-start | bytes 1572872 | tf_op jit(solution)/shard_map/ppermute | solution.py:88
  11.7 1.3 %collective-permute-start.2 = (f32[2,128,512]{2,1,0:T(8,128)}, f32[2,128,512]{2,1,0:T(8,128)S(1)}, u32[]{:S(2)}, u32[]{:S(2)}) collective-permute-start(f32[2,128,512]{2,1,0:T(8,128)} %get-tuple-element.12), channel_id=1, source_target_pairs={{1,0},{3,2},{5,4},{7,6},{9,8},{11,10},{13,12},{15,14},{17,16},{19,... | collective-permute-start | bytes 1572872 | tf_op jit(solution)/shard_map/ppermute | solution.py:88
  13.0 3.1 %collective-permute-start.3 = (f32[2,128,512]{2,1,0:T(8,128)}, f32[2,128,512]{2,1,0:T(8,128)S(1)}, u32[]{:S(2)}, u32[]{:S(2)}) collective-permute-start(f32[2,128,512]{2,1,0:T(8,128)} %get-tuple-element.13), channel_id=1, source_target_pairs={{0,1},{2,3},{4,5},{6,7},{8,9},{10,11},{12,13},{14,15},{16,17},{18,... | collective-permute-start | bytes 1572872 | tf_op jit(solution)/shard_map/ppermute | solution.py:88
  16.1 5.8 %collective-permute-done.refs_0_ = f32[2,128,512]{2,1,0:T(8,128)S(1)} collective-permute-done((f32[2,128,512]{2,1,0:T(8,128)}, f32[2,128,512]{2,1,0:T(8,128)S(1)}, u32[]{:S(2)}, u32[]{:S(2)}) %collective-permute-start) | collective-permute-done | bytes 524320 | tf_op jit(solution)/shard_map/ppermute | solution.py:88
  21.9 0.0 copy-start
  21.9 11.5 %collective-permute-done.1.refs_1_ = f32[2,128,512]{2,1,0:T(8,128)S(1)} collective-permute-done((f32[2,128,512]{2,1,0:T(8,128)}, f32[2,128,512]{2,1,0:T(8,128)S(1)}, u32[]{:S(2)}, u32[]{:S(2)}) %collective-permute-start.1) | collective-permute-done | bytes 524320 | tf_op jit(solution)/shard_map/ppermute | solution.py:88
  33.4 0.0 copy-start.1
  33.4 0.0 collective-permute-done.2.refs_2_
  33.4 0.0 copy-start.2
  33.4 0.0 collective-permute-done.3.refs_3_
  33.4 0.0 copy-start.3
  33.4 0.0 copy-done
  33.4 0.8 copy-done.1
  34.2 0.2 copy-done.2
  34.4 0.1 copy-done.3
  34.5 4.7 %shard_map.69 = (f32[512,512]{1,0:T(8,128)}, f32[10,128,128]{2,1,0:T(8,128)}) custom-call(s32[8]{0:T(128)} %landing_ref.1, s32[1]{0:T(128)} %bitcast.shift_ref, f32[4,128,512]{2,1,0:T(8,128)} %get-tuple-element.9.base_ref, f32[2,128,512]{2,1,0:T(8,128)} %copy-done, f32[2,128,512]{2,1,0:T(8,128)} %copy-done.1, f32[2,128,512]{2,1,0:T(8,128)} %copy-done.2, ...), custom_call_target="tpu_custom_call" | custom-call | tf_op jit(solution)/shard_map/pallas_call | solution.py:234
  39.2 1.1 fusion
  40.3 0.1 collective-permute-start.4
  40.5 1.6 %collective-permute-done.4 = f32[640,128]{1,0:T(8,128)S(1)} collective-permute-done((f32[640,128]{1,0:T(8,128)S(1)}, f32[640,128]{1,0:T(8,128)S(1)}, u32[]{:S(2)}, u32[]{:S(2)}) %collective-permute-start.4) | collective-permute-done | bytes 327712 | tf_op jit(solution)/shard_map/ppermute | solution.py:144
  42.1 3.5 %collective-permute-start.7 = (f32[160,128]{1,0:T(8,128)S(1)}, f32[160,128]{1,0:T(8,128)S(1)}, u32[]{:S(2)}, u32[]{:S(2)}) collective-permute-start(f32[160,128]{1,0:T(8,128)S(1)} %get-tuple-element.24), channel_id=1, source_target_pairs={{0,6},{2,4},{4,2},{6,0},{8,14},{10,12},{12,10},{14,8},{1,7},{3,5},... | collective-permute-start | bytes 245768 | tf_op jit(solution)/shard_map/ppermute | solution.py:152
  45.6 0.4 collective-permute-start.6
  46.0 0.2 collective-permute-start.5
  46.2 2.6 %collective-permute-done.7 = f32[160,128]{1,0:T(8,128)S(1)} collective-permute-done((f32[160,128]{1,0:T(8,128)S(1)}, f32[160,128]{1,0:T(8,128)S(1)}, u32[]{:S(2)}, u32[]{:S(2)}) %collective-permute-start.7) | collective-permute-done | bytes 81952 | tf_op jit(solution)/shard_map/ppermute | solution.py:152
  48.8 1.4 %collective-permute-done.6 = f32[160,128]{1,0:T(8,128)S(1)} collective-permute-done((f32[160,128]{1,0:T(8,128)S(1)}, f32[160,128]{1,0:T(8,128)S(1)}, u32[]{:S(2)}, u32[]{:S(2)}) %collective-permute-start.6) | collective-permute-done | bytes 81952 | tf_op jit(solution)/shard_map/ppermute | solution.py:152
  50.2 0.2 collective-permute-done.5
  50.5 2.6 %collective-permute-start.8 = (f32[80,128]{1,0:T(8,128)S(1)}, f32[80,128]{1,0:T(8,128)S(1)}, u32[]{:S(2)}, u32[]{:S(2)}) collective-permute-start(f32[80,128]{1,0:T(8,128)S(1)} %constant_dynamic-slice_fusion), channel_id=1, source_target_pairs={{0,8},{2,10},{4,12},{6,14},{8,0},{10,2},{12,4},{14,6},{1,9},{3,11}... | collective-permute-start | bytes 122888 | tf_op jit(solution)/shard_map/ppermute | solution.py:152
  53.1 2.3 %collective-permute-done.8 = f32[80,128]{1,0:T(8,128)S(1)} collective-permute-done((f32[80,128]{1,0:T(8,128)S(1)}, f32[80,128]{1,0:T(8,128)S(1)}, u32[]{:S(2)}, u32[]{:S(2)}) %collective-permute-start.8) | collective-permute-done | bytes 40992 | tf_op jit(solution)/shard_map/ppermute | solution.py:152
  55.5 2.6 %collective-permute-start.9 = (f32[80,128]{1,0:T(8,128)S(1)}, f32[80,128]{1,0:T(8,128)S(1)}, u32[]{:S(2)}, u32[]{:S(2)}) collective-permute-start(f32[80,128]{1,0:T(8,128)S(1)} %dynamic-slice_add_fusion), channel_id=1, source_target_pairs={{0,8},{2,10},{4,12},{6,14},{8,0},{10,2},{12,4},{14,6},{1,9},{3,11}... | collective-permute-start | bytes 122888 | tf_op jit(solution)/shard_map/ppermute | solution.py:159
  58.1 2.3 %collective-permute-done.9 = f32[80,128]{1,0:T(8,128)S(1)} collective-permute-done((f32[80,128]{1,0:T(8,128)S(1)}, f32[80,128]{1,0:T(8,128)S(1)}, u32[]{:S(2)}, u32[]{:S(2)}) %collective-permute-start.9) | collective-permute-done | bytes 40992 | tf_op jit(solution)/shard_map/ppermute | solution.py:159
  60.5 2.3 %collective-permute-start.10 = (f32[160,128]{1,0:T(8,128)S(1)}, f32[160,128]{1,0:T(8,128)S(1)}, u32[]{:S(2)}, u32[]{:S(2)}) collective-permute-start(f32[160,128]{1,0:T(8,128)S(1)} %pad_maximum_fusion.2), channel_id=1, source_target_pairs={{0,6},{2,4},{4,2},{6,0},{8,14},{10,12},{12,10},{14,8},{1,7},{3,5},... | collective-permute-start | bytes 245768 | tf_op jit(solution)/shard_map/ppermute | solution.py:159
  62.8 0.8 collective-permute-start.11
  63.6 0.4 collective-permute-start.12
  64.0 1.9 %collective-permute-done.10 = f32[160,128]{1,0:T(8,128)S(1)} collective-permute-done((f32[160,128]{1,0:T(8,128)S(1)}, f32[160,128]{1,0:T(8,128)S(1)}, u32[]{:S(2)}, u32[]{:S(2)}) %collective-permute-start.10) | collective-permute-done | bytes 81952 | tf_op jit(solution)/shard_map/ppermute | solution.py:159
  65.9 1.4 %collective-permute-done.11 = f32[160,128]{1,0:T(8,128)S(1)} collective-permute-done((f32[160,128]{1,0:T(8,128)S(1)}, f32[160,128]{1,0:T(8,128)S(1)}, u32[]{:S(2)}, u32[]{:S(2)}) %collective-permute-start.11) | collective-permute-done | bytes 81952 | tf_op jit(solution)/shard_map/ppermute | solution.py:159
  67.2 0.8 collective-permute-done.12
  68.2 0.1 collective-permute-start.13
  68.2 1.6 %collective-permute-done.13 = f32[640,128]{1,0:T(8,128)S(1)} collective-permute-done((f32[640,128]{1,0:T(8,128)S(1)}, f32[640,128]{1,0:T(8,128)S(1)}, u32[]{:S(2)}, u32[]{:S(2)}) %collective-permute-start.13) | collective-permute-done | bytes 327712 | tf_op jit(solution)/shard_map/ppermute | solution.py:159
  69.9 0.9 pad_maximum_fusion
  70.8 47.2 %shard_map.70 = (bf16[512,512]{1,0:T(8,128)(2,1)}, f32[512,512]{1,0:T(8,128)}) custom-call(f32[10,128,128]{2,1,0:T(8,128)} %bitcast.6, f32[512,512]{1,0:T(8,128)} %get-tuple-element.15.f_ref), custom_call_target="tpu_custom_call" | custom-call | tf_op jit(solution)/shard_map/pallas_call | solution.py:72
  (11 shorter events, 0.2 us)
Async XLA Ops:
  4.9 17.0 %collective-permute-start = (f32[2,128,512]{2,1,0:T(8,128)}, f32[2,128,512]{2,1,0:T(8,128)S(1)}, u32[]{:S(2)}, u32[]{:S(2)}) collective-permute-start(f32[2,128,512]{2,1,0:T(8,128)} %get-tuple-element.10), channel_id=1, source_target_pairs={{2,0},{4,2},{6,4},{8,6},{10,8},{12,10},{14,12},{3,1},{5,3},{7,5},{... | collective-permute-start | bytes 1572872 | tf_op jit(solution)/shard_map/ppermute | solution.py:88
  6.2 27.2 %collective-permute-start.1 = (f32[2,128,512]{2,1,0:T(8,128)}, f32[2,128,512]{2,1,0:T(8,128)S(1)}, u32[]{:S(2)}, u32[]{:S(2)}) collective-permute-start(f32[2,128,512]{2,1,0:T(8,128)} %get-tuple-element.11), channel_id=1, source_target_pairs={{0,2},{2,4},{4,6},{6,8},{8,10},{10,12},{12,14},{1,3},{3,5},{5,7},{... | collective-permute-start | bytes 1572872 | tf_op jit(solution)/shard_map/ppermute | solution.py:88
  11.7 21.7 %collective-permute-start.2 = (f32[2,128,512]{2,1,0:T(8,128)}, f32[2,128,512]{2,1,0:T(8,128)S(1)}, u32[]{:S(2)}, u32[]{:S(2)}) collective-permute-start(f32[2,128,512]{2,1,0:T(8,128)} %get-tuple-element.12), channel_id=1, source_target_pairs={{1,0},{3,2},{5,4},{7,6},{9,8},{11,10},{13,12},{15,14},{17,16},{19,... | collective-permute-start | bytes 1572872 | tf_op jit(solution)/shard_map/ppermute | solution.py:88
  13.0 20.4 %collective-permute-start.3 = (f32[2,128,512]{2,1,0:T(8,128)}, f32[2,128,512]{2,1,0:T(8,128)S(1)}, u32[]{:S(2)}, u32[]{:S(2)}) collective-permute-start(f32[2,128,512]{2,1,0:T(8,128)} %get-tuple-element.13), channel_id=1, source_target_pairs={{0,1},{2,3},{4,5},{6,7},{8,9},{10,11},{12,13},{14,15},{16,17},{18,... | collective-permute-start | bytes 1572872 | tf_op jit(solution)/shard_map/ppermute | solution.py:88
  21.9 11.5 %copy-start = (f32[2,128,512]{2,1,0:T(8,128)}, f32[2,128,512]{2,1,0:T(8,128)S(1)}, u32[]{:S(2)}) copy-start(f32[2,128,512]{2,1,0:T(8,128)S(1)} %collective-permute-done.refs_0_) | copy-start | bytes 1572868
  33.4 0.8 copy-start.1
  33.4 1.0 copy-start.2
  33.4 1.1 copy-start.3
  40.3 1.7 %collective-permute-start.4 = (f32[640,128]{1,0:T(8,128)S(1)}, f32[640,128]{1,0:T(8,128)S(1)}, u32[]{:S(2)}, u32[]{:S(2)}) collective-permute-start(f32[640,128]{1,0:T(8,128)S(1)} %bitcast.8), channel_id=1, source_target_pairs={{0,1},{1,0},{2,3},{3,2},{4,5},{5,4},{6,7},{7,6},{8,9},{9,8},{10,11... | collective-permute-start | bytes 983048 | tf_op jit(solution)/shard_map/ppermute | solution.py:144
  42.1 6.7 %collective-permute-start.7 = (f32[160,128]{1,0:T(8,128)S(1)}, f32[160,128]{1,0:T(8,128)S(1)}, u32[]{:S(2)}, u32[]{:S(2)}) collective-permute-start(f32[160,128]{1,0:T(8,128)S(1)} %get-tuple-element.24), channel_id=1, source_target_pairs={{0,6},{2,4},{4,2},{6,0},{8,14},{10,12},{12,10},{14,8},{1,7},{3,5},... | collective-permute-start | bytes 245768 | tf_op jit(solution)/shard_map/ppermute | solution.py:152
  45.6 4.7 %collective-permute-start.6 = (f32[160,128]{1,0:T(8,128)S(1)}, f32[160,128]{1,0:T(8,128)S(1)}, u32[]{:S(2)}, u32[]{:S(2)}) collective-permute-start(f32[160,128]{1,0:T(8,128)S(1)} %get-tuple-element.25), channel_id=1, source_target_pairs={{0,4},{2,6},{4,0},{6,2},{8,12},{10,14},{12,8},{14,10},{1,5},{3,7},... | collective-permute-start | bytes 245768 | tf_op jit(solution)/shard_map/ppermute | solution.py:152
  46.0 4.4 %collective-permute-start.5 = (f32[160,128]{1,0:T(8,128)S(1)}, f32[160,128]{1,0:T(8,128)S(1)}, u32[]{:S(2)}, u32[]{:S(2)}) collective-permute-start(f32[160,128]{1,0:T(8,128)S(1)} %get-tuple-element.23), channel_id=1, source_target_pairs={{0,2},{2,0},{4,6},{6,4},{8,10},{10,8},{12,14},{14,12},{1,3},{3,1},... | collective-permute-start | bytes 245768 | tf_op jit(solution)/shard_map/ppermute | solution.py:152
  50.5 5.0 %collective-permute-start.8 = (f32[80,128]{1,0:T(8,128)S(1)}, f32[80,128]{1,0:T(8,128)S(1)}, u32[]{:S(2)}, u32[]{:S(2)}) collective-permute-start(f32[80,128]{1,0:T(8,128)S(1)} %constant_dynamic-slice_fusion), channel_id=1, source_target_pairs={{0,8},{2,10},{4,12},{6,14},{8,0},{10,2},{12,4},{14,6},{1,9},{3,11}... | collective-permute-start | bytes 122888 | tf_op jit(solution)/shard_map/ppermute | solution.py:152
  55.5 5.0 %collective-permute-start.9 = (f32[80,128]{1,0:T(8,128)S(1)}, f32[80,128]{1,0:T(8,128)S(1)}, u32[]{:S(2)}, u32[]{:S(2)}) collective-permute-start(f32[80,128]{1,0:T(8,128)S(1)} %dynamic-slice_add_fusion), channel_id=1, source_target_pairs={{0,8},{2,10},{4,12},{6,14},{8,0},{10,2},{12,4},{14,6},{1,9},{3,11}... | collective-permute-start | bytes 122888 | tf_op jit(solution)/shard_map/ppermute | solution.py:159
  60.5 5.4 %collective-permute-start.10 = (f32[160,128]{1,0:T(8,128)S(1)}, f32[160,128]{1,0:T(8,128)S(1)}, u32[]{:S(2)}, u32[]{:S(2)}) collective-permute-start(f32[160,128]{1,0:T(8,128)S(1)} %pad_maximum_fusion.2), channel_id=1, source_target_pairs={{0,6},{2,4},{4,2},{6,0},{8,14},{10,12},{12,10},{14,8},{1,7},{3,5},... | collective-permute-start | bytes 245768 | tf_op jit(solution)/shard_map/ppermute | solution.py:159
  62.8 4.4 %collective-permute-start.11 = (f32[160,128]{1,0:T(8,128)S(1)}, f32[160,128]{1,0:T(8,128)S(1)}, u32[]{:S(2)}, u32[]{:S(2)}) collective-permute-start(f32[160,128]{1,0:T(8,128)S(1)} %pad_maximum_fusion.2), channel_id=1, source_target_pairs={{0,4},{2,6},{4,0},{6,2},{8,12},{10,14},{12,8},{14,10},{1,5},{3,7},... | collective-permute-start | bytes 245768 | tf_op jit(solution)/shard_map/ppermute | solution.py:159
  63.6 4.4 %collective-permute-start.12 = (f32[160,128]{1,0:T(8,128)S(1)}, f32[160,128]{1,0:T(8,128)S(1)}, u32[]{:S(2)}, u32[]{:S(2)}) collective-permute-start(f32[160,128]{1,0:T(8,128)S(1)} %pad_maximum_fusion.2), channel_id=1, source_target_pairs={{0,2},{2,0},{4,6},{6,4},{8,10},{10,8},{12,14},{14,12},{1,3},{3,1},... | collective-permute-start | bytes 245768 | tf_op jit(solution)/shard_map/ppermute | solution.py:159
  68.2 1.7 %collective-permute-start.13 = (f32[640,128]{1,0:T(8,128)S(1)}, f32[640,128]{1,0:T(8,128)S(1)}, u32[]{:S(2)}, u32[]{:S(2)}) collective-permute-start(f32[640,128]{1,0:T(8,128)S(1)} %pad_maximum_fusion.1), channel_id=1, source_target_pairs={{0,1},{1,0},{2,3},{3,2},{4,5},{5,4},{6,7},{7,6},{8,9},{9,8},{10,11... | collective-permute-start | bytes 983048 | tf_op jit(solution)/shard_map/ppermute | solution.py:159

commit v10 on v9

--- a/solution.py
+++ b/solution.py
@@ -129,19 +129,23 @@
 
 def grouped_sum(flat, rolled=False):
     levels = group_levels()
-    if levels is None:
+    if rolled:
+        head, tail = flat
+        side = lax.axis_index("ty")
+        flat = jnp.where(side == 0, jnp.concatenate([head, tail]), jnp.concatenate([tail, head]))
+    pieces = 1
+    for level in levels or ():
+        pieces *= level[3]
+    if levels is None or flat.shape[0] % pieces:
         return doubling_sum(doubling_sum(flat, "tx"), "ty")
-    pieces = 1
-    for level in levels:
-        pieces *= level[3]
-    if flat.shape[0] % pieces:
-        return doubling_sum(doubling_sum(flat, "tx"), "ty")
+    if rolled:
+        flat = head
     digits = []
     for axis, size, stride, group in levels:
         digit = lax.axis_index(axis) // stride % group
         chunk = flat.shape[0] // group
         if rolled and not digits:
-            kept = flat[:chunk] + lax.ppermute(flat[chunk:], axis, [(i, i ^ stride) for i in range(size)])
+            kept = head + lax.ppermute(tail, axis, [(i, i ^ stride) for i in range(size)])
             flat = kept
             digits.append(digit)
             continue
@@ -203,7 +207,9 @@
 
 def land_kernel(landing_ref, shift_ref, base_ref, *refs):
     pieces = refs[:4]
-    forecast_ref, tiles_ref, acc_ref = refs[4:]
+    forecast_ref, kept_ref, sent_ref, acc_ref = refs[4:]
+    lead = kept_ref.shape[0]
+    count = lead + sent_ref.shape[0]
     nblk, block, width = base_ref.shape
     rim = pieces[0].shape[0]
     acc_ref[...] = base_ref[...]
@@ -221,7 +227,17 @@
         band = lax.dot_general(left, right, (((0,), (0,)), ((), ())), precision=HI,
                                preferred_element_type=jnp.float32)
         for b in range(a, tiles):
-            tiles_ref[(t + shift_ref[0]) % tiles_ref.shape[0]] = band[:, (b - a) * block:(b - a + 1) * block]
+            tile = band[:, (b - a) * block:(b - a + 1) * block]
+            spot = (t + shift_ref[0]) % count
+
+            @pl.when(spot < lead)
+            def _():
+                kept_ref[jnp.minimum(spot, lead - 1)] = tile
+
+            @pl.when(spot >= lead)
+            def _():
+                sent_ref[jnp.maximum(spot - lead, 0)] = tile
+
             t += 1
 
 
@@ -235,10 +251,11 @@
         land_kernel,
         out_shape=(
             jax.ShapeDtypeStruct((nblk * block, width), jnp.float32),
-            jax.ShapeDtypeStruct((count, block, block), jnp.float32),
+            jax.ShapeDtypeStruct(((count + 1) // 2, block, block), jnp.float32),
+            jax.ShapeDtypeStruct((count // 2, block, block), jnp.float32),
         ),
         in_specs=[smem, smem, vmem] + [vmem] * len(pieces),
-        out_specs=(vmem, vmem),
+        out_specs=(vmem, vmem, vmem),
         scratch_shapes=[pltpu.VMEM((nblk, block, width), jnp.float32)],
     )(landing, shift, base, *pieces)
 
@@ -261,11 +278,16 @@
     rolled = bool(levels) and levels[0][0] == "ty" and levels[0][3] == 2 and count % 2 == 0
     shift = lax.axis_index("ty") * (count // 2) if rolled else 0
     shift = jnp.full((1,), shift, jnp.int32)
-    predicted_root, local_tiles = land_and_gram(
+    predicted_root, kept_tiles, sent_tiles = land_and_gram(
         landing, shift, base, [from_next_x, from_prev_x, from_next_y, from_prev_y])
+    local_tiles = (kept_tiles, sent_tiles) if rolled else jnp.concatenate([kept_tiles, sent_tiles])
     total_rows = state_rows * lax.axis_size("tx") * lax.axis_size("ty")
     tiles = mode_columns // block
-    upper_sum = grouped_sum(local_tiles.reshape(-1, block), rolled).reshape(local_tiles.shape)
+    if rolled:
+        flat = tuple(part.reshape(-1, block) for part in local_tiles)
+    else:
+        flat = local_tiles.reshape(-1, block)
+    upper_sum = grouped_sum(flat, rolled).reshape(count, block, block)
     rescaled_orthogonal_root, r_factor = factor_solve(upper_sum, predicted_root, total_rows, block)
     return (rescaled_orthogonal_root, r_factor)
 

time: 118 us -> 120 us (1.017)
  Pallas kernels: 56.2 us -> 57.8 us
    pallas_call x1, Pallas kernels: 4.68 us -> 6.25 us  [land_and_gram(): pl.pallas_call(land_kernel, out_shape=(jax.ShapeDtypeStruct((nblk * block...]
where the time goes in v10:
time: 120 us
  Pallas kernels  57.8 us (48%)
  waiting for transfers between devices  33.6 us (28%)
  starting transfers between devices  24.2 us (20%)
  other arithmetic  2.1 us (2%)
    pallas_call x1, Pallas kernels, factor_solve(): pl.pallas_call(functools.partial(factor_kernel, float(total)), out_shape=...  47.2 us
    ppermute x4, waiting for transfers between devices, shifted(): return lax.ppermute(block, axis, route)  17.3 us
    ppermute x4, starting transfers between devices, shifted(): return lax.ppermute(block, axis, route)  11.2 us
    ppermute x5, waiting for transfers between devices, grouped_sum(): got.append(lax.ppermute(flat, axis, route))  7.98 us
    ppermute x4, starting transfers between devices, grouped_sum(): kept = kept + lax.ppermute(sent, axis, route)  6.74 us
    ppermute x4, waiting for transfers between devices, grouped_sum(): kept = kept + lax.ppermute(sent, axis, route)  6.56 us
    ppermute x5, starting transfers between devices, grouped_sum(): got.append(lax.ppermute(flat, axis, route))  6.26 us
    pallas_call x1, Pallas kernels, land_and_gram(): pl.pallas_call(land_kernel, out_shape=(jax.ShapeDtypeStruct((nblk * block...  6.25 us
  transfers between devices with their start and end apart: 14, of which 12 were waited for; matrix products, arithmetic and copies ran while one was open for 0% of the time, Pallas kernels for 0%

profile of v10, /device:TPU:0, one launch (start us, length us, event | category | flops | bytes accessed | tf_op | source)
XLA Modules:
  0.0 119.6 jit_solution(1882141982728369502)
XLA Ops:
  0.6 4.3 %shard_map.68 = (f32[4,128,512]{2,1,0:T(8,128)}, f32[2,128,512]{2,1,0:T(8,128)}, f32[2,128,512]{2,1,0:T(8,128)}, f32[2,128,512]{2,1,0:T(8,128)}, f32[2,128,512]{2,1,0:T(8,128)}) custom-call(s32[28]{0:T(128)} %rows_ref.1, s32[28]{0:T(128)} %cols_ref.1, bf16[28,128,128]{2,1,0:T(8,128)(2,1)} %jac_ref.1, bf16[4,128,512]{2,1,0:T(8,128)(2,1)} %bitcast.7), custom_call_target="tpu_custom_call" | custom-call | tf_op jit(solution)/shard_map/pallas_call | solution.py:198
  4.9 1.3 %collective-permute-start = (f32[2,128,512]{2,1,0:T(8,128)}, f32[2,128,512]{2,1,0:T(8,128)S(1)}, u32[]{:S(2)}, u32[]{:S(2)}) collective-permute-start(f32[2,128,512]{2,1,0:T(8,128)} %get-tuple-element.11), channel_id=1, source_target_pairs={{2,0},{4,2},{6,4},{8,6},{10,8},{12,10},{14,12},{3,1},{5,3},{7,5},{... | collective-permute-start | bytes 1572872 | tf_op jit(solution)/shard_map/ppermute | solution.py:88
  6.2 5.5 %collective-permute-start.1 = (f32[2,128,512]{2,1,0:T(8,128)}, f32[2,128,512]{2,1,0:T(8,128)S(1)}, u32[]{:S(2)}, u32[]{:S(2)}) collective-permute-start(f32[2,128,512]{2,1,0:T(8,128)} %get-tuple-element.12), channel_id=1, source_target_pairs={{0,2},{2,4},{4,6},{6,8},{8,10},{10,12},{12,14},{1,3},{3,5},{5,7},{... | collective-permute-start | bytes 1572872 | tf_op jit(solution)/shard_map/ppermute | solution.py:88
  11.7 1.3 %collective-permute-start.2 = (f32[2,128,512]{2,1,0:T(8,128)}, f32[2,128,512]{2,1,0:T(8,128)S(1)}, u32[]{:S(2)}, u32[]{:S(2)}) collective-permute-start(f32[2,128,512]{2,1,0:T(8,128)} %get-tuple-element.13), channel_id=1, source_target_pairs={{1,0},{3,2},{5,4},{7,6},{9,8},{11,10},{13,12},{15,14},{17,16},{19,... | collective-permute-start | bytes 1572872 | tf_op jit(solution)/shard_map/ppermute | solution.py:88
  13.0 3.1 %collective-permute-start.3 = (f32[2,128,512]{2,1,0:T(8,128)}, f32[2,128,512]{2,1,0:T(8,128)S(1)}, u32[]{:S(2)}, u32[]{:S(2)}) collective-permute-start(f32[2,128,512]{2,1,0:T(8,128)} %get-tuple-element.14), channel_id=1, source_target_pairs={{0,1},{2,3},{4,5},{6,7},{8,9},{10,11},{12,13},{14,15},{16,17},{18,... | collective-permute-start | bytes 1572872 | tf_op jit(solution)/shard_map/ppermute | solution.py:88
  16.1 5.8 %collective-permute-done.refs_0_ = f32[2,128,512]{2,1,0:T(8,128)S(1)} collective-permute-done((f32[2,128,512]{2,1,0:T(8,128)}, f32[2,128,512]{2,1,0:T(8,128)S(1)}, u32[]{:S(2)}, u32[]{:S(2)}) %collective-permute-start) | collective-permute-done | bytes 524320 | tf_op jit(solution)/shard_map/ppermute | solution.py:88
  21.9 0.0 copy-start
  21.9 11.5 %collective-permute-done.1.refs_1_ = f32[2,128,512]{2,1,0:T(8,128)S(1)} collective-permute-done((f32[2,128,512]{2,1,0:T(8,128)}, f32[2,128,512]{2,1,0:T(8,128)S(1)}, u32[]{:S(2)}, u32[]{:S(2)}) %collective-permute-start.1) | collective-permute-done | bytes 524320 | tf_op jit(solution)/shard_map/ppermute | solution.py:88
  33.4 0.0 copy-start.1
  33.4 0.0 collective-permute-done.2.refs_2_
  33.4 0.0 copy-start.2
  33.4 0.0 collective-permute-done.3.refs_3_
  33.4 0.0 copy-start.3
  33.4 0.0 copy-done
  33.4 0.8 copy-done.1
  34.2 0.2 copy-done.2
  34.3 0.2 copy-done.3
  34.5 6.2 %shard_map.69 = (f32[512,512]{1,0:T(8,128)}, f32[5,128,128]{2,1,0:T(8,128)}, f32[5,128,128]{2,1,0:T(8,128)}) custom-call(s32[8]{0:T(128)} %landing_ref.1, s32[1]{0:T(128)} %bitcast.shift_ref, f32[4,128,512]{2,1,0:T(8,128)} %get-tuple-element.10.base_ref, f32[2,128,512]{2,1,0:T(8,128)} %copy-done, f32[2,128,512]{2,1,0:T(8,128)} %copy-done.1, ...), custom_call_target="tpu_custom_call" | custom-call | tf_op jit(solution)/shard_map/pallas_call | solution.py:250
  40.8 0.0 collective-permute-start.4
  40.8 1.8 %collective-permute-done.4 = f32[640,128]{1,0:T(8,128)S(1)} collective-permute-done((f32[640,128]{1,0:T(8,128)}, f32[640,128]{1,0:T(8,128)S(1)}, u32[]{:S(2)}, u32[]{:S(2)}) %collective-permute-start.4) | collective-permute-done | bytes 327712 | tf_op jit(solution)/shard_map/ppermute | solution.py:148
  42.6 1.0 bitcast_add_fusion
  43.6 3.5 %collective-permute-start.7 = (f32[160,128]{1,0:T(8,128)S(1)}, f32[160,128]{1,0:T(8,128)S(1)}, u32[]{:S(2)}, u32[]{:S(2)}) collective-permute-start(f32[160,128]{1,0:T(8,128)S(1)} %get-tuple-element.24), channel_id=1, source_target_pairs={{0,6},{2,4},{4,2},{6,0},{8,14},{10,12},{12,10},{14,8},{1,7},{3,5},... | collective-permute-start | bytes 245768 | tf_op jit(solution)/shard_map/ppermute | solution.py:156
  47.1 0.4 collective-permute-start.6
  47.5 0.2 collective-permute-start.5
  47.7 2.6 %collective-permute-done.7 = f32[160,128]{1,0:T(8,128)S(1)} collective-permute-done((f32[160,128]{1,0:T(8,128)S(1)}, f32[160,128]{1,0:T(8,128)S(1)}, u32[]{:S(2)}, u32[]{:S(2)}) %collective-permute-start.7) | collective-permute-done | bytes 81952 | tf_op jit(solution)/shard_map/ppermute | solution.py:156
  50.3 1.4 %collective-permute-done.6 = f32[160,128]{1,0:T(8,128)S(1)} collective-permute-done((f32[160,128]{1,0:T(8,128)S(1)}, f32[160,128]{1,0:T(8,128)S(1)}, u32[]{:S(2)}, u32[]{:S(2)}) %collective-permute-start.6) | collective-permute-done | bytes 81952 | tf_op jit(solution)/shard_map/ppermute | solution.py:156
  51.8 0.2 collective-permute-done.5
  52.0 2.6 %collective-permute-start.8 = (f32[80,128]{1,0:T(8,128)S(1)}, f32[80,128]{1,0:T(8,128)S(1)}, u32[]{:S(2)}, u32[]{:S(2)}) collective-permute-start(f32[80,128]{1,0:T(8,128)S(1)} %constant_dynamic-slice_fusion), channel_id=1, source_target_pairs={{0,8},{2,10},{4,12},{6,14},{8,0},{10,2},{12,4},{14,6},{1,9},{3,11}... | collective-permute-start | bytes 122888 | tf_op jit(solution)/shard_map/ppermute | solution.py:156
  54.7 2.3 %collective-permute-done.8 = f32[80,128]{1,0:T(8,128)S(1)} collective-permute-done((f32[80,128]{1,0:T(8,128)S(1)}, f32[80,128]{1,0:T(8,128)S(1)}, u32[]{:S(2)}, u32[]{:S(2)}) %collective-permute-start.8) | collective-permute-done | bytes 40992 | tf_op jit(solution)/shard_map/ppermute | solution.py:156
  57.0 2.6 %collective-permute-start.9 = (f32[80,128]{1,0:T(8,128)S(1)}, f32[80,128]{1,0:T(8,128)S(1)}, u32[]{:S(2)}, u32[]{:S(2)}) collective-permute-start(f32[80,128]{1,0:T(8,128)S(1)} %dynamic-slice_add_fusion), channel_id=1, source_target_pairs={{0,8},{2,10},{4,12},{6,14},{8,0},{10,2},{12,4},{14,6},{1,9},{3,11}... | collective-permute-start | bytes 122888 | tf_op jit(solution)/shard_map/ppermute | solution.py:163
  59.6 2.3 %collective-permute-done.9 = f32[80,128]{1,0:T(8,128)S(1)} collective-permute-done((f32[80,128]{1,0:T(8,128)S(1)}, f32[80,128]{1,0:T(8,128)S(1)}, u32[]{:S(2)}, u32[]{:S(2)}) %collective-permute-start.9) | collective-permute-done | bytes 40992 | tf_op jit(solution)/shard_map/ppermute | solution.py:163
  62.0 2.3 %collective-permute-start.10 = (f32[160,128]{1,0:T(8,128)S(1)}, f32[160,128]{1,0:T(8,128)S(1)}, u32[]{:S(2)}, u32[]{:S(2)}) collective-permute-start(f32[160,128]{1,0:T(8,128)S(1)} %pad_maximum_fusion.2), channel_id=1, source_target_pairs={{0,6},{2,4},{4,2},{6,0},{8,14},{10,12},{12,10},{14,8},{1,7},{3,5},... | collective-permute-start | bytes 245768 | tf_op jit(solution)/shard_map/ppermute | solution.py:163
  64.3 0.8 collective-permute-start.11
  65.2 0.4 collective-permute-start.12
  65.5 1.9 %collective-permute-done.10 = f32[160,128]{1,0:T(8,128)S(1)} collective-permute-done((f32[160,128]{1,0:T(8,128)S(1)}, f32[160,128]{1,0:T(8,128)S(1)}, u32[]{:S(2)}, u32[]{:S(2)}) %collective-permute-start.10) | collective-permute-done | bytes 81952 | tf_op jit(solution)/shard_map/ppermute | solution.py:163
  67.4 1.4 %collective-permute-done.11 = f32[160,128]{1,0:T(8,128)S(1)} collective-permute-done((f32[160,128]{1,0:T(8,128)S(1)}, f32[160,128]{1,0:T(8,128)S(1)}, u32[]{:S(2)}, u32[]{:S(2)}) %collective-permute-start.11) | collective-permute-done | bytes 81952 | tf_op jit(solution)/shard_map/ppermute | solution.py:163
  68.8 0.8 collective-permute-done.12
  69.7 0.1 collective-permute-start.13
  69.8 1.6 %collective-permute-done.13 = f32[640,128]{1,0:T(8,128)S(1)} collective-permute-done((f32[640,128]{1,0:T(8,128)S(1)}, f32[640,128]{1,0:T(8,128)S(1)}, u32[]{:S(2)}, u32[]{:S(2)}) %collective-permute-start.13) | collective-permute-done | bytes 327712 | tf_op jit(solution)/shard_map/ppermute | solution.py:163
  71.4 0.9 pad_maximum_fusion
  72.4 47.2 %shard_map.70 = (bf16[512,512]{1,0:T(8,128)(2,1)}, f32[512,512]{1,0:T(8,128)}) custom-call(f32[10,128,128]{2,1,0:T(8,128)} %bitcast.6, f32[512,512]{1,0:T(8,128)} %get-tuple-element.17.f_ref), custom_call_target="tpu_custom_call" | custom-call | tf_op jit(solution)/shard_map/pallas_call | solution.py:72
  (10 shorter events, 0.2 us)
Async XLA Ops:
  4.9 17.0 %collective-permute-start = (f32[2,128,512]{2,1,0:T(8,128)}, f32[2,128,512]{2,1,0:T(8,128)S(1)}, u32[]{:S(2)}, u32[]{:S(2)}) collective-permute-start(f32[2,128,512]{2,1,0:T(8,128)} %get-tuple-element.11), channel_id=1, source_target_pairs={{2,0},{4,2},{6,4},{8,6},{10,8},{12,10},{14,12},{3,1},{5,3},{7,5},{... | collective-permute-start | bytes 1572872 | tf_op jit(solution)/shard_map/ppermute | solution.py:88
  6.2 27.2 %collective-permute-start.1 = (f32[2,128,512]{2,1,0:T(8,128)}, f32[2,128,512]{2,1,0:T(8,128)S(1)}, u32[]{:S(2)}, u32[]{:S(2)}) collective-permute-start(f32[2,128,512]{2,1,0:T(8,128)} %get-tuple-element.12), channel_id=1, source_target_pairs={{0,2},{2,4},{4,6},{6,8},{8,10},{10,12},{12,14},{1,3},{3,5},{5,7},{... | collective-permute-start | bytes 1572872 | tf_op jit(solution)/shard_map/ppermute | solution.py:88
  11.7 21.7 %collective-permute-start.2 = (f32[2,128,512]{2,1,0:T(8,128)}, f32[2,128,512]{2,1,0:T(8,128)S(1)}, u32[]{:S(2)}, u32[]{:S(2)}) collective-permute-start(f32[2,128,512]{2,1,0:T(8,128)} %get-tuple-element.13), channel_id=1, source_target_pairs={{1,0},{3,2},{5,4},{7,6},{9,8},{11,10},{13,12},{15,14},{17,16},{19,... | collective-permute-start | bytes 1572872 | tf_op jit(solution)/shard_map/ppermute | solution.py:88
  13.0 20.4 %collective-permute-start.3 = (f32[2,128,512]{2,1,0:T(8,128)}, f32[2,128,512]{2,1,0:T(8,128)S(1)}, u32[]{:S(2)}, u32[]{:S(2)}) collective-permute-start(f32[2,128,512]{2,1,0:T(8,128)} %get-tuple-element.14), channel_id=1, source_target_pairs={{0,1},{2,3},{4,5},{6,7},{8,9},{10,11},{12,13},{14,15},{16,17},{18,... | collective-permute-start | bytes 1572872 | tf_op jit(solution)/shard_map/ppermute | solution.py:88
  21.9 11.5 %copy-start = (f32[2,128,512]{2,1,0:T(8,128)}, f32[2,128,512]{2,1,0:T(8,128)S(1)}, u32[]{:S(2)}) copy-start(f32[2,128,512]{2,1,0:T(8,128)S(1)} %collective-permute-done.refs_0_) | copy-start | bytes 1572868
  33.4 0.8 copy-start.1
  33.4 1.0 copy-start.2
  33.4 1.1 copy-start.3
  40.8 1.8 %collective-permute-start.4 = (f32[640,128]{1,0:T(8,128)}, f32[640,128]{1,0:T(8,128)S(1)}, u32[]{:S(2)}, u32[]{:S(2)}) collective-permute-start(f32[640,128]{1,0:T(8,128)} %bitcast.8), channel_id=1, source_target_pairs={{0,1},{1,0},{2,3},{3,2},{4,5},{5,4},{6,7},{7,6},{8,9},{9,8},{10,11... | collective-permute-start | bytes 983048 | tf_op jit(solution)/shard_map/ppermute | solution.py:148
  43.6 6.7 %collective-permute-start.7 = (f32[160,128]{1,0:T(8,128)S(1)}, f32[160,128]{1,0:T(8,128)S(1)}, u32[]{:S(2)}, u32[]{:S(2)}) collective-permute-start(f32[160,128]{1,0:T(8,128)S(1)} %get-tuple-element.24), channel_id=1, source_target_pairs={{0,6},{2,4},{4,2},{6,0},{8,14},{10,12},{12,10},{14,8},{1,7},{3,5},... | collective-permute-start | bytes 245768 | tf_op jit(solution)/shard_map/ppermute | solution.py:156
  47.1 4.7 %collective-permute-start.6 = (f32[160,128]{1,0:T(8,128)S(1)}, f32[160,128]{1,0:T(8,128)S(1)}, u32[]{:S(2)}, u32[]{:S(2)}) collective-permute-start(f32[160,128]{1,0:T(8,128)S(1)} %get-tuple-element.25), channel_id=1, source_target_pairs={{0,4},{2,6},{4,0},{6,2},{8,12},{10,14},{12,8},{14,10},{1,5},{3,7},... | collective-permute-start | bytes 245768 | tf_op jit(solution)/shard_map/ppermute | solution.py:156
  47.5 4.4 %collective-permute-start.5 = (f32[160,128]{1,0:T(8,128)S(1)}, f32[160,128]{1,0:T(8,128)S(1)}, u32[]{:S(2)}, u32[]{:S(2)}) collective-permute-start(f32[160,128]{1,0:T(8,128)S(1)} %get-tuple-element.23), channel_id=1, source_target_pairs={{0,2},{2,0},{4,6},{6,4},{8,10},{10,8},{12,14},{14,12},{1,3},{3,1},... | collective-permute-start | bytes 245768 | tf_op jit(solution)/shard_map/ppermute | solution.py:156
  52.0 5.0 %collective-permute-start.8 = (f32[80,128]{1,0:T(8,128)S(1)}, f32[80,128]{1,0:T(8,128)S(1)}, u32[]{:S(2)}, u32[]{:S(2)}) collective-permute-start(f32[80,128]{1,0:T(8,128)S(1)} %constant_dynamic-slice_fusion), channel_id=1, source_target_pairs={{0,8},{2,10},{4,12},{6,14},{8,0},{10,2},{12,4},{14,6},{1,9},{3,11}... | collective-permute-start | bytes 122888 | tf_op jit(solution)/shard_map/ppermute | solution.py:156
  57.0 5.0 %collective-permute-start.9 = (f32[80,128]{1,0:T(8,128)S(1)}, f32[80,128]{1,0:T(8,128)S(1)}, u32[]{:S(2)}, u32[]{:S(2)}) collective-permute-start(f32[80,128]{1,0:T(8,128)S(1)} %dynamic-slice_add_fusion), channel_id=1, source_target_pairs={{0,8},{2,10},{4,12},{6,14},{8,0},{10,2},{12,4},{14,6},{1,9},{3,11}... | collective-permute-start | bytes 122888 | tf_op jit(solution)/shard_map/ppermute | solution.py:163
  62.0 5.4 %collective-permute-start.10 = (f32[160,128]{1,0:T(8,128)S(1)}, f32[160,128]{1,0:T(8,128)S(1)}, u32[]{:S(2)}, u32[]{:S(2)}) collective-permute-start(f32[160,128]{1,0:T(8,128)S(1)} %pad_maximum_fusion.2), channel_id=1, source_target_pairs={{0,6},{2,4},{4,2},{6,0},{8,14},{10,12},{12,10},{14,8},{1,7},{3,5},... | collective-permute-start | bytes 245768 | tf_op jit(solution)/shard_map/ppermute | solution.py:163
  64.3 4.4 %collective-permute-start.11 = (f32[160,128]{1,0:T(8,128)S(1)}, f32[160,128]{1,0:T(8,128)S(1)}, u32[]{:S(2)}, u32[]{:S(2)}) collective-permute-start(f32[160,128]{1,0:T(8,128)S(1)} %pad_maximum_fusion.2), channel_id=1, source_target_pairs={{0,4},{2,6},{4,0},{6,2},{8,12},{10,14},{12,8},{14,10},{1,5},{3,7},... | collective-permute-start | bytes 245768 | tf_op jit(solution)/shard_map/ppermute | solution.py:163
  65.2 4.4 %collective-permute-start.12 = (f32[160,128]{1,0:T(8,128)S(1)}, f32[160,128]{1,0:T(8,128)S(1)}, u32[]{:S(2)}, u32[]{:S(2)}) collective-permute-start(f32[160,128]{1,0:T(8,128)S(1)} %pad_maximum_fusion.2), channel_id=1, source_target_pairs={{0,2},{2,0},{4,6},{6,4},{8,10},{10,8},{12,14},{14,12},{1,3},{3,1},... | collective-permute-start | bytes 245768 | tf_op jit(solution)/shard_map/ppermute | solution.py:163
  69.7 1.7 %collective-permute-start.13 = (f32[640,128]{1,0:T(8,128)S(1)}, f32[640,128]{1,0:T(8,128)S(1)}, u32[]{:S(2)}, u32[]{:S(2)}) collective-permute-start(f32[640,128]{1,0:T(8,128)S(1)} %pad_maximum_fusion.1), channel_id=1, source_target_pairs={{0,1},{1,0},{2,3},{3,2},{4,5},{5,4},{6,7},{7,6},{8,9},{9,8},{10,11... | collective-permute-start | bytes 983048 | tf_op jit(solution)/shard_map/ppermute | solution.py:163

commit v11 on v7

--- a/solution.py
+++ b/solution.py
@@ -10,18 +10,31 @@
 HI = lax.Precision.HIGHEST
 
 
-def factor_kernel(total, g_ref, f_ref, x_ref, u_ref, w_ref, inv_ref, xs_ref):
-    n = f_ref.shape[1]
-    b = inv_ref.shape[1]
-    nb = n // b
+def fill_gram(w_ref, halves, total, nb, b):
+    lead = halves[0].shape[0]
     t = 0
     for first in range(nb):
         for second in range(first, nb):
-            tile = g_ref[t] / total
+            tile = halves[t // lead][t % lead] / total
             w_ref[first * b:(first + 1) * b, second * b:(second + 1) * b] = tile
             if second > first:
                 w_ref[second * b:(second + 1) * b, first * b:(first + 1) * b] = tile.T
             t += 1
+
+
+def factor_kernel(total, side_ref, g_ref, h_ref, f_ref, x_ref, u_ref, w_ref, inv_ref, xs_ref):
+    n = f_ref.shape[1]
+    b = inv_ref.shape[1]
+    nb = n // b
+
+    @pl.when(side_ref[0] == 0)
+    def _():
+        fill_gram(w_ref, (g_ref, h_ref), total, nb, b)
+
+    @pl.when(side_ref[0] != 0)
+    def _():
+        fill_gram(w_ref, (h_ref, g_ref), total, nb, b)
+
     u_ref[...] = jnp.zeros(u_ref.shape, jnp.float32)
     lane = lax.broadcasted_iota(jnp.int32, (1, b), 1)
     rows = lax.broadcasted_iota(jnp.int32, (b, 1), 0)
@@ -65,21 +78,21 @@
     x_ref[...] = xs_ref[...].astype(x_ref.dtype)
 
 
-def factor_solve(tiles, forecast, total, block=128):
+def factor_solve(side, kept, other, forecast, total, block=128):
     n = forecast.shape[1]
     m = forecast.shape[0]
     vmem = pl.BlockSpec(memory_space=pltpu.VMEM)
     return pl.pallas_call(
         functools.partial(factor_kernel, float(total)),
         out_shape=(jax.ShapeDtypeStruct((m, n), jnp.bfloat16), jax.ShapeDtypeStruct((n, n), jnp.float32)),
-        in_specs=[vmem, vmem],
+        in_specs=[pl.BlockSpec(memory_space=pltpu.SMEM), vmem, vmem, vmem],
         out_specs=(vmem, vmem),
         scratch_shapes=[
             pltpu.VMEM((n, n), jnp.float32),
             pltpu.VMEM((n // block, block, block), jnp.float32),
             pltpu.VMEM((m, n), jnp.float32),
         ],
-    )(tiles, forecast)
+    )(side, kept, other, forecast)
 
 
 def shifted(block, axis, distance):
@@ -127,7 +140,7 @@
     return levels
 
 
-def grouped_sum(flat):
+def grouped_sum(flat, split=False):
     levels = group_levels()
     if levels is None:
         return doubling_sum(doubling_sum(flat, "tx"), "ty")
@@ -147,11 +160,13 @@
             kept = kept + lax.ppermute(sent, axis, route)
         flat = kept
         digits.append(digit)
-    for (axis, size, stride, group), digit in reversed(list(zip(levels, digits))):
+    for depth, ((axis, size, stride, group), digit) in reversed(list(enumerate(zip(levels, digits)))):
         got = [flat]
         for offset in range(1, group):
             route = [(i, i ^ (offset * stride)) for i in range(size)]
             got.append(lax.ppermute(flat, axis, route))
+        if split and depth == 0 and group == 2:
+            return got[0], got[1], digit
         placed = []
         for position in range(group):
             pick = got[0]
@@ -254,8 +269,20 @@
         landing, base, [from_next_x, from_prev_x, from_next_y, from_prev_y])
     total_rows = state_rows * lax.axis_size("tx") * lax.axis_size("ty")
     tiles = mode_columns // block
-    upper_sum = grouped_sum(local_tiles.reshape(-1, block)).reshape(local_tiles.shape)
-    rescaled_orthogonal_root, r_factor = factor_solve(upper_sum, predicted_root, total_rows, block)
+    levels = group_levels()
+    count = local_tiles.shape[0]
+    if levels and levels[0][0] == "ty" and levels[0][3] == 2 and count % 2 == 0:
+        kept, other, side = grouped_sum(local_tiles.reshape(-1, block), True)
+        if isinstance(kept, tuple):
+            raise ValueError("unsplit")
+    else:
+        kept = grouped_sum(local_tiles.reshape(-1, block))
+        other = kept[:0]
+        side = 0
+    kept = kept.reshape(-1, block, block)
+    other = other.reshape(-1, block, block)
+    side = jnp.full((1,), side, jnp.int32)
+    rescaled_orthogonal_root, r_factor = factor_solve(side, kept, other, predicted_root, total_rows, block)
     return (rescaled_orthogonal_root, r_factor)
 
 

time: 118 us -> 118 us (level)
  no operation moved by 1% of the time
where the time goes in v11:
time: 118 us
  Pallas kernels  56.5 us (48%)
  waiting for transfers between devices  33.4 us (28%)
  starting transfers between devices  24.2 us (21%)
  local copies, waits for them, and re-layouts  2.95 us (2%)
    pallas_call x1, Pallas kernels, factor_solve(): pl.pallas_call(functools.partial(factor_kernel, float(total)), out_shape=...  47.6 us
    ppermute x4, waiting for transfers between devices, shifted(): return lax.ppermute(block, axis, route)  17.2 us
    ppermute x4, starting transfers between devices, shifted(): return lax.ppermute(block, axis, route)  11.2 us
    ppermute x5, waiting for transfers between devices, grouped_sum(): kept = kept + lax.ppermute(sent, axis, route)  8.14 us
    ppermute x5, waiting for transfers between devices, grouped_sum(): got.append(lax.ppermute(flat, axis, route))  7.98 us
    ppermute x5, starting transfers between devices, grouped_sum(): kept = kept + lax.ppermute(sent, axis, route)  6.82 us
    ppermute x5, starting transfers between devices, grouped_sum(): got.append(lax.ppermute(flat, axis, route))  6.26 us
    pallas_call x1, Pallas kernels, land_and_gram(): pl.pallas_call(land_kernel, out_shape=(jax.ShapeDtypeStruct((nblk * block...  4.65 us
  transfers between devices with their start and end apart: 14, of which 12 were waited for; matrix products, arithmetic and copies ran while one was open for 0% of the time, Pallas kernels for 0%

profile of v11, /device:TPU:0, one launch (start us, length us, event | category | flops | bytes accessed | tf_op | source)
XLA Modules:
  0.0 118.1 jit_solution(9078644748654599937)
XLA Ops:
  0.6 4.3 %shard_map.68 = (f32[4,128,512]{2,1,0:T(8,128)}, f32[2,128,512]{2,1,0:T(8,128)}, f32[2,128,512]{2,1,0:T(8,128)}, f32[2,128,512]{2,1,0:T(8,128)}, f32[2,128,512]{2,1,0:T(8,128)}) custom-call(s32[28]{0:T(128)} %rows_ref.1, s32[28]{0:T(128)} %cols_ref.1, bf16[28,128,128]{2,1,0:T(8,128)(2,1)} %jac_ref.1, bf16[4,128,512]{2,1,0:T(8,128)(2,1)} %bitcast.8), custom_call_target="tpu_custom_call" | custom-call | tf_op jit(solution)/shard_map/pallas_call | solution.py:204
  4.9 1.3 %collective-permute-start = (f32[2,128,512]{2,1,0:T(8,128)}, f32[2,128,512]{2,1,0:T(8,128)S(1)}, u32[]{:S(2)}, u32[]{:S(2)}) collective-permute-start(f32[2,128,512]{2,1,0:T(8,128)} %get-tuple-element.10), channel_id=1, source_target_pairs={{2,0},{4,2},{6,4},{8,6},{10,8},{12,10},{14,12},{3,1},{5,3},{7,5},{... | collective-permute-start | bytes 1572872 | tf_op jit(solution)/shard_map/ppermute | solution.py:101
  6.2 5.5 %collective-permute-start.1 = (f32[2,128,512]{2,1,0:T(8,128)}, f32[2,128,512]{2,1,0:T(8,128)S(1)}, u32[]{:S(2)}, u32[]{:S(2)}) collective-permute-start(f32[2,128,512]{2,1,0:T(8,128)} %get-tuple-element.11), channel_id=1, source_target_pairs={{0,2},{2,4},{4,6},{6,8},{8,10},{10,12},{12,14},{1,3},{3,5},{5,7},{... | collective-permute-start | bytes 1572872 | tf_op jit(solution)/shard_map/ppermute | solution.py:101
  11.7 1.3 %collective-permute-start.2 = (f32[2,128,512]{2,1,0:T(8,128)}, f32[2,128,512]{2,1,0:T(8,128)S(1)}, u32[]{:S(2)}, u32[]{:S(2)}) collective-permute-start(f32[2,128,512]{2,1,0:T(8,128)} %get-tuple-element.12), channel_id=1, source_target_pairs={{1,0},{3,2},{5,4},{7,6},{9,8},{11,10},{13,12},{15,14},{17,16},{19,... | collective-permute-start | bytes 1572872 | tf_op jit(solution)/shard_map/ppermute | solution.py:101
  13.0 3.1 %collective-permute-start.3 = (f32[2,128,512]{2,1,0:T(8,128)}, f32[2,128,512]{2,1,0:T(8,128)S(1)}, u32[]{:S(2)}, u32[]{:S(2)}) collective-permute-start(f32[2,128,512]{2,1,0:T(8,128)} %get-tuple-element.13), channel_id=1, source_target_pairs={{0,1},{2,3},{4,5},{6,7},{8,9},{10,11},{12,13},{14,15},{16,17},{18,... | collective-permute-start | bytes 1572872 | tf_op jit(solution)/shard_map/ppermute | solution.py:101
  16.1 5.7 %collective-permute-done.refs_0_ = f32[2,128,512]{2,1,0:T(8,128)S(1)} collective-permute-done((f32[2,128,512]{2,1,0:T(8,128)}, f32[2,128,512]{2,1,0:T(8,128)S(1)}, u32[]{:S(2)}, u32[]{:S(2)}) %collective-permute-start) | collective-permute-done | bytes 524320 | tf_op jit(solution)/shard_map/ppermute | solution.py:101
  21.9 0.0 copy-start.2
  21.9 11.5 %collective-permute-done.1.refs_1_ = f32[2,128,512]{2,1,0:T(8,128)S(1)} collective-permute-done((f32[2,128,512]{2,1,0:T(8,128)}, f32[2,128,512]{2,1,0:T(8,128)S(1)}, u32[]{:S(2)}, u32[]{:S(2)}) %collective-permute-start.1) | collective-permute-done | bytes 524320 | tf_op jit(solution)/shard_map/ppermute | solution.py:101
  33.4 0.0 copy-start.3
  33.4 0.0 collective-permute-done.2.refs_2_
  33.4 0.0 copy-start.4
  33.4 0.0 collective-permute-done.3.refs_3_
  33.4 0.0 copy-start.5
  33.4 0.0 copy-done.2
  33.4 0.8 copy-done.3
  34.2 0.2 copy-done.4
  34.4 0.2 copy-done.5
  34.5 4.7 %shard_map.69 = (f32[512,512]{1,0:T(8,128)}, f32[10,128,128]{2,1,0:T(8,128)}) custom-call(s32[8]{0:T(128)} %landing_ref.1, f32[4,128,512]{2,1,0:T(8,128)} %get-tuple-element.9.base_ref, f32[2,128,512]{2,1,0:T(8,128)} %copy-done.2, f32[2,128,512]{2,1,0:T(8,128)} %copy-done.3, f32[2,128,512]{2,1,0:T(8,128)} %copy-done.4, f32[2,128,512]{2,1,0:T(8,128)} %copy-done.5), custom_call_target="tpu_custom_call" | custom-call | tf_op jit(solution)/shard_map/pallas_call | solution.py:244
  39.2 0.0 copy-start.1
  39.2 1.1 constant_dynamic-slice_fusion.4
  40.2 0.1 collective-permute-start.4
  40.4 1.6 %collective-permute-done.4 = f32[640,128]{1,0:T(8,128)S(1)} collective-permute-done((f32[640,128]{1,0:T(8,128)S(1)}, f32[640,128]{1,0:T(8,128)S(1)}, u32[]{:S(2)}, u32[]{:S(2)}) %collective-permute-start.4) | collective-permute-done | bytes 327712 | tf_op jit(solution)/shard_map/ppermute | solution.py:160
  41.9 0.0 copy-done.1
  42.0 3.5 %collective-permute-start.7 = (f32[160,128]{1,0:T(8,128)S(1)}, f32[160,128]{1,0:T(8,128)S(1)}, u32[]{:S(2)}, u32[]{:S(2)}) collective-permute-start(f32[160,128]{1,0:T(8,128)S(1)} %get-tuple-element.20), channel_id=1, source_target_pairs={{0,6},{2,4},{4,2},{6,0},{8,14},{10,12},{12,10},{14,8},{1,7},{3,5},... | collective-permute-start | bytes 245768 | tf_op jit(solution)/shard_map/ppermute | solution.py:160
  45.5 0.4 collective-permute-start.6
  45.9 0.2 collective-permute-start.5
  46.1 2.6 %collective-permute-done.7 = f32[160,128]{1,0:T(8,128)S(1)} collective-permute-done((f32[160,128]{1,0:T(8,128)S(1)}, f32[160,128]{1,0:T(8,128)S(1)}, u32[]{:S(2)}, u32[]{:S(2)}) %collective-permute-start.7) | collective-permute-done | bytes 81952 | tf_op jit(solution)/shard_map/ppermute | solution.py:160
  48.7 1.4 %collective-permute-done.6 = f32[160,128]{1,0:T(8,128)S(1)} collective-permute-done((f32[160,128]{1,0:T(8,128)S(1)}, f32[160,128]{1,0:T(8,128)S(1)}, u32[]{:S(2)}, u32[]{:S(2)}) %collective-permute-start.6) | collective-permute-done | bytes 81952 | tf_op jit(solution)/shard_map/ppermute | solution.py:160
  50.1 0.2 collective-permute-done.5
  50.4 2.6 %collective-permute-start.8 = (f32[80,128]{1,0:T(8,128)S(1)}, f32[80,128]{1,0:T(8,128)S(1)}, u32[]{:S(2)}, u32[]{:S(2)}) collective-permute-start(f32[80,128]{1,0:T(8,128)S(1)} %constant_dynamic-slice_fusion), channel_id=1, source_target_pairs={{0,8},{2,10},{4,12},{6,14},{8,0},{10,2},{12,4},{14,6},{1,9},{3,11}... | collective-permute-start | bytes 122888 | tf_op jit(solution)/shard_map/ppermute | solution.py:160
  53.1 2.3 %collective-permute-done.8 = f32[80,128]{1,0:T(8,128)S(1)} collective-permute-done((f32[80,128]{1,0:T(8,128)S(1)}, f32[80,128]{1,0:T(8,128)S(1)}, u32[]{:S(2)}, u32[]{:S(2)}) %collective-permute-start.8) | collective-permute-done | bytes 40992 | tf_op jit(solution)/shard_map/ppermute | solution.py:160
  55.4 2.6 %collective-permute-start.9 = (f32[80,128]{1,0:T(8,128)S(1)}, f32[80,128]{1,0:T(8,128)S(1)}, u32[]{:S(2)}, u32[]{:S(2)}) collective-permute-start(f32[80,128]{1,0:T(8,128)S(1)} %dynamic-slice_add_fusion.1), channel_id=1, source_target_pairs={{0,8},{2,10},{4,12},{6,14},{8,0},{10,2},{12,4},{14,6},{1,9},{3,11}... | collective-permute-start | bytes 122888 | tf_op jit(solution)/shard_map/ppermute | solution.py:167
  58.0 2.3 %collective-permute-done.9 = f32[80,128]{1,0:T(8,128)S(1)} collective-permute-done((f32[80,128]{1,0:T(8,128)S(1)}, f32[80,128]{1,0:T(8,128)S(1)}, u32[]{:S(2)}, u32[]{:S(2)}) %collective-permute-start.9) | collective-permute-done | bytes 40992 | tf_op jit(solution)/shard_map/ppermute | solution.py:167
  60.4 2.3 %collective-permute-start.10 = (f32[160,128]{1,0:T(8,128)S(1)}, f32[160,128]{1,0:T(8,128)S(1)}, u32[]{:S(2)}, u32[]{:S(2)}) collective-permute-start(f32[160,128]{1,0:T(8,128)S(1)} %pad_maximum_fusion.1), channel_id=1, source_target_pairs={{0,6},{2,4},{4,2},{6,0},{8,14},{10,12},{12,10},{14,8},{1,7},{3,5},... | collective-permute-start | bytes 245768 | tf_op jit(solution)/shard_map/ppermute | solution.py:167
  62.7 0.8 collective-permute-start.11
  63.5 0.4 collective-permute-start.12
  63.9 1.9 %collective-permute-done.10 = f32[160,128]{1,0:T(8,128)S(1)} collective-permute-done((f32[160,128]{1,0:T(8,128)S(1)}, f32[160,128]{1,0:T(8,128)S(1)}, u32[]{:S(2)}, u32[]{:S(2)}) %collective-permute-start.10) | collective-permute-done | bytes 81952 | tf_op jit(solution)/shard_map/ppermute | solution.py:167
  65.8 1.4 %collective-permute-done.11 = f32[160,128]{1,0:T(8,128)S(1)} collective-permute-done((f32[160,128]{1,0:T(8,128)S(1)}, f32[160,128]{1,0:T(8,128)S(1)}, u32[]{:S(2)}, u32[]{:S(2)}) %collective-permute-start.11) | collective-permute-done | bytes 81952 | tf_op jit(solution)/shard_map/ppermute | solution.py:167
  67.1 0.8 collective-permute-done.12
  68.1 0.0 copy-start
  68.1 0.1 collective-permute-start.13
  68.2 1.6 %collective-permute-done.13 = f32[640,128]{1,0:T(8,128)S(1)} collective-permute-done((f32[640,128]{1,0:T(8,128)S(1)}, f32[640,128]{1,0:T(8,128)S(1)}, u32[]{:S(2)}, u32[]{:S(2)}) %collective-permute-start.13) | collective-permute-done | bytes 327712 | tf_op jit(solution)/shard_map/ppermute | solution.py:167
  69.8 0.0 copy-start.6
  69.8 0.0 copy-done
  69.8 0.7 copy-done.6
  70.5 47.6 %shard_map.70 = (bf16[512,512]{1,0:T(8,128)(2,1)}, f32[512,512]{1,0:T(8,128)}) custom-call(s32[1]{0:T(128)} %bitcast.side_ref, f32[5,128,128]{2,1,0:T(8,128)} %bitcast.5, f32[5,128,128]{2,1,0:T(8,128)} %bitcast.9, f32[512,512]{1,0:T(8,128)} %get-tuple-element.15.f_ref), custom_call_target="tpu_custom_call" | custom-call | tf_op jit(solution)/shard_map/pallas_call | solution.py:85
  (10 shorter events, 0.2 us)
Async XLA Ops:
  4.9 17.0 %collective-permute-start = (f32[2,128,512]{2,1,0:T(8,128)}, f32[2,128,512]{2,1,0:T(8,128)S(1)}, u32[]{:S(2)}, u32[]{:S(2)}) collective-permute-start(f32[2,128,512]{2,1,0:T(8,128)} %get-tuple-element.10), channel_id=1, source_target_pairs={{2,0},{4,2},{6,4},{8,6},{10,8},{12,10},{14,12},{3,1},{5,3},{7,5},{... | collective-permute-start | bytes 1572872 | tf_op jit(solution)/shard_map/ppermute | solution.py:101
  6.2 27.2 %collective-permute-start.1 = (f32[2,128,512]{2,1,0:T(8,128)}, f32[2,128,512]{2,1,0:T(8,128)S(1)}, u32[]{:S(2)}, u32[]{:S(2)}) collective-permute-start(f32[2,128,512]{2,1,0:T(8,128)} %get-tuple-element.11), channel_id=1, source_target_pairs={{0,2},{2,4},{4,6},{6,8},{8,10},{10,12},{12,14},{1,3},{3,5},{5,7},{... | collective-permute-start | bytes 1572872 | tf_op jit(solution)/shard_map/ppermute | solution.py:101
  11.7 21.7 %collective-permute-start.2 = (f32[2,128,512]{2,1,0:T(8,128)}, f32[2,128,512]{2,1,0:T(8,128)S(1)}, u32[]{:S(2)}, u32[]{:S(2)}) collective-permute-start(f32[2,128,512]{2,1,0:T(8,128)} %get-tuple-element.12), channel_id=1, source_target_pairs={{1,0},{3,2},{5,4},{7,6},{9,8},{11,10},{13,12},{15,14},{17,16},{19,... | collective-permute-start | bytes 1572872 | tf_op jit(solution)/shard_map/ppermute | solution.py:101
  13.0 20.4 %collective-permute-start.3 = (f32[2,128,512]{2,1,0:T(8,128)}, f32[2,128,512]{2,1,0:T(8,128)S(1)}, u32[]{:S(2)}, u32[]{:S(2)}) collective-permute-start(f32[2,128,512]{2,1,0:T(8,128)} %get-tuple-element.13), channel_id=1, source_target_pairs={{0,1},{2,3},{4,5},{6,7},{8,9},{10,11},{12,13},{14,15},{16,17},{18,... | collective-permute-start | bytes 1572872 | tf_op jit(solution)/shard_map/ppermute | solution.py:101
  21.9 11.5 %copy-start.2 = (f32[2,128,512]{2,1,0:T(8,128)}, f32[2,128,512]{2,1,0:T(8,128)S(1)}, u32[]{:S(2)}) copy-start(f32[2,128,512]{2,1,0:T(8,128)S(1)} %collective-permute-done.refs_0_) | copy-start | bytes 1572868
  33.4 0.8 copy-start.3
  33.4 1.0 copy-start.4
  33.4 1.1 copy-start.5
  39.2 2.8 %copy-start.1 = (f32[10,128,128]{2,1,0:T(8,128)S(1)}, f32[10,128,128]{2,1,0:T(8,128)}, u32[]{:S(2)}) copy-start(f32[10,128,128]{2,1,0:T(8,128)} %get-tuple-element.14) | copy-start | bytes 1966084
  40.2 1.7 %collective-permute-start.4 = (f32[640,128]{1,0:T(8,128)S(1)}, f32[640,128]{1,0:T(8,128)S(1)}, u32[]{:S(2)}, u32[]{:S(2)}) collective-permute-start(f32[640,128]{1,0:T(8,128)S(1)} %constant_dynamic-slice_fusion.4), channel_id=1, source_target_pairs={{0,1},{1,0},{2,3},{3,2},{4,5},{5,4},{6,7},{7,6},{8,9},{9,8},{10,11... | collective-permute-start | bytes 983048 | tf_op jit(solution)/shard_map/ppermute | solution.py:160
  42.0 6.7 %collective-permute-start.7 = (f32[160,128]{1,0:T(8,128)S(1)}, f32[160,128]{1,0:T(8,128)S(1)}, u32[]{:S(2)}, u32[]{:S(2)}) collective-permute-start(f32[160,128]{1,0:T(8,128)S(1)} %get-tuple-element.20), channel_id=1, source_target_pairs={{0,6},{2,4},{4,2},{6,0},{8,14},{10,12},{12,10},{14,8},{1,7},{3,5},... | collective-permute-start | bytes 245768 | tf_op jit(solution)/shard_map/ppermute | solution.py:160
  45.5 4.7 %collective-permute-start.6 = (f32[160,128]{1,0:T(8,128)S(1)}, f32[160,128]{1,0:T(8,128)S(1)}, u32[]{:S(2)}, u32[]{:S(2)}) collective-permute-start(f32[160,128]{1,0:T(8,128)S(1)} %get-tuple-element.21), channel_id=1, source_target_pairs={{0,4},{2,6},{4,0},{6,2},{8,12},{10,14},{12,8},{14,10},{1,5},{3,7},... | collective-permute-start | bytes 245768 | tf_op jit(solution)/shard_map/ppermute | solution.py:160
  45.9 4.4 %collective-permute-start.5 = (f32[160,128]{1,0:T(8,128)S(1)}, f32[160,128]{1,0:T(8,128)S(1)}, u32[]{:S(2)}, u32[]{:S(2)}) collective-permute-start(f32[160,128]{1,0:T(8,128)S(1)} %get-tuple-element.19), channel_id=1, source_target_pairs={{0,2},{2,0},{4,6},{6,4},{8,10},{10,8},{12,14},{14,12},{1,3},{3,1},... | collective-permute-start | bytes 245768 | tf_op jit(solution)/shard_map/ppermute | solution.py:160
  50.4 5.0 %collective-permute-start.8 = (f32[80,128]{1,0:T(8,128)S(1)}, f32[80,128]{1,0:T(8,128)S(1)}, u32[]{:S(2)}, u32[]{:S(2)}) collective-permute-start(f32[80,128]{1,0:T(8,128)S(1)} %constant_dynamic-slice_fusion), channel_id=1, source_target_pairs={{0,8},{2,10},{4,12},{6,14},{8,0},{10,2},{12,4},{14,6},{1,9},{3,11}... | collective-permute-start | bytes 122888 | tf_op jit(solution)/shard_map/ppermute | solution.py:160
  55.4 5.0 %collective-permute-start.9 = (f32[80,128]{1,0:T(8,128)S(1)}, f32[80,128]{1,0:T(8,128)S(1)}, u32[]{:S(2)}, u32[]{:S(2)}) collective-permute-start(f32[80,128]{1,0:T(8,128)S(1)} %dynamic-slice_add_fusion.1), channel_id=1, source_target_pairs={{0,8},{2,10},{4,12},{6,14},{8,0},{10,2},{12,4},{14,6},{1,9},{3,11}... | collective-permute-start | bytes 122888 | tf_op jit(solution)/shard_map/ppermute | solution.py:167
  60.4 5.4 %collective-permute-start.10 = (f32[160,128]{1,0:T(8,128)S(1)}, f32[160,128]{1,0:T(8,128)S(1)}, u32[]{:S(2)}, u32[]{:S(2)}) collective-permute-start(f32[160,128]{1,0:T(8,128)S(1)} %pad_maximum_fusion.1), channel_id=1, source_target_pairs={{0,6},{2,4},{4,2},{6,0},{8,14},{10,12},{12,10},{14,8},{1,7},{3,5},... | collective-permute-start | bytes 245768 | tf_op jit(solution)/shard_map/ppermute | solution.py:167
  62.7 4.4 %collective-permute-start.11 = (f32[160,128]{1,0:T(8,128)S(1)}, f32[160,128]{1,0:T(8,128)S(1)}, u32[]{:S(2)}, u32[]{:S(2)}) collective-permute-start(f32[160,128]{1,0:T(8,128)S(1)} %pad_maximum_fusion.1), channel_id=1, source_target_pairs={{0,4},{2,6},{4,0},{6,2},{8,12},{10,14},{12,8},{14,10},{1,5},{3,7},... | collective-permute-start | bytes 245768 | tf_op jit(solution)/shard_map/ppermute | solution.py:167
  63.5 4.4 %collective-permute-start.12 = (f32[160,128]{1,0:T(8,128)S(1)}, f32[160,128]{1,0:T(8,128)S(1)}, u32[]{:S(2)}, u32[]{:S(2)}) collective-permute-start(f32[160,128]{1,0:T(8,128)S(1)} %pad_maximum_fusion.1), channel_id=1, source_target_pairs={{0,2},{2,0},{4,6},{6,4},{8,10},{10,8},{12,14},{14,12},{1,3},{3,1},... | collective-permute-start | bytes 245768 | tf_op jit(solution)/shard_map/ppermute | solution.py:167
  68.1 1.7 %copy-start = (f32[640,128]{1,0:T(8,128)}, f32[640,128]{1,0:T(8,128)S(1)}, u32[]{:S(2)}) copy-start(f32[640,128]{1,0:T(8,128)S(1)} %pad_maximum_fusion) | copy-start | bytes 983044
  68.1 1.7 %collective-permute-start.13 = (f32[640,128]{1,0:T(8,128)S(1)}, f32[640,128]{1,0:T(8,128)S(1)}, u32[]{:S(2)}, u32[]{:S(2)}) collective-permute-start(f32[640,128]{1,0:T(8,128)S(1)} %pad_maximum_fusion), channel_id=1, source_target_pairs={{0,1},{1,0},{2,3},{3,2},{4,5},{5,4},{6,7},{7,6},{8,9},{9,8},{10,11... | collective-permute-start | bytes 983048 | tf_op jit(solution)/shard_map/ppermute | solution.py:167
  69.8 0.7 copy-start.6

commit v12 on v7

--- a/solution.py
+++ b/solution.py
@@ -22,7 +22,8 @@
             if second > first:
                 w_ref[second * b:(second + 1) * b, first * b:(first + 1) * b] = tile.T
             t += 1
-    u_ref[...] = jnp.zeros(u_ref.shape, jnp.float32)
+    for first in range(1, nb):
+        u_ref[first * b:, (first - 1) * b:first * b] = jnp.zeros(((nb - first) * b, b), jnp.float32)
     lane = lax.broadcasted_iota(jnp.int32, (1, b), 1)
     rows = lax.broadcasted_iota(jnp.int32, (b, 1), 0)
     eye = jnp.where(lax.broadcasted_iota(jnp.int32, (b, b), 0) == lax.broadcasted_iota(jnp.int32, (b, b), 1), 1.0, 0.0)

time: 118 us -> 118 us (level)
  no operation moved by 1% of the time
where the time goes in v12:
time: 118 us
  Pallas kernels  56.1 us (48%)
  waiting for transfers between devices  33.4 us (28%)
  starting transfers between devices  24.3 us (21%)
  local copies, waits for them, and re-layouts  2.23 us (2%)
    pallas_call x1, Pallas kernels, factor_solve(): pl.pallas_call(functools.partial(factor_kernel, float(total)), out_shape=...  47.2 us
    ppermute x4, waiting for transfers between devices, shifted(): return lax.ppermute(block, axis, route)  17.2 us
    ppermute x4, starting transfers between devices, shifted(): return lax.ppermute(block, axis, route)  11.2 us
    ppermute x5, waiting for transfers between devices, grouped_sum(): kept = kept + lax.ppermute(sent, axis, route)  8.14 us
    ppermute x5, waiting for transfers between devices, grouped_sum(): got.append(lax.ppermute(flat, axis, route))  7.98 us
    ppermute x5, starting transfers between devices, grouped_sum(): kept = kept + lax.ppermute(sent, axis, route)  6.82 us
    ppermute x5, starting transfers between devices, grouped_sum(): got.append(lax.ppermute(flat, axis, route))  6.26 us
    pallas_call x1, Pallas kernels, land_and_gram(): pl.pallas_call(land_kernel, out_shape=(jax.ShapeDtypeStruct((nblk * block...  4.66 us
  transfers between devices with their start and end apart: 14, of which 12 were waited for; matrix products, arithmetic and copies ran while one was open for 0% of the time, Pallas kernels for 0%

profile of v12, /device:TPU:0, one launch (start us, length us, event | category | flops | bytes accessed | tf_op | source)
XLA Modules:
  0.0 117.9 jit_solution(3128780379314397103)
XLA Ops:
  0.6 4.3 %shard_map.68 = (f32[4,128,512]{2,1,0:T(8,128)}, f32[2,128,512]{2,1,0:T(8,128)}, f32[2,128,512]{2,1,0:T(8,128)}, f32[2,128,512]{2,1,0:T(8,128)}, f32[2,128,512]{2,1,0:T(8,128)}) custom-call(s32[28]{0:T(128)} %rows_ref.1, s32[28]{0:T(128)} %cols_ref.1, bf16[28,128,128]{2,1,0:T(8,128)(2,1)} %jac_ref.1, bf16[4,128,512]{2,1,0:T(8,128)(2,1)} %bitcast.6), custom_call_target="tpu_custom_call" | custom-call | tf_op jit(solution)/shard_map/pallas_call | solution.py:190
  4.9 1.3 %collective-permute-start = (f32[2,128,512]{2,1,0:T(8,128)}, f32[2,128,512]{2,1,0:T(8,128)S(1)}, u32[]{:S(2)}, u32[]{:S(2)}) collective-permute-start(f32[2,128,512]{2,1,0:T(8,128)} %get-tuple-element.10), channel_id=1, source_target_pairs={{2,0},{4,2},{6,4},{8,6},{10,8},{12,10},{14,12},{3,1},{5,3},{7,5},{... | collective-permute-start | bytes 1572872 | tf_op jit(solution)/shard_map/ppermute | solution.py:89
  6.2 5.5 %collective-permute-start.1 = (f32[2,128,512]{2,1,0:T(8,128)}, f32[2,128,512]{2,1,0:T(8,128)S(1)}, u32[]{:S(2)}, u32[]{:S(2)}) collective-permute-start(f32[2,128,512]{2,1,0:T(8,128)} %get-tuple-element.11), channel_id=1, source_target_pairs={{0,2},{2,4},{4,6},{6,8},{8,10},{10,12},{12,14},{1,3},{3,5},{5,7},{... | collective-permute-start | bytes 1572872 | tf_op jit(solution)/shard_map/ppermute | solution.py:89
  11.7 1.3 %collective-permute-start.2 = (f32[2,128,512]{2,1,0:T(8,128)}, f32[2,128,512]{2,1,0:T(8,128)S(1)}, u32[]{:S(2)}, u32[]{:S(2)}) collective-permute-start(f32[2,128,512]{2,1,0:T(8,128)} %get-tuple-element.12), channel_id=1, source_target_pairs={{1,0},{3,2},{5,4},{7,6},{9,8},{11,10},{13,12},{15,14},{17,16},{19,... | collective-permute-start | bytes 1572872 | tf_op jit(solution)/shard_map/ppermute | solution.py:89
  13.0 3.1 %collective-permute-start.3 = (f32[2,128,512]{2,1,0:T(8,128)}, f32[2,128,512]{2,1,0:T(8,128)S(1)}, u32[]{:S(2)}, u32[]{:S(2)}) collective-permute-start(f32[2,128,512]{2,1,0:T(8,128)} %get-tuple-element.13), channel_id=1, source_target_pairs={{0,1},{2,3},{4,5},{6,7},{8,9},{10,11},{12,13},{14,15},{16,17},{18,... | collective-permute-start | bytes 1572872 | tf_op jit(solution)/shard_map/ppermute | solution.py:89
  16.2 5.7 %collective-permute-done.refs_0_ = f32[2,128,512]{2,1,0:T(8,128)S(1)} collective-permute-done((f32[2,128,512]{2,1,0:T(8,128)}, f32[2,128,512]{2,1,0:T(8,128)S(1)}, u32[]{:S(2)}, u32[]{:S(2)}) %collective-permute-start) | collective-permute-done | bytes 524320 | tf_op jit(solution)/shard_map/ppermute | solution.py:89
  21.9 0.0 copy-start.1
  21.9 11.5 %collective-permute-done.1.refs_1_ = f32[2,128,512]{2,1,0:T(8,128)S(1)} collective-permute-done((f32[2,128,512]{2,1,0:T(8,128)}, f32[2,128,512]{2,1,0:T(8,128)S(1)}, u32[]{:S(2)}, u32[]{:S(2)}) %collective-permute-start.1) | collective-permute-done | bytes 524320 | tf_op jit(solution)/shard_map/ppermute | solution.py:89
  33.4 0.0 copy-start.2
  33.4 0.0 collective-permute-done.2.refs_2_
  33.4 0.0 copy-start.3
  33.4 0.0 collective-permute-done.3.refs_3_
  33.4 0.0 copy-start.4
  33.4 0.0 copy-done.1
  33.4 0.8 copy-done.2
  34.2 0.2 copy-done.3
  34.4 0.1 copy-done.4
  34.5 4.7 %shard_map.69 = (f32[512,512]{1,0:T(8,128)}, f32[10,128,128]{2,1,0:T(8,128)}) custom-call(s32[8]{0:T(128)} %landing_ref.1, f32[4,128,512]{2,1,0:T(8,128)} %get-tuple-element.9.base_ref, f32[2,128,512]{2,1,0:T(8,128)} %copy-done.1, f32[2,128,512]{2,1,0:T(8,128)} %copy-done.2, f32[2,128,512]{2,1,0:T(8,128)} %copy-done.3, f32[2,128,512]{2,1,0:T(8,128)} %copy-done.4), custom_call_target="tpu_custom_call" | custom-call | tf_op jit(solution)/shard_map/pallas_call | solution.py:230
  39.2 0.0 copy-start
  39.2 1.1 constant_dynamic-slice_fusion.4
  40.3 0.1 collective-permute-start.4
  40.4 1.6 %collective-permute-done.4 = f32[640,128]{1,0:T(8,128)S(1)} collective-permute-done((f32[640,128]{1,0:T(8,128)S(1)}, f32[640,128]{1,0:T(8,128)S(1)}, u32[]{:S(2)}, u32[]{:S(2)}) %collective-permute-start.4) | collective-permute-done | bytes 327712 | tf_op jit(solution)/shard_map/ppermute | solution.py:148
  42.0 0.0 copy-done
  42.0 3.5 %collective-permute-start.7 = (f32[160,128]{1,0:T(8,128)S(1)}, f32[160,128]{1,0:T(8,128)S(1)}, u32[]{:S(2)}, u32[]{:S(2)}) collective-permute-start(f32[160,128]{1,0:T(8,128)S(1)} %get-tuple-element.22), channel_id=1, source_target_pairs={{0,6},{2,4},{4,2},{6,0},{8,14},{10,12},{12,10},{14,8},{1,7},{3,5},... | collective-permute-start | bytes 245768 | tf_op jit(solution)/shard_map/ppermute | solution.py:148
  45.5 0.4 collective-permute-start.6
  45.9 0.2 collective-permute-start.5
  46.1 2.6 %collective-permute-done.7 = f32[160,128]{1,0:T(8,128)S(1)} collective-permute-done((f32[160,128]{1,0:T(8,128)S(1)}, f32[160,128]{1,0:T(8,128)S(1)}, u32[]{:S(2)}, u32[]{:S(2)}) %collective-permute-start.7) | collective-permute-done | bytes 81952 | tf_op jit(solution)/shard_map/ppermute | solution.py:148
  48.7 1.4 %collective-permute-done.6 = f32[160,128]{1,0:T(8,128)S(1)} collective-permute-done((f32[160,128]{1,0:T(8,128)S(1)}, f32[160,128]{1,0:T(8,128)S(1)}, u32[]{:S(2)}, u32[]{:S(2)}) %collective-permute-start.6) | collective-permute-done | bytes 81952 | tf_op jit(solution)/shard_map/ppermute | solution.py:148
  50.2 0.2 collective-permute-done.5
  50.4 2.6 %collective-permute-start.8 = (f32[80,128]{1,0:T(8,128)S(1)}, f32[80,128]{1,0:T(8,128)S(1)}, u32[]{:S(2)}, u32[]{:S(2)}) collective-permute-start(f32[80,128]{1,0:T(8,128)S(1)} %constant_dynamic-slice_fusion), channel_id=1, source_target_pairs={{0,8},{2,10},{4,12},{6,14},{8,0},{10,2},{12,4},{14,6},{1,9},{3,11}... | collective-permute-start | bytes 122888 | tf_op jit(solution)/shard_map/ppermute | solution.py:148
  53.1 2.3 %collective-permute-done.8 = f32[80,128]{1,0:T(8,128)S(1)} collective-permute-done((f32[80,128]{1,0:T(8,128)S(1)}, f32[80,128]{1,0:T(8,128)S(1)}, u32[]{:S(2)}, u32[]{:S(2)}) %collective-permute-start.8) | collective-permute-done | bytes 40992 | tf_op jit(solution)/shard_map/ppermute | solution.py:148
  55.4 2.6 %collective-permute-start.9 = (f32[80,128]{1,0:T(8,128)S(1)}, f32[80,128]{1,0:T(8,128)S(1)}, u32[]{:S(2)}, u32[]{:S(2)}) collective-permute-start(f32[80,128]{1,0:T(8,128)S(1)} %dynamic-slice_add_fusion.1), channel_id=1, source_target_pairs={{0,8},{2,10},{4,12},{6,14},{8,0},{10,2},{12,4},{14,6},{1,9},{3,11}... | collective-permute-start | bytes 122888 | tf_op jit(solution)/shard_map/ppermute | solution.py:155
  58.0 2.3 %collective-permute-done.9 = f32[80,128]{1,0:T(8,128)S(1)} collective-permute-done((f32[80,128]{1,0:T(8,128)S(1)}, f32[80,128]{1,0:T(8,128)S(1)}, u32[]{:S(2)}, u32[]{:S(2)}) %collective-permute-start.9) | collective-permute-done | bytes 40992 | tf_op jit(solution)/shard_map/ppermute | solution.py:155
  60.4 2.3 %collective-permute-start.10 = (f32[160,128]{1,0:T(8,128)S(1)}, f32[160,128]{1,0:T(8,128)S(1)}, u32[]{:S(2)}, u32[]{:S(2)}) collective-permute-start(f32[160,128]{1,0:T(8,128)S(1)} %pad_maximum_fusion.2), channel_id=1, source_target_pairs={{0,6},{2,4},{4,2},{6,0},{8,14},{10,12},{12,10},{14,8},{1,7},{3,5},... | collective-permute-start | bytes 245768 | tf_op jit(solution)/shard_map/ppermute | solution.py:155
  62.7 0.8 collective-permute-start.11
  63.5 0.4 collective-permute-start.12
  63.9 1.9 %collective-permute-done.10 = f32[160,128]{1,0:T(8,128)S(1)} collective-permute-done((f32[160,128]{1,0:T(8,128)S(1)}, f32[160,128]{1,0:T(8,128)S(1)}, u32[]{:S(2)}, u32[]{:S(2)}) %collective-permute-start.10) | collective-permute-done | bytes 81952 | tf_op jit(solution)/shard_map/ppermute | solution.py:155
  65.8 1.4 %collective-permute-done.11 = f32[160,128]{1,0:T(8,128)S(1)} collective-permute-done((f32[160,128]{1,0:T(8,128)S(1)}, f32[160,128]{1,0:T(8,128)S(1)}, u32[]{:S(2)}, u32[]{:S(2)}) %collective-permute-start.11) | collective-permute-done | bytes 81952 | tf_op jit(solution)/shard_map/ppermute | solution.py:155
  67.1 0.8 collective-permute-done.12
  68.1 0.1 collective-permute-start.13
  68.2 1.6 %collective-permute-done.13 = f32[640,128]{1,0:T(8,128)S(1)} collective-permute-done((f32[640,128]{1,0:T(8,128)S(1)}, f32[640,128]{1,0:T(8,128)S(1)}, u32[]{:S(2)}, u32[]{:S(2)}) %collective-permute-start.13) | collective-permute-done | bytes 327712 | tf_op jit(solution)/shard_map/ppermute | solution.py:155
  69.8 0.9 pad_maximum_fusion
  70.7 47.2 %shard_map.70 = (bf16[512,512]{1,0:T(8,128)(2,1)}, f32[512,512]{1,0:T(8,128)}) custom-call(f32[10,128,128]{2,1,0:T(8,128)} %bitcast.3, f32[512,512]{1,0:T(8,128)} %get-tuple-element.15.f_ref), custom_call_target="tpu_custom_call" | custom-call | tf_op jit(solution)/shard_map/pallas_call | solution.py:73
  (11 shorter events, 0.2 us)
Async XLA Ops:
  4.9 17.0 %collective-permute-start = (f32[2,128,512]{2,1,0:T(8,128)}, f32[2,128,512]{2,1,0:T(8,128)S(1)}, u32[]{:S(2)}, u32[]{:S(2)}) collective-permute-start(f32[2,128,512]{2,1,0:T(8,128)} %get-tuple-element.10), channel_id=1, source_target_pairs={{2,0},{4,2},{6,4},{8,6},{10,8},{12,10},{14,12},{3,1},{5,3},{7,5},{... | collective-permute-start | bytes 1572872 | tf_op jit(solution)/shard_map/ppermute | solution.py:89
  6.2 27.2 %collective-permute-start.1 = (f32[2,128,512]{2,1,0:T(8,128)}, f32[2,128,512]{2,1,0:T(8,128)S(1)}, u32[]{:S(2)}, u32[]{:S(2)}) collective-permute-start(f32[2,128,512]{2,1,0:T(8,128)} %get-tuple-element.11), channel_id=1, source_target_pairs={{0,2},{2,4},{4,6},{6,8},{8,10},{10,12},{12,14},{1,3},{3,5},{5,7},{... | collective-permute-start | bytes 1572872 | tf_op jit(solution)/shard_map/ppermute | solution.py:89
  11.7 21.7 %collective-permute-start.2 = (f32[2,128,512]{2,1,0:T(8,128)}, f32[2,128,512]{2,1,0:T(8,128)S(1)}, u32[]{:S(2)}, u32[]{:S(2)}) collective-permute-start(f32[2,128,512]{2,1,0:T(8,128)} %get-tuple-element.12), channel_id=1, source_target_pairs={{1,0},{3,2},{5,4},{7,6},{9,8},{11,10},{13,12},{15,14},{17,16},{19,... | collective-permute-start | bytes 1572872 | tf_op jit(solution)/shard_map/ppermute | solution.py:89
  13.0 20.4 %collective-permute-start.3 = (f32[2,128,512]{2,1,0:T(8,128)}, f32[2,128,512]{2,1,0:T(8,128)S(1)}, u32[]{:S(2)}, u32[]{:S(2)}) collective-permute-start(f32[2,128,512]{2,1,0:T(8,128)} %get-tuple-element.13), channel_id=1, source_target_pairs={{0,1},{2,3},{4,5},{6,7},{8,9},{10,11},{12,13},{14,15},{16,17},{18,... | collective-permute-start | bytes 1572872 | tf_op jit(solution)/shard_map/ppermute | solution.py:89
  21.9 11.5 %copy-start.1 = (f32[2,128,512]{2,1,0:T(8,128)}, f32[2,128,512]{2,1,0:T(8,128)S(1)}, u32[]{:S(2)}) copy-start(f32[2,128,512]{2,1,0:T(8,128)S(1)} %collective-permute-done.refs_0_) | copy-start | bytes 1572868
  33.4 0.8 copy-start.2
  33.4 1.0 copy-start.3
  33.4 1.1 copy-start.4
  39.2 2.8 %copy-start = (f32[10,128,128]{2,1,0:T(8,128)S(1)}, f32[10,128,128]{2,1,0:T(8,128)}, u32[]{:S(2)}) copy-start(f32[10,128,128]{2,1,0:T(8,128)} %get-tuple-element.14) | copy-start | bytes 1966084
  40.3 1.7 %collective-permute-start.4 = (f32[640,128]{1,0:T(8,128)S(1)}, f32[640,128]{1,0:T(8,128)S(1)}, u32[]{:S(2)}, u32[]{:S(2)}) collective-permute-start(f32[640,128]{1,0:T(8,128)S(1)} %constant_dynamic-slice_fusion.4), channel_id=1, source_target_pairs={{0,1},{1,0},{2,3},{3,2},{4,5},{5,4},{6,7},{7,6},{8,9},{9,8},{10,11... | collective-permute-start | bytes 983048 | tf_op jit(solution)/shard_map/ppermute | solution.py:148
  42.0 6.7 %collective-permute-start.7 = (f32[160,128]{1,0:T(8,128)S(1)}, f32[160,128]{1,0:T(8,128)S(1)}, u32[]{:S(2)}, u32[]{:S(2)}) collective-permute-start(f32[160,128]{1,0:T(8,128)S(1)} %get-tuple-element.22), channel_id=1, source_target_pairs={{0,6},{2,4},{4,2},{6,0},{8,14},{10,12},{12,10},{14,8},{1,7},{3,5},... | collective-permute-start | bytes 245768 | tf_op jit(solution)/shard_map/ppermute | solution.py:148
  45.5 4.7 %collective-permute-start.6 = (f32[160,128]{1,0:T(8,128)S(1)}, f32[160,128]{1,0:T(8,128)S(1)}, u32[]{:S(2)}, u32[]{:S(2)}) collective-permute-start(f32[160,128]{1,0:T(8,128)S(1)} %get-tuple-element.23), channel_id=1, source_target_pairs={{0,4},{2,6},{4,0},{6,2},{8,12},{10,14},{12,8},{14,10},{1,5},{3,7},... | collective-permute-start | bytes 245768 | tf_op jit(solution)/shard_map/ppermute | solution.py:148
  45.9 4.4 %collective-permute-start.5 = (f32[160,128]{1,0:T(8,128)S(1)}, f32[160,128]{1,0:T(8,128)S(1)}, u32[]{:S(2)}, u32[]{:S(2)}) collective-permute-start(f32[160,128]{1,0:T(8,128)S(1)} %get-tuple-element.21), channel_id=1, source_target_pairs={{0,2},{2,0},{4,6},{6,4},{8,10},{10,8},{12,14},{14,12},{1,3},{3,1},... | collective-permute-start | bytes 245768 | tf_op jit(solution)/shard_map/ppermute | solution.py:148
  50.4 5.0 %collective-permute-start.8 = (f32[80,128]{1,0:T(8,128)S(1)}, f32[80,128]{1,0:T(8,128)S(1)}, u32[]{:S(2)}, u32[]{:S(2)}) collective-permute-start(f32[80,128]{1,0:T(8,128)S(1)} %constant_dynamic-slice_fusion), channel_id=1, source_target_pairs={{0,8},{2,10},{4,12},{6,14},{8,0},{10,2},{12,4},{14,6},{1,9},{3,11}... | collective-permute-start | bytes 122888 | tf_op jit(solution)/shard_map/ppermute | solution.py:148
  55.4 5.0 %collective-permute-start.9 = (f32[80,128]{1,0:T(8,128)S(1)}, f32[80,128]{1,0:T(8,128)S(1)}, u32[]{:S(2)}, u32[]{:S(2)}) collective-permute-start(f32[80,128]{1,0:T(8,128)S(1)} %dynamic-slice_add_fusion.1), channel_id=1, source_target_pairs={{0,8},{2,10},{4,12},{6,14},{8,0},{10,2},{12,4},{14,6},{1,9},{3,11}... | collective-permute-start | bytes 122888 | tf_op jit(solution)/shard_map/ppermute | solution.py:155
  60.4 5.4 %collective-permute-start.10 = (f32[160,128]{1,0:T(8,128)S(1)}, f32[160,128]{1,0:T(8,128)S(1)}, u32[]{:S(2)}, u32[]{:S(2)}) collective-permute-start(f32[160,128]{1,0:T(8,128)S(1)} %pad_maximum_fusion.2), channel_id=1, source_target_pairs={{0,6},{2,4},{4,2},{6,0},{8,14},{10,12},{12,10},{14,8},{1,7},{3,5},... | collective-permute-start | bytes 245768 | tf_op jit(solution)/shard_map/ppermute | solution.py:155
  62.7 4.4 %collective-permute-start.11 = (f32[160,128]{1,0:T(8,128)S(1)}, f32[160,128]{1,0:T(8,128)S(1)}, u32[]{:S(2)}, u32[]{:S(2)}) collective-permute-start(f32[160,128]{1,0:T(8,128)S(1)} %pad_maximum_fusion.2), channel_id=1, source_target_pairs={{0,4},{2,6},{4,0},{6,2},{8,12},{10,14},{12,8},{14,10},{1,5},{3,7},... | collective-permute-start | bytes 245768 | tf_op jit(solution)/shard_map/ppermute | solution.py:155
  63.5 4.4 %collective-permute-start.12 = (f32[160,128]{1,0:T(8,128)S(1)}, f32[160,128]{1,0:T(8,128)S(1)}, u32[]{:S(2)}, u32[]{:S(2)}) collective-permute-start(f32[160,128]{1,0:T(8,128)S(1)} %pad_maximum_fusion.2), channel_id=1, source_target_pairs={{0,2},{2,0},{4,6},{6,4},{8,10},{10,8},{12,14},{14,12},{1,3},{3,1},... | collective-permute-start | bytes 245768 | tf_op jit(solution)/shard_map/ppermute | solution.py:155
  68.1 1.7 %collective-permute-start.13 = (f32[640,128]{1,0:T(8,128)S(1)}, f32[640,128]{1,0:T(8,128)S(1)}, u32[]{:S(2)}, u32[]{:S(2)}) collective-permute-start(f32[640,128]{1,0:T(8,128)S(1)} %pad_maximum_fusion.1), channel_id=1, source_target_pairs={{0,1},{1,0},{2,3},{3,2},{4,5},{5,4},{6,7},{7,6},{8,9},{9,8},{10,11... | collective-permute-start | bytes 983048 | tf_op jit(solution)/shard_map/ppermute | solution.py:155
